TPU v7x, 32 devices: a whole 2x2x4 slice. The times are simulated.
32 devices in a mesh: grp: 2 (over y), gx: 16 (over z, x, core).
Axes of the slice: x: 2, y: 2, z: 4, core: 2. Of those that a mesh axis runs over, the one named last changes fastest.
Arguments:
- volume: float32 [512, 896], P(('grp', 'gx')), parts along dimension 0, may hold values from -45 to 45
- bank: float32 [8, 4096], P(None, 'gx'), may hold values from -43 to 43
- orient: int32 [8], replicated, may hold values from 0 to 47
- bank_id: int32 [8], replicated, may hold values from 0 to 7, each once
- counts: int32 [8], replicated, may hold values from 1 to 16
Outputs:
- fields: float32 [4, 512, 896], P(None, ('grp', 'gx')), parts along dimension 1
There are 2 independent parts, one for each index of `grp`. A program takes and returns all parts, laid end to end along the dimension named above; an argument that names none is the same for every part. Nothing has to cross between parts.
Inputs may be any that keep to these rules, and one draw needn't show every extreme that they name: `bank_id`: each of the 8 base templates is named by exactly one list entry.
All inputs are finite; a program needn't handle non-finite values.
Results may differ from a plain program's by a relative error of at most 0.0003.
Values sent between devices are 32-bit elements; how exact they have to be, the bound alone decides.
No kernel may reach another device: no remote copies, remote signals or barrier semaphores. Data moves between devices by JAX's collectives and lax.ppermute only.
A program may use at most 64 MiB of HBM per device.

v0:
```python
import jax
import jax.numpy as jnp
import numpy as np
from jax import lax
from jax.sharding import PartitionSpec as P

BY = 8
BZ = 112
TS = 16
NT = 8
FIELDS = 4
ZB = 16

epsilon = 1e-05
sharpness = 80.0
AXIS_ORDERS = np.array([[0, 1, 2], [0, 2, 1], [1, 0, 2], [1, 2, 0], [2, 0, 1], [2, 1, 0]], np.int32)


def extended(x, sides, width):
    for axis, dim in sides:
        size, length = (lax.axis_size(axis), x.shape[dim])
        up = [(i, (i + 1) % size) for i in range(size - 1)]
        down = [(j, i) for i, j in up]
        last = lax.slice_in_dim(x, length - width, length, axis=dim)
        leading = lax.slice_in_dim(x, 0, width, axis=dim)
        before = lax.ppermute(last, axis, up)
        after = lax.ppermute(leading, axis, down)
        x = jnp.concatenate([before, x, after], axis=dim)
    return x


def band_table(positions, targets, period):
    offset = (positions[:, None] - targets[None, :]) % period
    return (offset < TS).astype(jnp.float32)


def contract(letters, data, table):
    return jnp.einsum(letters, data, table, precision=lax.Precision.HIGHEST)


def expand(flag):
    return flag[:, None, None, None]


def gather_planes(bank, axis):
    size = lax.axis_size(axis)
    me = lax.axis_index(axis)
    held = bank[None]
    step = 1
    while step < size:
        pairs = [(i, i ^ step) for i in range(size)]
        other = lax.ppermute(held, axis, pairs)
        low = (me // step) % 2 == 0
        held = jnp.where(low, jnp.concatenate([held, other], 0), jnp.concatenate([other, held], 0))
        step *= 2
    return held


def rotated_kernels(planes, orient, bank_id):
    count = planes.shape[1]
    picked = jnp.zeros((orient.shape[0], TS, TS, TS), jnp.float32)
    for m in range(count):
        base = planes[:, m, :].reshape(TS, TS, TS)
        picked = picked + jnp.where(expand(bank_id == m), base[None], 0.0)
    flips = orient % 8
    for axis_num in range(3):
        bit = (flips // 2**axis_num) % 2 == 1
        picked = jnp.where(expand(bit), jnp.flip(picked, axis=axis_num + 1), picked)
    order_row = orient // 8
    rotated = jnp.zeros_like(picked)
    for row in range(AXIS_ORDERS.shape[0]):
        perm = (0,) + tuple(1 + int(p) for p in np.argsort(AXIS_ORDERS[row]))
        rotated = rotated + jnp.where(expand(order_row == row), jnp.transpose(picked, perm), 0.0)
    flat = rotated.reshape(rotated.shape[0], -1)
    centered = flat - jnp.mean(flat, axis=1, keepdims=True)
    norm = jnp.sqrt(jnp.sum(centered * centered, axis=1, keepdims=True) + epsilon)
    return (centered / norm).reshape(rotated.shape)


def toeplitz_rhs(kernels):
    nt = kernels.shape[0]
    kt = jnp.transpose(kernels, (1, 2, 3, 0)).reshape(TS * TS, TS * nt)
    c = lax.broadcasted_iota(jnp.int32, (TS, nt, TS + ZB, nt, ZB), 0)
    t = lax.broadcasted_iota(jnp.int32, (TS, nt, TS + ZB, nt, ZB), 1)
    w = lax.broadcasted_iota(jnp.int32, (TS, nt, TS + ZB, nt, ZB), 2)
    t2 = lax.broadcasted_iota(jnp.int32, (TS, nt, TS + ZB, nt, ZB), 3)
    zl = lax.broadcasted_iota(jnp.int32, (TS, nt, TS + ZB, nt, ZB), 4)
    shift = ((w - zl == c) & (t == t2)).astype(jnp.float32).reshape(TS * nt, -1)
    rhs = jnp.dot(kt, shift, precision=lax.Precision.HIGHEST)
    return rhs.reshape(TS, 1, TS * (TS + ZB), nt * ZB)


def local(volume, bank, orient, bank_id, counts):
    rows_x = volume.shape[0]
    half = TS // 2
    nt = orient.shape[0]
    grid = volume.reshape(rows_x, BY, BZ)
    len_x = rows_x + TS
    len_y = BY + TS
    len_z = BZ + TS
    blocks = BZ // ZB
    planes = gather_planes(bank, "gx")
    kernels = rotated_kernels(planes, orient, bank_id)
    rhs = toeplitz_rhs(kernels)
    field_in = extended(grid, (("gx", 0),), half)
    padded = jnp.pad(field_in, ((0, 0), (half, TS - half), (half, TS - half)))
    zwin = jnp.stack([padded[: len_x - 1, :, zb * ZB: zb * ZB + TS + ZB] for zb in range(blocks)], axis=1)
    cols = jnp.concatenate([zwin[:, :, b: b + BY] for b in range(TS)], axis=3)
    cols = cols.reshape(1, len_x - 1, blocks * BY, TS * (TS + ZB))
    numer = lax.conv_general_dilated(
        cols, rhs, (1, 1), "VALID", dimension_numbers=("NHWC", "HWIO", "NHWC"),
        precision=lax.Precision.HIGH,
    )
    numer = numer.reshape(rows_x, blocks, BY, nt, ZB)
    pos_x = jnp.arange(len_x, dtype=jnp.int32)
    out_x = jnp.arange(rows_x, dtype=jnp.int32)
    pos_y = half + jnp.arange(BY, dtype=jnp.int32)
    pos_z = half + jnp.arange(BZ, dtype=jnp.int32)
    squares = field_in * field_in
    energy = contract(
        "xyz,zn->xyn", squares, band_table(pos_z, jnp.arange(BZ, dtype=jnp.int32), len_z)
    )
    energy = contract(
        "xyn,ym->xmn", energy, band_table(pos_y, jnp.arange(BY, dtype=jnp.int32), len_y)
    )
    energy = contract("xmn,xl->lmn", energy, band_table(pos_x, out_x, len_x))
    energy = jnp.transpose(energy.reshape(rows_x, BY, blocks, ZB), (0, 2, 1, 3))[:, :, :, None]
    scores = numer / jnp.sqrt(energy + epsilon)
    weights = counts.astype(jnp.float32)
    weighted = weights[:, None] * jnp.exp(sharpness * scores)
    grouped = jnp.sum(weighted.reshape(rows_x, blocks, BY, FIELDS, nt // FIELDS, ZB), axis=4)
    totals = jnp.sum(weights.reshape(FIELDS, nt // FIELDS), axis=1)
    fields = jnp.log(grouped / totals[:, None])
    fields = jnp.transpose(fields, (3, 0, 2, 1, 4))
    return fields.reshape(FIELDS, rows_x, BY * BZ)


def solution(mesh):
    in_specs = (P(("grp", "gx"), None), P(None, "gx"), P(), P(), P())
    out_specs = P(None, ("grp", "gx"), None)
    return jax.shard_map(local, mesh=mesh, in_specs=in_specs, out_specs=out_specs, check_vma=False)
```

profile of v0, /device:TPU:0, one launch (start us, length us, event | category | flops | bytes accessed | tf_op | source)
XLA Modules:
  0.0 94.6 jit_solution(142638842370766325)
XLA Ops:
  0.0 0.8 fusion.81
  0.9 2.4 %collective-permute-start = (f32[8,8,112]{2,0,1:T(8,128)S(1)}, f32[8,8,112]{2,0,1:T(8,128)S(1)}, u32[]{:S(2)}, u32[]{:S(2)}) collective-permute-start(f32[8,8,112]{2,0,1:T(8,128)S(1)} %copy.55), channel_id=1, source_target_pairs={{0,1},{1,2},{2,3},{3,4},{4,5},{5,6},{6,7},{7,8},{8,9},{9,10},{10,1... | collective-permute-start | bytes 86024 | tf_op jit(solution)/shard_map/ppermute | solution.py:26
  3.3 1.3 %collective-permute-start.1 = (f32[8,8,112]{2,0,1:T(8,128)S(1)}, f32[8,8,112]{2,0,1:T(8,128)S(1)}, u32[]{:S(2)}, u32[]{:S(2)}) collective-permute-start(f32[8,8,112]{2,0,1:T(8,128)S(1)} %copy.56), channel_id=1, source_target_pairs={{1,0},{2,1},{3,2},{4,3},{5,4},{6,5},{7,6},{8,7},{9,8},{10,9},{11,1... | collective-permute-start | bytes 86024 | tf_op jit(solution)/shard_map/ppermute | solution.py:27
  4.6 3.3 %collective-permute-start.2 = (f32[1,8,256]{2,1,0:T(8,128)}, f32[1,8,256]{2,1,0:T(8,128)S(1)}, u32[]{:S(2)}, u32[]{:S(2)}) collective-permute-start(f32[1,8,256]{2,1,0:T(8,128)} %bitcast.75), channel_id=1, source_target_pairs={{0,1},{1,0},{2,3},{3,2},{4,5},{5,4},{6,7},{7,6},{8,9},{9,8},{10,11... | collective-permute-start | bytes 24584 | tf_op jit(solution)/shard_map/ppermute | solution.py:52
  9.3 0.8 maximum_select_fusion.3
  10.1 1.6 %collective-permute-start.3 = (f32[2,8,256]{2,1,0:T(8,128)S(1)}, f32[2,8,256]{2,1,0:T(8,128)S(1)}, u32[]{:S(2)}, u32[]{:S(2)}) collective-permute-start(f32[2,8,256]{2,1,0:T(8,128)S(1)} %maximum_select_fusion.3), channel_id=1, source_target_pairs={{0,2},{1,3},{2,0},{3,1},{4,6},{5,7},{6,4},{7,5},{8,10},{9,11},{10,... | collective-permute-start | bytes 49160 | tf_op jit(solution)/shard_map/ppermute | solution.py:52
  11.8 0.9 reshape.109
  14.0 2.4 %collective-permute-start.4 = (f32[4,8,256]{2,1,0:T(8,128)S(1)}, f32[4,8,256]{2,1,0:T(8,128)S(1)}, u32[]{:S(2)}, u32[]{:S(2)}) collective-permute-start(f32[4,8,256]{2,1,0:T(8,128)S(1)} %maximum_select_fusion.2), channel_id=1, source_target_pairs={{0,4},{1,5},{2,6},{3,7},{4,0},{5,1},{6,2},{7,3},{8,12},{9,13},{10,... | collective-permute-start | bytes 98312 | tf_op jit(solution)/shard_map/ppermute | solution.py:52
  17.3 5.4 %fusion.80 = (f32[31,7,8,32]{3,0,2,1:T(8,128)}, f32[31,7,8,32]{3,0,2,1:T(8,128)}, f32[31,7,8,32]{3,0,2,1:T(8,128)}, f32[31,7,8,32]{3,0,2,1:T(8,128)}, f32[31,7,8...) fusion(f32[31,7,24,32]{3,0,2,1:T(8,128)S(1)} %fusion.25), kind=kLoop, calls=%fused_computation.162 | loop fusion | bytes 7110656 | tf_op jit(solution)/shard_map/slice | solution.py:108
  23.3 2.7 %collective-permute-start.5 = (f32[8,8,256]{2,1,0:T(8,128)S(1)}, f32[8,8,256]{2,1,0:T(8,128)S(1)}, u32[]{:S(2)}, u32[]{:S(2)}) collective-permute-start(f32[8,8,256]{2,1,0:T(8,128)S(1)} %maximum_select_fusion.1), channel_id=1, source_target_pairs={{0,8},{1,9},{2,10},{3,11},{4,12},{5,13},{6,14},{7,15},{8,0},{9,1},... | collective-permute-start | bytes 196616 | tf_op jit(solution)/shard_map/ppermute | solution.py:52
  26.4 1.0 %copy.89 = f32[16,7,8,16]{3,0,2,1:T(8,128)} copy(f32[16,7,8,16]{3,1,2,0:T(8,128)S(1)} %bitcast.74) | data formatting | bytes 114688 | tf_op jit(solution)/shard_map/sqrt | solution.py:128
  27.4 10.6 %concatenate.31 = f32[31,7,8,512]{3,0,2,1:T(8,128)} concatenate(f32[31,7,8,32]{3,0,2,1:T(8,128)} %get-tuple-element.34, f32[31,7,8,32]{3,0,2,1:T(8,128)} %get-tuple-element.33, f32[31,7,8,32]{3,0,2,1:T(8,128)} %get-tuple-element.32, f32[31,7,8,32]{3,0,2,1:T(8,128)} %get-tuple-element.31, f32[31,7,8,32]{3,0,2,1:T(8,128)} %get-tuple-element.30, ...), dimensions={3} | concatenate | bytes 7110656 | tf_op jit(solution)/shard_map/concatenate | solution.py:108
  40.5 0.8 broadcast_select_fusion
  43.0 1.7 %bitcast_add_fusion.3 = f32[8,16,16,16]{3,2,0,1:T(8,128)} fusion(f32[8,16,16,16]{3,1,0,2:T(8,128)S(1)} %broadcast_select_fusion.1, f32[8,16,16,16]{2,3,0,1:T(8,128)S(1)} %copy.76, pred[8]{0:T(512)(128)(4,1)S(1)} %get-tuple-element.56, pred[8]{0:T(512)(128)(4,1)S(1)} %get-tuple-element.55, pred[8]{0:T(512)(128)(4,1)S(1)} %get-tuple-element.54), kind=kLoop, calls=%fused_computation.16 | loop fusion | flops 163840 | bytes 393240 | tf_op jit(solution)/shard_map/add | solution.py:73
  44.7 2.2 %copy.79 = f32[8,16,16,16]{1,2,0,3:T(8,128)S(1)} copy(f32[8,16,16,16]{3,2,0,1:T(8,128)} %bitcast_add_fusion.3) | data formatting | bytes 262144 | tf_op jit(solution)/shard_map/add | solution.py:73
  46.9 1.3 %bitcast_add_fusion.1 = f32[8,16,16,16]{1,2,0,3:T(8,128)} fusion(f32[8,16,16,16]{1,2,0,3:T(8,128)S(1)} %copy.79, f32[8,16,16,16]{2,3,0,1:T(8,128)S(1)} %copy.76, f32[8,16,16,16]{3,1,0,2:T(8,128)S(1)} %broadcast_select_fusion.1, pred[8]{0:T(512)(128)(4,1)S(1)} %get-tuple-element.57, pred[8]{0:T(512)(128)(4,1)S(1)} %get-tuple-element.58), kind=kLoop, calls=%fused_computation.14 | loop fusion | flops 131072 | bytes 524304 | tf_op jit(solution)/shard_map/add | solution.py:73
  48.1 1.5 %copy.82 = f32[8,16,16,16]{2,1,0,3:T(8,128)S(1)} copy(f32[8,16,16,16]{1,2,0,3:T(8,128)} %bitcast_add_fusion.1) | data formatting | bytes 262144 | tf_op jit(solution)/shard_map/add | solution.py:73
  51.0 3.9 %fusion.3 = f32[256,4096]{1,0:T(8,128)} fusion(f32[256,128]{0,1:T(8,128)S(1)} %reshape.111, s32[4096]{0:T(1024)S(1)} %iota.85, s32[4096]{0:T(1024)S(1)} %sub.88, s32[128]{0:T(128)S(1)} %iota.82, s32[128]{0:T(128)S(1)} %iota.79), kind=kOutput, calls=%fused_computation.4 | convolution fusion | flops 1612185600 | bytes 4359168 | tf_op jit(solution)/shard_map/dot_general | solution.py:89
  54.9 4.9 %reshape.112 = f32[16,1,512,128]{3,2,0,1:T(8,128)} reshape(f32[256,4096]{1,0:T(8,128)} %fusion.3) | data formatting | bytes 8388608 | tf_op jit(solution)/shard_map/reshape | solution.py:90
  59.9 15.6 %fusion = f32[16,8,7,128]{3,1,2,0:T(8,128)S(1)} fusion(f32[16,1,512,128]{3,2,0,1:T(8,128)} %reshape.112, f32[31,8,7,512]{3,0,2,1:T(8,128)} %bitcast.73), kind=kOutput, calls=%fused_computation | convolution fusion | flops 5637144576 | bytes 8208384 | tf_op jit(solution)/shard_map/conv_general_dilated | solution.py:110
  75.6 6.5 %reshape.113 = f32[16,7,8,4,2,16]{5,4,3,0,2,1:T(2,128)} reshape(f32[16,8,7,128]{3,0,2,1:T(8,128)S(1)} %copy.85) | data formatting | bytes 917504 | tf_op jit(solution)/shard_map/reshape | solution.py:114
  82.1 9.4 %multiply_reduce_fusion = f32[16,7,8,4,16]{4,3,0,2,1:T(4,128)S(1)} fusion(f32[16,7,8,4,2,16]{5,4,3,0,2,1:T(2,128)} %reshape.113, f32[16,7,8,16]{3,0,2,1:T(8,128)S(1)} %copy-done.2, f32[4,2]{1,0:T(4,128)S(1)} %mul.33), kind=kLoop, calls=%fused_computation.2 | loop fusion | flops 401408 | bytes 745504 | tf_op jit(solution)/shard_map/reduce_sum | solution.py:131
  92.1 1.1 %copy.90 = f32[4,16,8,7,16]{4,3,2,1,0:T(8,128)S(1)} copy(f32[4,16,8,7,16]{4,0,1,2,3:T(4,128)S(1)} %log_bitcast_fusion) | data formatting | bytes 458752 | tf_op jit(solution)/shard_map/log | solution.py:133
  93.2 1.4 %reshape.114 = f32[4,16,896]{2,1,0:T(8,128)} reshape(f32[4,16,8,7,16]{4,3,2,1,0:T(8,128)S(1)} %copy.90) | data formatting | bytes 458752 | tf_op jit(solution)/shard_map/reshape | solution.py:135
  (81 shorter events, 10.4 us)
Async XLA Ops:
  0.9 15.6 %collective-permute-start = (f32[8,8,112]{2,0,1:T(8,128)S(1)}, f32[8,8,112]{2,0,1:T(8,128)S(1)}, u32[]{:S(2)}, u32[]{:S(2)}) collective-permute-start(f32[8,8,112]{2,0,1:T(8,128)S(1)} %copy.55), channel_id=1, source_target_pairs={{0,1},{1,2},{2,3},{3,4},{4,5},{5,6},{6,7},{7,8},{8,9},{9,10},{10,1... | collective-permute-start | bytes 86024 | tf_op jit(solution)/shard_map/ppermute | solution.py:26
  3.3 13.2 %collective-permute-start.1 = (f32[8,8,112]{2,0,1:T(8,128)S(1)}, f32[8,8,112]{2,0,1:T(8,128)S(1)}, u32[]{:S(2)}, u32[]{:S(2)}) collective-permute-start(f32[8,8,112]{2,0,1:T(8,128)S(1)} %copy.56), channel_id=1, source_target_pairs={{1,0},{2,1},{3,2},{4,3},{5,4},{6,5},{7,6},{8,7},{9,8},{10,9},{11,1... | collective-permute-start | bytes 86024 | tf_op jit(solution)/shard_map/ppermute | solution.py:27
  4.6 4.7 %collective-permute-start.2 = (f32[1,8,256]{2,1,0:T(8,128)}, f32[1,8,256]{2,1,0:T(8,128)S(1)}, u32[]{:S(2)}, u32[]{:S(2)}) collective-permute-start(f32[1,8,256]{2,1,0:T(8,128)} %bitcast.75), channel_id=1, source_target_pairs={{0,1},{1,0},{2,3},{3,2},{4,5},{5,4},{6,7},{7,6},{8,9},{9,8},{10,11... | collective-permute-start | bytes 24584 | tf_op jit(solution)/shard_map/ppermute | solution.py:52
  10.1 3.9 %collective-permute-start.3 = (f32[2,8,256]{2,1,0:T(8,128)S(1)}, f32[2,8,256]{2,1,0:T(8,128)S(1)}, u32[]{:S(2)}, u32[]{:S(2)}) collective-permute-start(f32[2,8,256]{2,1,0:T(8,128)S(1)} %maximum_select_fusion.3), channel_id=1, source_target_pairs={{0,2},{1,3},{2,0},{3,1},{4,6},{5,7},{6,4},{7,5},{8,10},{9,11},{10,... | collective-permute-start | bytes 49160 | tf_op jit(solution)/shard_map/ppermute | solution.py:52
  14.0 9.2 %collective-permute-start.4 = (f32[4,8,256]{2,1,0:T(8,128)S(1)}, f32[4,8,256]{2,1,0:T(8,128)S(1)}, u32[]{:S(2)}, u32[]{:S(2)}) collective-permute-start(f32[4,8,256]{2,1,0:T(8,128)S(1)} %maximum_select_fusion.2), channel_id=1, source_target_pairs={{0,4},{1,5},{2,6},{3,7},{4,0},{5,1},{6,2},{7,3},{8,12},{9,13},{10,... | collective-permute-start | bytes 98312 | tf_op jit(solution)/shard_map/ppermute | solution.py:52
  22.7 4.7 %copy-start = (f32[31,7,8,32]{3,0,2,1:T(8,128)S(1)}, f32[31,7,8,32]{3,0,2,1:T(8,128)}, u32[]{:S(2)}) copy-start(f32[31,7,8,32]{3,0,2,1:T(8,128)} %get-tuple-element.19) | copy-start | bytes 666628
  22.7 4.7 %copy-start.1 = (f32[31,7,8,32]{3,0,2,1:T(8,128)S(1)}, f32[31,7,8,32]{3,0,2,1:T(8,128)}, u32[]{:S(2)}) copy-start(f32[31,7,8,32]{3,0,2,1:T(8,128)} %get-tuple-element.20) | copy-start | bytes 666628
  23.3 14.7 %collective-permute-start.5 = (f32[8,8,256]{2,1,0:T(8,128)S(1)}, f32[8,8,256]{2,1,0:T(8,128)S(1)}, u32[]{:S(2)}, u32[]{:S(2)}) collective-permute-start(f32[8,8,256]{2,1,0:T(8,128)S(1)} %maximum_select_fusion.1), channel_id=1, source_target_pairs={{0,8},{1,9},{2,10},{3,11},{4,12},{5,13},{6,14},{7,15},{8,0},{9,1},... | collective-permute-start | bytes 196616 | tf_op jit(solution)/shard_map/ppermute | solution.py:52
  75.5 6.6 %copy-start.2 = (f32[16,7,8,16]{3,0,2,1:T(8,128)S(1)}, f32[16,7,8,16]{3,0,2,1:T(8,128)}, u32[]{:S(2)}) copy-start(f32[16,7,8,16]{3,0,2,1:T(8,128)} %copy.89) | copy-start | bytes 172036
where the time goes:
time: 95.4 us; the launch traced here: 94.6 us
  local copies, waits for them, and re-layouts  41.2 us (43%)
  matrix products  20.3 us (21%)
  other arithmetic  18.8 us (20%)
  starting transfers between devices  13.7 us (14%)
    conv_general_dilated x1, matrix products, local(): lax.conv_general_dilated(cols, rhs, (1, 1), 'VALID', dimension_numbers=('...  15.6 us
    concatenate x1, local copies, waits for them, and re-layouts, local(): cols = jnp.concatenate([zwin[:, :, b:b + BY] for b in range(TS)], axis=3)  10.6 us
    ppermute x4, starting transfers between devices, gather_planes(): other = lax.ppermute(held, axis, pairs)  10 us
    reduce_sum x1, other arithmetic, local(): jnp.sum(weighted.reshape(rows_x, blocks, BY, FIELDS, nt // FIELDS, ZB), a...  9.44 us
    reshape x1, local copies, waits for them, and re-layouts, local(): numer = numer.reshape(rows_x, blocks, BY, nt, ZB)  6.48 us
    slice x1, local copies, waits for them, and re-layouts, local(): cols = jnp.concatenate([zwin[:, :, b:b + BY] for b in range(TS)], axis=3)  5.43 us
    reshape x1, local copies, waits for them, and re-layouts, toeplitz_rhs(): return rhs.reshape(TS, 1, TS * (TS + ZB), nt * ZB)  4.91 us
    dot_general x1, matrix products, toeplitz_rhs(): rhs = jnp.dot(kt, shift, precision=lax.Precision.HIGHEST)  3.92 us
  transfers between devices with their start and end apart: 6, of which 0 were waited for; matrix products, arithmetic and copies ran while one was open for 24% of the time, Pallas kernels for 0%

commit v1 on v0

--- a/solution.py
+++ b/solution.py
@@ -2,6 +2,8 @@
 import jax.numpy as jnp
 import numpy as np
 from jax import lax
+from jax.experimental import pallas as pl
+from jax.experimental.pallas import tpu as pltpu
 from jax.sharding import PartitionSpec as P
 
 BY = 8
@@ -80,14 +82,31 @@
 def toeplitz_rhs(kernels):
     nt = kernels.shape[0]
     kt = jnp.transpose(kernels, (1, 2, 3, 0)).reshape(TS * TS, TS * nt)
-    c = lax.broadcasted_iota(jnp.int32, (TS, nt, TS + ZB, nt, ZB), 0)
-    t = lax.broadcasted_iota(jnp.int32, (TS, nt, TS + ZB, nt, ZB), 1)
-    w = lax.broadcasted_iota(jnp.int32, (TS, nt, TS + ZB, nt, ZB), 2)
-    t2 = lax.broadcasted_iota(jnp.int32, (TS, nt, TS + ZB, nt, ZB), 3)
-    zl = lax.broadcasted_iota(jnp.int32, (TS, nt, TS + ZB, nt, ZB), 4)
-    shift = ((w - zl == c) & (t == t2)).astype(jnp.float32).reshape(TS * nt, -1)
-    rhs = jnp.dot(kt, shift, precision=lax.Precision.HIGHEST)
+    dims = (TS, nt, TS + ZB, nt, ZB)
+    c = lax.broadcasted_iota(jnp.int32, dims, 0)
+    t = lax.broadcasted_iota(jnp.int32, dims, 1)
+    w = lax.broadcasted_iota(jnp.int32, dims, 2)
+    t2 = lax.broadcasted_iota(jnp.int32, dims, 3)
+    zl = lax.broadcasted_iota(jnp.int32, dims, 4)
+    shift = ((w - zl == c) & (t == t2)).astype(jnp.float32).reshape(TS * nt, TS + ZB, nt * ZB)
+    rhs = jnp.einsum("rk,kwn->rwn", kt, shift, precision=lax.Precision.HIGHEST)
     return rhs.reshape(TS, 1, TS * (TS + ZB), nt * ZB)
+
+
+def im2col_kernel(p_ref, o_ref):
+    for zb in range(o_ref.shape[1]):
+        for b in range(TS):
+            o_ref[:, zb, :, b * (TS + ZB):(b + 1) * (TS + ZB)] = p_ref[:, b:b + BY, zb * ZB: zb * ZB + TS + ZB]
+
+
+def im2col(padded, blocks):
+    rows = padded.shape[0]
+    return pl.pallas_call(
+        im2col_kernel,
+        out_shape=jax.ShapeDtypeStruct((rows, blocks, BY, TS * (TS + ZB)), jnp.float32),
+        in_specs=[pl.BlockSpec(memory_space=pltpu.VMEM)],
+        out_specs=pl.BlockSpec(memory_space=pltpu.VMEM),
+    )(padded)
 
 
 def local(volume, bank, orient, bank_id, counts):
@@ -100,18 +119,19 @@
     len_z = BZ + TS
     blocks = BZ // ZB
     planes = gather_planes(bank, "gx")
-    kernels = rotated_kernels(planes, orient, bank_id)
+    per = nt // FIELDS
+    order = [k * per + p for p in range(per) for k in range(FIELDS)]
+    kernels = rotated_kernels(planes, orient[np.array(order)], bank_id[np.array(order)])
     rhs = toeplitz_rhs(kernels)
     field_in = extended(grid, (("gx", 0),), half)
     padded = jnp.pad(field_in, ((0, 0), (half, TS - half), (half, TS - half)))
-    zwin = jnp.stack([padded[: len_x - 1, :, zb * ZB: zb * ZB + TS + ZB] for zb in range(blocks)], axis=1)
-    cols = jnp.concatenate([zwin[:, :, b: b + BY] for b in range(TS)], axis=3)
+    cols = im2col(padded[: len_x - 1], blocks)
     cols = cols.reshape(1, len_x - 1, blocks * BY, TS * (TS + ZB))
     numer = lax.conv_general_dilated(
         cols, rhs, (1, 1), "VALID", dimension_numbers=("NHWC", "HWIO", "NHWC"),
         precision=lax.Precision.HIGH,
     )
-    numer = numer.reshape(rows_x, blocks, BY, nt, ZB)
+    numer = numer.reshape(rows_x, blocks * BY, nt * ZB)
     pos_x = jnp.arange(len_x, dtype=jnp.int32)
     out_x = jnp.arange(rows_x, dtype=jnp.int32)
     pos_y = half + jnp.arange(BY, dtype=jnp.int32)
@@ -124,13 +144,20 @@
         "xyn,ym->xmn", energy, band_table(pos_y, jnp.arange(BY, dtype=jnp.int32), len_y)
     )
     energy = contract("xmn,xl->lmn", energy, band_table(pos_x, out_x, len_x))
-    energy = jnp.transpose(energy.reshape(rows_x, BY, blocks, ZB), (0, 2, 1, 3))[:, :, :, None]
+    energy = jnp.transpose(energy.reshape(rows_x, BY, blocks, ZB), (0, 2, 1, 3))
+    energy = jnp.tile(energy.reshape(rows_x, blocks * BY, ZB), (1, 1, nt))
     scores = numer / jnp.sqrt(energy + epsilon)
-    weights = counts.astype(jnp.float32)
-    weighted = weights[:, None] * jnp.exp(sharpness * scores)
-    grouped = jnp.sum(weighted.reshape(rows_x, blocks, BY, FIELDS, nt // FIELDS, ZB), axis=4)
-    totals = jnp.sum(weights.reshape(FIELDS, nt // FIELDS), axis=1)
-    fields = jnp.log(grouped / totals[:, None])
+    weights = counts[np.array(order)].astype(jnp.float32)
+    weighted = jnp.repeat(weights, ZB)[None, None] * jnp.exp(sharpness * scores)
+    half_lanes = FIELDS * ZB
+    grouped = weighted[:, :, :half_lanes]
+    for p in range(1, per):
+        grouped = grouped + weighted[:, :, p * half_lanes:(p + 1) * half_lanes]
+    totals = weights[:FIELDS]
+    for p in range(1, per):
+        totals = totals + weights[p * FIELDS:(p + 1) * FIELDS]
+    fields = jnp.log(grouped / jnp.repeat(totals, ZB)[None, None])
+    fields = fields.reshape(rows_x, blocks, BY, FIELDS, ZB)
     fields = jnp.transpose(fields, (3, 0, 2, 1, 4))
     return fields.reshape(FIELDS, rows_x, BY * BZ)
 

time: 95.4 us -> 79.5 us (0.83)
  other arithmetic: 18.8 us -> 8.78 us
  local copies, waits for them, and re-layouts: 41.2 us -> 33.3 us
  Pallas kernels: 0 us -> 6.03 us
  matrix products: 20.3 us -> 16.2 us
  waiting for transfers between devices: 0.02 us -> 1.44 us
    concatenate x1 -> x0, local copies, waits for them, and re-layouts: 10.6 us -> none  [local(): cols = jnp.concatenate([zwin[:, :, b:b + BY] for b in range(TS)], axis=3)]
    reduce_sum x2 -> x0, other arithmetic: 9.56 us -> none  [the longest x1 9.44 us: local(): jnp.sum(weighted.reshape(rows_x, blocks, BY, FIELDS, nt // FIELDS, ZB), a...]
    reshape x2 -> x1, local copies, waits for them, and re-layouts: 11.4 us -> 2.05 us  [local(): fields = fields.reshape(rows_x, blocks, BY, FIELDS, ZB)]
    pallas_call x0 -> x1, Pallas kernels: none -> 6.03 us  [im2col(): pl.pallas_call(im2col_kernel, out_shape=jax.ShapeDtypeStruct((rows, block...]
    pallas_call x0 -> x1, local copies, waits for them, and re-layouts: none -> 5.81 us  [im2col(): pl.pallas_call(im2col_kernel, out_shape=jax.ShapeDtypeStruct((rows, block...]
    slice x1, local copies, waits for them, and re-layouts: 5.43 us -> 0.84 us  [local(): cols = im2col(padded[:len_x - 1], blocks)]
    and x0 -> x1, local copies, waits for them, and re-layouts: none -> 3.7 us  [toeplitz_rhs(): (w - zl == c) & (t == t2)]
    gather x0 -> x3, local copies, waits for them, and re-layouts: none -> 3.24 us  [the longest x1 1.3 us: local(): orient[np.array(order)]]
  transfers between devices with their start and end apart: 6 -> 6, of which waited for: 0 -> 1; matrix products, arithmetic and copies ran while one was open for 24% -> 26% of each run, Pallas kernels for 0% -> 8%
where the time goes in v1:
time: 79.5 us; the launch traced here: 79 us
  local copies, waits for them, and re-layouts  33.3 us (42%)
  matrix products  16.2 us (20%)
  starting transfers between devices  12.8 us (16%)
  other arithmetic  8.78 us (11%)
  Pallas kernels  6.03 us (8%)
  waiting for transfers between devices  1.44 us (2%)
    conv_general_dilated x1, matrix products, local(): lax.conv_general_dilated(cols, rhs, (1, 1), 'VALID', dimension_numbers=('...  13.5 us
    ppermute x4, starting transfers between devices, gather_planes(): other = lax.ppermute(held, axis, pairs)  9.55 us
    pallas_call x1, Pallas kernels, im2col(): pl.pallas_call(im2col_kernel, out_shape=jax.ShapeDtypeStruct((rows, block...  6.03 us
    pallas_call x1, local copies, waits for them, and re-layouts, im2col(): pl.pallas_call(im2col_kernel, out_shape=jax.ShapeDtypeStruct((rows, block...  5.81 us
    add x2, local copies, waits for them, and re-layouts, rotated_kernels(): rotated + jnp.where(expand(order_row == row), jnp.transpose(picked, perm)...  3.73 us
    and x1, local copies, waits for them, and re-layouts, toeplitz_rhs(): (w - zl == c) & (t == t2)  3.7 us
    add x2, other arithmetic, rotated_kernels(): rotated + jnp.where(expand(order_row == row), jnp.transpose(picked, perm)...  2.99 us
    transpose x1, local copies, waits for them, and re-layouts, local(): fields = jnp.transpose(fields, (3, 0, 2, 1, 4))  2.58 us
  transfers between devices with their start and end apart: 6, of which 1 were waited for; matrix products, arithmetic and copies ran while one was open for 26% of the time, Pallas kernels for 8%

profile of v1, /device:TPU:0, one launch (start us, length us, event | category | flops | bytes accessed | tf_op | source)
XLA Modules:
  0.0 79.0 jit_solution(17312531964029615572)
XLA Ops:
  1.3 2.0 %collective-permute-start = (f32[8,8,112]{2,1,0:T(8,128)S(1)}, f32[8,8,112]{2,1,0:T(8,128)S(1)}, u32[]{:S(2)}, u32[]{:S(2)}) collective-permute-start(f32[8,8,112]{2,1,0:T(8,128)S(1)} %slice.52), channel_id=1, source_target_pairs={{0,1},{1,2},{2,3},{3,4},{4,5},{5,6},{6,7},{7,8},{8,9},{9,10},{10,1... | collective-permute-start | bytes 86024 | tf_op jit(solution)/shard_map/ppermute | solution.py:28
  3.3 1.3 %collective-permute-start.1 = (f32[8,8,112]{2,1,0:T(8,128)S(1)}, f32[8,8,112]{2,1,0:T(8,128)S(1)}, u32[]{:S(2)}, u32[]{:S(2)}) collective-permute-start(f32[8,8,112]{2,1,0:T(8,128)S(1)} %slice.54), channel_id=1, source_target_pairs={{1,0},{2,1},{3,2},{4,3},{5,4},{6,5},{7,6},{8,7},{9,8},{10,9},{11,1... | collective-permute-start | bytes 86024 | tf_op jit(solution)/shard_map/ppermute | solution.py:29
  4.6 1.0 %fusion = pred[16,8,32,8,16]{2,4,3,1,0:T(8,128)(4,1)S(1)} fusion(), kind=kLoop, calls=%fused_computation.5 | loop fusion | flops 2097152 | bytes 524288 | tf_op jit(solution)/shard_map/and | solution.py:91
  6.9 1.3 %gather_fusion.1 = s32[8]{0:T(128)S(1)} fusion(s32[8]{0:T(128)} %param.13, s32[1024]{0:T(1024)S(1)} %pad_clamp_fusion), kind=kCustom, calls=%fused_computation.1 | custom fusion | bytes 96 | tf_op jit(solution)/shard_map/gather | solution.py:124
  8.3 1.3 %gather_fusion = s32[8]{0:T(128)S(1)} fusion(s32[8]{0:T(128)} %param.15, s32[1024]{0:T(1024)S(1)} %pad_clamp_fusion), kind=kCustom, calls=%fused_computation | custom fusion | bytes 96 | tf_op jit(solution)/shard_map/gather | solution.py:150
  10.5 4.8 %collective-permute-start.3 = (f32[2,8,256]{2,1,0:T(8,128)S(1)}, f32[2,8,256]{2,1,0:T(8,128)S(1)}, u32[]{:S(2)}, u32[]{:S(2)}) collective-permute-start(f32[2,8,256]{2,1,0:T(8,128)S(1)} %maximum_select_fusion.3), channel_id=1, source_target_pairs={{0,2},{1,3},{2,0},{3,1},{4,6},{5,7},{6,4},{7,5},{8,10},{9,11},{10,... | collective-permute-start | bytes 49160 | tf_op jit(solution)/shard_map/ppermute | solution.py:54
  15.3 0.9 %reshape.273 = f32[16,8,112]{2,1,0:T(8,128)S(1)} reshape(f32[16,896]{1,0:T(8,128)} %param.11) | data formatting | bytes 114688 | tf_op jit(solution)/shard_map/reshape | solution.py:116
  16.2 3.7 %copy.65 = pred[128,32,128]{2,0,1:T(32,128)(4,1)} copy(pred[128,32,128]{1,2,0:T(8,128)(4,1)S(1)} %bitcast.60) | data formatting | bytes 1048576 | tf_op jit(solution)/shard_map/and | solution.py:91
  20.3 1.6 %collective-permute-start.4 = (f32[4,8,256]{2,1,0:T(8,128)S(1)}, f32[4,8,256]{2,1,0:T(8,128)S(1)}, u32[]{:S(2)}, u32[]{:S(2)}) collective-permute-start(f32[4,8,256]{2,1,0:T(8,128)S(1)} %maximum_select_fusion.2), channel_id=1, source_target_pairs={{0,4},{1,5},{2,6},{3,7},{4,0},{5,1},{6,2},{7,3},{8,12},{9,13},{10,... | collective-permute-start | bytes 98312 | tf_op jit(solution)/shard_map/ppermute | solution.py:54
  22.8 1.4 %collective-permute-done.4 = f32[4,8,256]{2,1,0:T(8,128)S(1)} collective-permute-done((f32[4,8,256]{2,1,0:T(8,128)S(1)}, f32[4,8,256]{2,1,0:T(8,128)S(1)}, u32[]{:S(2)}, u32[]{:S(2)}) %collective-permute-start.4) | collective-permute-done | bytes 32800 | tf_op jit(solution)/shard_map/ppermute | solution.py:54
  24.3 2.7 %collective-permute-start.5 = (f32[8,8,256]{2,1,0:T(8,128)S(1)}, f32[8,8,256]{2,1,0:T(8,128)S(1)}, u32[]{:S(2)}, u32[]{:S(2)}) collective-permute-start(f32[8,8,256]{2,1,0:T(8,128)S(1)} %maximum_select_fusion.1), channel_id=1, source_target_pairs={{0,8},{1,9},{2,10},{3,11},{4,12},{5,13},{6,14},{7,15},{8,0},{9,1},... | collective-permute-start | bytes 196616 | tf_op jit(solution)/shard_map/ppermute | solution.py:54
  27.8 6.0 %shard_map.109 = f32[31,7,8,512]{3,2,1,0:T(8,128)} custom-call(f32[31,24,128]{2,1,0:T(8,128)} %pad_slice_fusion.p_ref), custom_call_target="tpu_custom_call" | custom-call | tf_op jit(solution)/shard_map/pallas_call | solution.py:104
  33.8 5.8 %copy.38 = f32[31,7,8,512]{3,0,2,1:T(8,128)} copy(f32[31,7,8,512]{3,2,1,0:T(8,128)} %shard_map.109) | data formatting | bytes 7110656 | tf_op jit(solution)/shard_map/pallas_call | solution.py:104
  40.2 1.1 %copy.73 = f32[16,56,128]{2,0,1:T(8,128)} copy(f32[16,56,128]{1,2,0:T(8,128)S(1)} %bitcast.62) | data formatting | bytes 917504 | tf_op jit(solution)/shard_map/sqrt | solution.py:149
  46.5 1.7 %bitcast_add_fusion.3 = f32[8,16,16,16]{3,2,0,1:T(8,128)} fusion(f32[8,16,16,16]{3,1,0,2:T(8,128)S(1)} %broadcast_select_fusion.1, f32[8,16,16,16]{2,3,0,1:T(8,128)S(1)} %copy.57, pred[8]{0:T(512)(128)(4,1)S(1)} %get-tuple-element.40, pred[8]{0:T(512)(128)(4,1)S(1)} %get-tuple-element.39, pred[8]{0:T(512)(128)(4,1)S(1)} %get-tuple-element.38), kind=kLoop, calls=%fused_computation.14 | loop fusion | flops 163840 | bytes 393240 | tf_op jit(solution)/shard_map/add | solution.py:75
  48.2 2.2 %copy.60 = f32[8,16,16,16]{1,2,0,3:T(8,128)S(1)} copy(f32[8,16,16,16]{3,2,0,1:T(8,128)} %bitcast_add_fusion.3) | data formatting | bytes 262144 | tf_op jit(solution)/shard_map/add | solution.py:75
  50.4 1.3 %bitcast_add_fusion.1 = f32[8,16,16,16]{1,2,0,3:T(8,128)} fusion(f32[8,16,16,16]{1,2,0,3:T(8,128)S(1)} %copy.60, f32[8,16,16,16]{2,3,0,1:T(8,128)S(1)} %copy.57, f32[8,16,16,16]{3,1,0,2:T(8,128)S(1)} %broadcast_select_fusion.1, pred[8]{0:T(512)(128)(4,1)S(1)} %get-tuple-element.41, pred[8]{0:T(512)(128)(4,1)S(1)} %get-tuple-element.42), kind=kLoop, calls=%fused_computation.12 | loop fusion | flops 131072 | bytes 524304 | tf_op jit(solution)/shard_map/add | solution.py:75
  51.7 1.5 %copy.63 = f32[8,16,16,16]{2,1,0,3:T(8,128)S(1)} copy(f32[8,16,16,16]{1,2,0,3:T(8,128)} %bitcast_add_fusion.1) | data formatting | bytes 262144 | tf_op jit(solution)/shard_map/add | solution.py:75
  54.5 1.9 %fusion.10 = f32[256,32,128]{2,0,1:T(8,128)S(1)} fusion(pred[128,32,128]{2,0,1:T(32,128)(4,1)S(1)} %copy-done.2, f32[256,128]{0,1:T(8,128)S(1)} %reshape.275), kind=kOutput, calls=%fused_computation.33 | convolution fusion | flops 1610612736 | bytes 4849664 | tf_op jit(solution)/shard_map/rk,kwn->rwn/dot_general | solution.py:92
  56.4 2.4 %copy.66 = f32[256,32,128]{2,1,0:T(8,128)S(1)} copy(f32[256,32,128]{2,0,1:T(8,128)S(1)} %fusion.10) | data formatting | bytes 8388608 | tf_op jit(solution)/shard_map/rk,kwn->rwn/dot_general | solution.py:92
  58.9 13.5 %fusion.1 = f32[16,8,7,128]{3,1,2,0:T(8,128)S(1)} fusion(f32[16,1,512,128]{3,2,1,0:T(8,128)S(1)} %bitcast.59, f32[31,8,7,512]{3,0,2,1:T(8,128)S(1)} %bitcast.58), kind=kOutput, calls=%fused_computation.6 | convolution fusion | flops 5637144576 | bytes 8208384 | tf_op jit(solution)/shard_map/conv_general_dilated | solution.py:130
  73.0 2.1 %reshape.278 = f32[16,7,8,4,16]{4,3,2,1,0:T(4,128)} reshape(f32[16,56,64]{2,1,0:T(8,128)S(1)} %copy.74) | data formatting | bytes 458752 | tf_op jit(solution)/shard_map/reshape | solution.py:160
  75.0 2.6 %copy.75 = f32[4,16,8,7,16]{4,3,2,1,0:T(8,128)S(1)} copy(f32[4,16,8,7,16]{4,0,2,3,1:T(4,128)} %bitcast.61) | data formatting | bytes 458752 | tf_op jit(solution)/shard_map/transpose | solution.py:161
  77.6 1.4 %reshape.279 = f32[4,16,896]{2,1,0:T(8,128)} reshape(f32[4,16,8,7,16]{4,3,2,1,0:T(8,128)S(1)} %copy.75) | data formatting | bytes 458752 | tf_op jit(solution)/shard_map/reshape | solution.py:162
  (81 shorter events, 13.0 us)
Async XLA Ops:
  0.0 6.3 %copy-start = (s32[8]{0:T(128)S(1)}, s32[8]{0:T(128)}, u32[]{:S(2)}) copy-start(s32[8]{0:T(128)} %param.14) | copy-start | bytes 100
  0.0 9.7 %collective-permute-start.2 = (f32[1,8,256]{2,1,0:T(8,128)}, f32[1,8,256]{2,1,0:T(8,128)S(1)}, u32[]{:S(2)}, u32[]{:S(2)}) collective-permute-start(f32[1,8,256]{2,1,0:T(8,128)} %bitcast.65), channel_id=1, source_target_pairs={{0,1},{1,0},{2,3},{3,2},{4,5},{5,4},{6,7},{7,6},{8,9},{9,8},{10,11... | collective-permute-start | bytes 24584 | tf_op jit(solution)/shard_map/ppermute | solution.py:54
  1.3 20.6 %collective-permute-start = (f32[8,8,112]{2,1,0:T(8,128)S(1)}, f32[8,8,112]{2,1,0:T(8,128)S(1)}, u32[]{:S(2)}, u32[]{:S(2)}) collective-permute-start(f32[8,8,112]{2,1,0:T(8,128)S(1)} %slice.52), channel_id=1, source_target_pairs={{0,1},{1,2},{2,3},{3,4},{4,5},{5,6},{6,7},{7,8},{8,9},{9,10},{10,1... | collective-permute-start | bytes 86024 | tf_op jit(solution)/shard_map/ppermute | solution.py:28
  3.3 18.6 %collective-permute-start.1 = (f32[8,8,112]{2,1,0:T(8,128)S(1)}, f32[8,8,112]{2,1,0:T(8,128)S(1)}, u32[]{:S(2)}, u32[]{:S(2)}) collective-permute-start(f32[8,8,112]{2,1,0:T(8,128)S(1)} %slice.54), channel_id=1, source_target_pairs={{1,0},{2,1},{3,2},{4,3},{5,4},{6,5},{7,6},{8,7},{9,8},{10,9},{11,1... | collective-permute-start | bytes 86024 | tf_op jit(solution)/shard_map/ppermute | solution.py:29
  10.5 9.8 %collective-permute-start.3 = (f32[2,8,256]{2,1,0:T(8,128)S(1)}, f32[2,8,256]{2,1,0:T(8,128)S(1)}, u32[]{:S(2)}, u32[]{:S(2)}) collective-permute-start(f32[2,8,256]{2,1,0:T(8,128)S(1)} %maximum_select_fusion.3), channel_id=1, source_target_pairs={{0,2},{1,3},{2,0},{3,1},{4,6},{5,7},{6,4},{7,5},{8,10},{9,11},{10,... | collective-permute-start | bytes 49160 | tf_op jit(solution)/shard_map/ppermute | solution.py:54
  20.3 4.0 %collective-permute-start.4 = (f32[4,8,256]{2,1,0:T(8,128)S(1)}, f32[4,8,256]{2,1,0:T(8,128)S(1)}, u32[]{:S(2)}, u32[]{:S(2)}) collective-permute-start(f32[4,8,256]{2,1,0:T(8,128)S(1)} %maximum_select_fusion.2), channel_id=1, source_target_pairs={{0,4},{1,5},{2,6},{3,7},{4,0},{5,1},{6,2},{7,3},{8,12},{9,13},{10,... | collective-permute-start | bytes 98312 | tf_op jit(solution)/shard_map/ppermute | solution.py:54
  24.3 17.0 %collective-permute-start.5 = (f32[8,8,256]{2,1,0:T(8,128)S(1)}, f32[8,8,256]{2,1,0:T(8,128)S(1)}, u32[]{:S(2)}, u32[]{:S(2)}) collective-permute-start(f32[8,8,256]{2,1,0:T(8,128)S(1)} %maximum_select_fusion.1), channel_id=1, source_target_pairs={{0,8},{1,9},{2,10},{3,11},{4,12},{5,13},{6,14},{7,15},{8,0},{9,1},... | collective-permute-start | bytes 196616 | tf_op jit(solution)/shard_map/ppermute | solution.py:54
  53.2 1.3 %copy-start.2 = (pred[128,32,128]{2,0,1:T(32,128)(4,1)S(1)}, pred[128,32,128]{2,0,1:T(32,128)(4,1)}, u32[]{:S(2)}) copy-start(pred[128,32,128]{2,0,1:T(32,128)(4,1)} %copy.65) | copy-start | bytes 1572868
  56.4 2.4 %copy-start.1 = (f32[31,7,8,512]{3,0,2,1:T(8,128)S(1)}, f32[31,7,8,512]{3,0,2,1:T(8,128)}, u32[]{:S(2)}) copy-start(f32[31,7,8,512]{3,0,2,1:T(8,128)} %copy.38) | copy-start | bytes 10665988
  58.9 13.6 %copy-start.3 = (f32[16,56,128]{2,0,1:T(8,128)S(1)}, f32[16,56,128]{2,0,1:T(8,128)}, u32[]{:S(2)}) copy-start(f32[16,56,128]{2,0,1:T(8,128)} %copy.73) | copy-start | bytes 1376260

commit v2 on v1

--- a/solution.py
+++ b/solution.py
@@ -81,32 +81,38 @@
 
 def toeplitz_rhs(kernels):
     nt = kernels.shape[0]
-    kt = jnp.transpose(kernels, (1, 2, 3, 0)).reshape(TS * TS, TS * nt)
-    dims = (TS, nt, TS + ZB, nt, ZB)
-    c = lax.broadcasted_iota(jnp.int32, dims, 0)
-    t = lax.broadcasted_iota(jnp.int32, dims, 1)
-    w = lax.broadcasted_iota(jnp.int32, dims, 2)
-    t2 = lax.broadcasted_iota(jnp.int32, dims, 3)
-    zl = lax.broadcasted_iota(jnp.int32, dims, 4)
-    shift = ((w - zl == c) & (t == t2)).astype(jnp.float32).reshape(TS * nt, TS + ZB, nt * ZB)
-    rhs = jnp.einsum("rk,kwn->rwn", kt, shift, precision=lax.Precision.HIGHEST)
+    kt = jnp.transpose(kernels, (1, 2, 0, 3)).reshape(TS * TS, nt * TS)
+    spread = jnp.pad(kt, ((0, 0), (ZB - 1, TS + ZB - ZB)))
+    lanes = np.arange(nt * ZB) % ZB
+    pieces = []
+    for w in range(TS + ZB):
+        keep = (lanes + w - (ZB - 1) >= 0) & (lanes + w - (ZB - 1) < TS)
+        pieces.append(jnp.where(jnp.asarray(keep)[None], spread[:, w: w + nt * ZB], 0.0))
+    rhs = jnp.stack(pieces, axis=1)
     return rhs.reshape(TS, 1, TS * (TS + ZB), nt * ZB)
 
 
 def im2col_kernel(p_ref, o_ref):
-    for zb in range(o_ref.shape[1]):
-        for b in range(TS):
-            o_ref[:, zb, :, b * (TS + ZB):(b + 1) * (TS + ZB)] = p_ref[:, b:b + BY, zb * ZB: zb * ZB + TS + ZB]
+    def body(y, carry):
+        for zb in range(o_ref.shape[0]):
+            for b in range(TS):
+                o_ref[zb, y, :, b * (TS + ZB):(b + 1) * (TS + ZB)] = p_ref[y + b, :, zb * ZB: zb * ZB + TS + ZB]
+        return carry
+    lax.fori_loop(0, BY, body, 0)
 
 
-def im2col(padded, blocks):
-    rows = padded.shape[0]
+def im2col(padded_t, blocks):
+    rows = padded_t.shape[1]
     return pl.pallas_call(
         im2col_kernel,
-        out_shape=jax.ShapeDtypeStruct((rows, blocks, BY, TS * (TS + ZB)), jnp.float32),
+        out_shape=jax.ShapeDtypeStruct((blocks, BY, rows, TS * (TS + ZB)), jnp.float32),
         in_specs=[pl.BlockSpec(memory_space=pltpu.VMEM)],
         out_specs=pl.BlockSpec(memory_space=pltpu.VMEM),
-    )(padded)
+    )(padded_t)
+
+
+def reorder(values, order):
+    return jnp.concatenate([values[i: i + 1] for i in order])
 
 
 def local(volume, bank, orient, bank_id, counts):
@@ -121,14 +127,15 @@
     planes = gather_planes(bank, "gx")
     per = nt // FIELDS
     order = [k * per + p for p in range(per) for k in range(FIELDS)]
-    kernels = rotated_kernels(planes, orient[np.array(order)], bank_id[np.array(order)])
+    kernels = rotated_kernels(planes, reorder(orient, order), reorder(bank_id, order))
     rhs = toeplitz_rhs(kernels)
     field_in = extended(grid, (("gx", 0),), half)
     padded = jnp.pad(field_in, ((0, 0), (half, TS - half), (half, TS - half)))
-    cols = im2col(padded[: len_x - 1], blocks)
-    cols = cols.reshape(1, len_x - 1, blocks * BY, TS * (TS + ZB))
+    cols = im2col(jnp.transpose(padded[: len_x - 1], (1, 0, 2)), blocks)
+    cols = cols.reshape(1, blocks * BY, len_x - 1, TS * (TS + ZB))
     numer = lax.conv_general_dilated(
-        cols, rhs, (1, 1), "VALID", dimension_numbers=("NHWC", "HWIO", "NHWC"),
+        cols, rhs, (1, 1), "VALID",
+        dimension_numbers=lax.ConvDimensionNumbers((0, 3, 2, 1), (3, 2, 0, 1), (0, 3, 1, 2)),
         precision=lax.Precision.HIGH,
     )
     numer = numer.reshape(rows_x, blocks * BY, nt * ZB)
@@ -144,10 +151,10 @@
         "xyn,ym->xmn", energy, band_table(pos_y, jnp.arange(BY, dtype=jnp.int32), len_y)
     )
     energy = contract("xmn,xl->lmn", energy, band_table(pos_x, out_x, len_x))
-    energy = jnp.transpose(energy.reshape(rows_x, BY, blocks, ZB), (0, 2, 1, 3))
+    energy = jnp.transpose(jnp.flip(energy.reshape(rows_x, BY, blocks, ZB), axis=3), (0, 2, 1, 3))
     energy = jnp.tile(energy.reshape(rows_x, blocks * BY, ZB), (1, 1, nt))
     scores = numer / jnp.sqrt(energy + epsilon)
-    weights = counts[np.array(order)].astype(jnp.float32)
+    weights = reorder(counts, order).astype(jnp.float32)
     weighted = jnp.repeat(weights, ZB)[None, None] * jnp.exp(sharpness * scores)
     half_lanes = FIELDS * ZB
     grouped = weighted[:, :, :half_lanes]
@@ -158,7 +165,7 @@
         totals = totals + weights[p * FIELDS:(p + 1) * FIELDS]
     fields = jnp.log(grouped / jnp.repeat(totals, ZB)[None, None])
     fields = fields.reshape(rows_x, blocks, BY, FIELDS, ZB)
-    fields = jnp.transpose(fields, (3, 0, 2, 1, 4))
+    fields = jnp.transpose(jnp.flip(fields, axis=4), (3, 0, 2, 1, 4))
     return fields.reshape(FIELDS, rows_x, BY * BZ)
 
 

time: 79.5 us -> 105 us (1.32)
  local copies, waits for them, and re-layouts: 33.3 us -> 54.8 us
  starting transfers between devices: 12.8 us -> 14.9 us
    concatenate x0 -> x3, local copies, waits for them, and re-layouts: none -> 15.3 us  [reorder(): return jnp.concatenate([values[i:i + 1] for i in order])]
    another operation x0 -> x2, local copies, waits for them, and re-layouts: none -> 12.8 us  [toeplitz_rhs(): rhs = jnp.stack(pieces, axis=1)]
    pallas_call x1 -> x0, local copies, waits for them, and re-layouts: 5.81 us -> none  [im2col(): pl.pallas_call(im2col_kernel, out_shape=jax.ShapeDtypeStruct((rows, block...]
    rev x0 -> x2, local copies, waits for them, and re-layouts: none -> 4.62 us  [the longest x1 4.43 us: local(): fields = jnp.transpose(jnp.flip(fields, axis=4), (3, 0, 2, 1, 4))]
    slice x1 -> x3, local copies, waits for them, and re-layouts: 0.84 us -> 4.91 us  [reorder(): return jnp.concatenate([values[i:i + 1] for i in order])]
    and x1 -> x0, local copies, waits for them, and re-layouts: 3.7 us -> none  [toeplitz_rhs(): (w - zl == c) & (t == t2)]
    gather x3 -> x0, local copies, waits for them, and re-layouts: 3.24 us -> none  [the longest x1 1.3 us: local(): orient[np.array(order)]]
    select_n x0 -> x4, other arithmetic: none -> 2.84 us  [toeplitz_rhs(): jnp.where(jnp.asarray(keep)[None], spread[:, w:w + nt * ZB], 0.0)]
  transfers between devices with their start and end apart: 6 -> 6, of which waited for: 1 -> 2; matrix products, arithmetic and copies ran while one was open for 26% -> 26% of each run, Pallas kernels for 8% -> 6%
where the time goes in v2:
time: 105 us; the launch traced here: 104 us
  local copies, waits for them, and re-layouts  54.8 us (52%)
  matrix products  16.5 us (16%)
  starting transfers between devices  14.9 us (14%)
  other arithmetic  9.08 us (9%)
  Pallas kernels  6.61 us (6%)
    conv_general_dilated x1, matrix products, local(): lax.conv_general_dilated(cols, rhs, (1, 1), 'VALID', dimension_numbers=la...  15.6 us
    concatenate x3, local copies, waits for them, and re-layouts, reorder(): return jnp.concatenate([values[i:i + 1] for i in order])  15.3 us
    another operation x2, local copies, waits for them, and re-layouts, toeplitz_rhs(): rhs = jnp.stack(pieces, axis=1)  12.8 us
    ppermute x4, starting transfers between devices, gather_planes(): other = lax.ppermute(held, axis, pairs)  11.6 us
    pallas_call x1, Pallas kernels, im2col(): pl.pallas_call(im2col_kernel, out_shape=jax.ShapeDtypeStruct((blocks, BY,...  6.61 us
    slice x3, local copies, waits for them, and re-layouts, reorder(): return jnp.concatenate([values[i:i + 1] for i in order])  4.91 us
    rev x1, local copies, waits for them, and re-layouts, local(): fields = jnp.transpose(jnp.flip(fields, axis=4), (3, 0, 2, 1, 4))  4.43 us
    select_n x4, other arithmetic, toeplitz_rhs(): jnp.where(jnp.asarray(keep)[None], spread[:, w:w + nt * ZB], 0.0)  2.84 us
  transfers between devices with their start and end apart: 6, of which 2 were waited for; matrix products, arithmetic and copies ran while one was open for 26% of the time, Pallas kernels for 6%

profile of v2, /device:TPU:0, one launch (start us, length us, event | category | flops | bytes accessed | tf_op | source)
XLA Modules:
  0.0 103.7 jit_solution(3750924917103692491)
XLA Ops:
  1.3 2.0 %collective-permute-start = (f32[8,8,112]{2,0,1:T(8,128)S(1)}, f32[8,8,112]{2,0,1:T(8,128)S(1)}, u32[]{:S(2)}, u32[]{:S(2)}) collective-permute-start(f32[8,8,112]{2,0,1:T(8,128)S(1)} %copy.93), channel_id=1, source_target_pairs={{0,1},{1,2},{2,3},{3,4},{4,5},{5,6},{6,7},{7,8},{8,9},{9,10},{10,1... | collective-permute-start | bytes 86024 | tf_op jit(solution)/shard_map/ppermute | solution.py:28
  3.4 1.3 %collective-permute-start.1 = (f32[8,8,112]{2,0,1:T(8,128)S(1)}, f32[8,8,112]{2,0,1:T(8,128)S(1)}, u32[]{:S(2)}, u32[]{:S(2)}) collective-permute-start(f32[8,8,112]{2,0,1:T(8,128)S(1)} %copy.94), channel_id=1, source_target_pairs={{1,0},{2,1},{3,2},{4,3},{5,4},{6,5},{7,6},{8,7},{9,8},{10,9},{11,1... | collective-permute-start | bytes 86024 | tf_op jit(solution)/shard_map/ppermute | solution.py:29
  4.7 1.6 %fusion.97 = (s32[1]{0:T(128)}, s32[1]{0:T(128)}, s32[1]{0:T(128)}, s32[1]{0:T(128)}, s32[1]{0:T(128)}, /*index=5*/s32[1]{0:T(128)}, s32[1]{0:T(128)}, s32[1]{0:T(128)}) fusion(s32[8]{0:T(128)} %param.40), kind=kLoop, calls=%fused_computation.202 | loop fusion | bytes 64 | tf_op jit(solution)/shard_map/slice | solution.py:115
  6.3 5.1 %concatenate.153 = s32[8]{0:T(128)S(1)} concatenate(s32[1]{0:T(128)} %get-tuple-element.90, s32[1]{0:T(128)} %get-tuple-element.89, s32[1]{0:T(128)} %get-tuple-element.88, s32[1]{0:T(128)} %get-tuple-element.87, s32[1]{0:T(128)} %get-tuple-element.86, s32[1]{0:T(128)} %get-tuple-element.85, s32[1]{0:T(128)} %get-tuple-element.91, s32[1]{0:T(128)} %get-tuple-element.84), dimensions={0} | concatenate | bytes 64 | tf_op jit(solution)/shard_map/concatenate | solution.py:115
  11.4 1.6 %fusion.96 = (s32[1]{0:T(128)}, s32[1]{0:T(128)}, s32[1]{0:T(128)}, s32[1]{0:T(128)}, s32[1]{0:T(128)}, /*index=5*/s32[1]{0:T(128)}, s32[1]{0:T(128)}, s32[1]{0:T(128)}) fusion(s32[8]{0:T(128)} %param.39), kind=kLoop, calls=%fused_computation.201 | loop fusion | bytes 64 | tf_op jit(solution)/shard_map/slice | solution.py:115
  13.1 5.1 %concatenate.152 = s32[8]{0:T(128)S(1)} concatenate(s32[1]{0:T(128)} %get-tuple-element.74, s32[1]{0:T(128)} %get-tuple-element.73, s32[1]{0:T(128)} %get-tuple-element.72, s32[1]{0:T(128)} %get-tuple-element.71, s32[1]{0:T(128)} %get-tuple-element.70, s32[1]{0:T(128)} %get-tuple-element.69, s32[1]{0:T(128)} %get-tuple-element.75, s32[1]{0:T(128)} %get-tuple-element.68), dimensions={0} | concatenate | bytes 64 | tf_op jit(solution)/shard_map/concatenate | solution.py:115
  18.2 1.6 %fusion.95 = (s32[1]{0:T(128)}, s32[1]{0:T(128)}, s32[1]{0:T(128)}, s32[1]{0:T(128)}, s32[1]{0:T(128)}, /*index=5*/s32[1]{0:T(128)}, s32[1]{0:T(128)}, s32[1]{0:T(128)}) fusion(s32[8]{0:T(128)} %param.41), kind=kLoop, calls=%fused_computation.200 | loop fusion | bytes 64 | tf_op jit(solution)/shard_map/slice | solution.py:115
  19.8 5.1 %concatenate.150 = s32[8]{0:T(128)S(1)} concatenate(s32[1]{0:T(128)} %get-tuple-element.57, s32[1]{0:T(128)} %get-tuple-element.56, s32[1]{0:T(128)} %get-tuple-element.55, s32[1]{0:T(128)} %get-tuple-element.54, s32[1]{0:T(128)} %get-tuple-element.53, s32[1]{0:T(128)} %get-tuple-element.52, s32[1]{0:T(128)} %get-tuple-element.58, s32[1]{0:T(128)} %get-tuple-element.51), dimensions={0} | concatenate | bytes 64 | tf_op jit(solution)/shard_map/concatenate | solution.py:115
  25.8 4.8 %collective-permute-start.3 = (f32[2,8,256]{2,1,0:T(8,128)S(1)}, f32[2,8,256]{2,1,0:T(8,128)S(1)}, u32[]{:S(2)}, u32[]{:S(2)}) collective-permute-start(f32[2,8,256]{2,1,0:T(8,128)S(1)} %maximum_select_fusion.3), channel_id=1, source_target_pairs={{0,2},{1,3},{2,0},{3,1},{4,6},{5,7},{6,4},{7,5},{8,10},{9,11},{10,... | collective-permute-start | bytes 49160 | tf_op jit(solution)/shard_map/ppermute | solution.py:54
  30.6 0.9 reshape.1723
  32.3 3.0 %collective-permute-start.4 = (f32[4,8,256]{2,1,0:T(8,128)S(1)}, f32[4,8,256]{2,1,0:T(8,128)S(1)}, u32[]{:S(2)}, u32[]{:S(2)}) collective-permute-start(f32[4,8,256]{2,1,0:T(8,128)S(1)} %maximum_select_fusion.2), channel_id=1, source_target_pairs={{0,4},{1,5},{2,6},{3,7},{4,0},{5,1},{6,2},{7,3},{8,12},{9,13},{10,... | collective-permute-start | bytes 98312 | tf_op jit(solution)/shard_map/ppermute | solution.py:54
  37.3 3.4 %collective-permute-start.5 = (f32[8,8,256]{2,1,0:T(8,128)S(1)}, f32[8,8,256]{2,1,0:T(8,128)S(1)}, u32[]{:S(2)}, u32[]{:S(2)}) collective-permute-start(f32[8,8,256]{2,1,0:T(8,128)S(1)} %maximum_select_fusion.1), channel_id=1, source_target_pairs={{0,8},{1,9},{2,10},{3,11},{4,12},{5,13},{6,14},{7,15},{8,0},{9,1},... | collective-permute-start | bytes 196616 | tf_op jit(solution)/shard_map/ppermute | solution.py:54
  40.6 0.9 slice_bitcast_fusion.p_ref
  41.5 6.6 %shard_map.343 = f32[7,8,31,512]{3,2,1,0:T(8,128)} custom-call(f32[24,31,128]{2,1,0:T(8,128)} %slice_bitcast_fusion.p_ref), custom_call_target="tpu_custom_call" | custom-call | tf_op jit(solution)/shard_map/pallas_call | solution.py:106
  48.4 1.1 %copy.155 = f32[16,56,128]{2,0,1:T(8,128)} copy(f32[16,56,128]{1,2,0:T(8,128)S(1)} %bitcast.147) | data formatting | bytes 917504 | tf_op jit(solution)/shard_map/sqrt | solution.py:156
  53.3 2.0 %copy.112 = f32[8,16,16,16]{1,0,3,2:T(8,128)} copy(f32[8,16,16,16]{2,0,3,1:T(8,128)S(1)} %reverse_select_fusion) | data formatting | bytes 262144 | tf_op jit(solution)/shard_map/jit(_where)/select_n | solution.py:70
  56.0 2.5 %bitcast_add_fusion.3 = f32[8,16,16,16]{1,0,3,2:T(8,128)} fusion(f32[8,16,16,16]{1,0,2,3:T(8,128)S(1)} %copy.114, f32[8,16,16,16]{1,0,3,2:T(8,128)} %copy.112, pred[8]{0:T(512)(128)(4,1)S(1)} %get-tuple-element.94, pred[8]{0:T(512)(128)(4,1)S(1)} %get-tuple-element.93, pred[8]{0:T(512)(128)(4,1)S(1)} %get-tuple-element.92, ...), kind=kLoop, calls=%fused_computation.37 | loop fusion | flops 196608 | bytes 524320 | tf_op jit(solution)/shard_map/add | solution.py:75
  58.5 1.6 %copy.117 = f32[8,16,16,16]{3,0,1,2:T(8,128)S(1)} copy(f32[8,16,16,16]{1,0,3,2:T(8,128)} %bitcast_add_fusion.3) | data formatting | bytes 262144 | tf_op jit(solution)/shard_map/add | solution.py:75
  63.5 1.9 %fusion.34 = (f32[256,128]{1,0:T(8,128)S(1)}, f32[256,128]{1,0:T(8,128)S(1)}, f32[256,128]{1,0:T(8,128)S(1)}, f32[256,128]{1,0:T(8,128)S(1)}, f32[256,128]{1,0:T...) fusion(f32[256,128]{1,0:T(8,128)S(1)} %reshape.1725, ...), kind=kLoop, calls=%fused_computation.80 | loop fusion | flops 294912 | bytes 1311872 | tf_op jit(solution)/shard_map/jit(_where)/select_n | solution.py:90
  65.5 12.7 %stack.128 = f32[256,32,128]{2,1,0:T(8,128)} concatenate(f32[256,1,128]{2,1,0:T(1,128)S(1)} %bitcast.151, f32[256,1,128]{2,1,0:T(1,128)S(1)} %bitcast.153, f32[256,1,128]{2,1,0:T(1,128)S(1)} %bitcast.154, f32[256,1,128]{2,1,0:T(1,128)S(1)} %bitcast.155, f32[256,1,128]{2,1,0:T(1,128)S(1)} %bitcast.156, f32[256,1,128]{2,1,0:T(1,128)S(1)} %bitcast.157, ...), dimensions={1} | concatenate | bytes 8388608 | tf_op jit(solution)/shard_map/stack | solution.py:91
  78.2 15.6 %fusion = f32[16,8,7,128]{3,1,2,0:T(8,128)S(1)} fusion(f32[16,1,512,128]{3,2,1,0:T(8,128)} %bitcast.145, f32[8,7,31,512]{3,2,1,0:T(8,128)} %bitcast.144), kind=kOutput, calls=%fused_computation | convolution fusion | flops 5637144576 | bytes 8208384 | tf_op jit(solution)/shard_map/conv_general_dilated | solution.py:136
  95.2 4.4 %rev.24 = f32[16,7,8,4,16]{4,3,2,1,0:T(4,128)} reverse(f32[16,7,8,4,16]{4,3,2,1,0:T(4,128)S(1)} %reshape.1730), dimensions={4} | reverse | bytes 458752 | tf_op jit(solution)/shard_map/jit(_flip)/rev | solution.py:168
  99.7 2.6 %copy.157 = f32[4,16,8,7,16]{4,3,2,1,0:T(8,128)S(1)} copy(f32[4,16,8,7,16]{4,0,2,3,1:T(4,128)} %bitcast.146) | data formatting | bytes 458752 | tf_op jit(solution)/shard_map/transpose | solution.py:168
  102.3 1.4 %reshape.1731 = f32[4,16,896]{2,1,0:T(8,128)} reshape(f32[4,16,8,7,16]{4,3,2,1,0:T(8,128)S(1)} %copy.157) | data formatting | bytes 458752 | tf_op jit(solution)/shard_map/reshape | solution.py:169
  (127 shorter events, 13.9 us)
Async XLA Ops:
  0.0 25.0 %collective-permute-start.2 = (f32[1,8,256]{2,1,0:T(8,128)}, f32[1,8,256]{2,1,0:T(8,128)S(1)}, u32[]{:S(2)}, u32[]{:S(2)}) collective-permute-start(f32[1,8,256]{2,1,0:T(8,128)} %bitcast.179), channel_id=1, source_target_pairs={{0,1},{1,0},{2,3},{3,2},{4,5},{5,4},{6,7},{7,6},{8,9},{9,8},{10,11... | collective-permute-start | bytes 24584 | tf_op jit(solution)/shard_map/ppermute | solution.py:54
  1.3 34.0 %collective-permute-start = (f32[8,8,112]{2,0,1:T(8,128)S(1)}, f32[8,8,112]{2,0,1:T(8,128)S(1)}, u32[]{:S(2)}, u32[]{:S(2)}) collective-permute-start(f32[8,8,112]{2,0,1:T(8,128)S(1)} %copy.93), channel_id=1, source_target_pairs={{0,1},{1,2},{2,3},{3,4},{4,5},{5,6},{6,7},{7,8},{8,9},{9,10},{10,1... | collective-permute-start | bytes 86024 | tf_op jit(solution)/shard_map/ppermute | solution.py:28
  3.4 32.0 %collective-permute-start.1 = (f32[8,8,112]{2,0,1:T(8,128)S(1)}, f32[8,8,112]{2,0,1:T(8,128)S(1)}, u32[]{:S(2)}, u32[]{:S(2)}) collective-permute-start(f32[8,8,112]{2,0,1:T(8,128)S(1)} %copy.94), channel_id=1, source_target_pairs={{1,0},{2,1},{3,2},{4,3},{5,4},{6,5},{7,6},{8,7},{9,8},{10,9},{11,1... | collective-permute-start | bytes 86024 | tf_op jit(solution)/shard_map/ppermute | solution.py:29
  25.8 6.5 %collective-permute-start.3 = (f32[2,8,256]{2,1,0:T(8,128)S(1)}, f32[2,8,256]{2,1,0:T(8,128)S(1)}, u32[]{:S(2)}, u32[]{:S(2)}) collective-permute-start(f32[2,8,256]{2,1,0:T(8,128)S(1)} %maximum_select_fusion.3), channel_id=1, source_target_pairs={{0,2},{1,3},{2,0},{3,1},{4,6},{5,7},{6,4},{7,5},{8,10},{9,11},{10,... | collective-permute-start | bytes 49160 | tf_op jit(solution)/shard_map/ppermute | solution.py:54
  32.3 4.9 %collective-permute-start.4 = (f32[4,8,256]{2,1,0:T(8,128)S(1)}, f32[4,8,256]{2,1,0:T(8,128)S(1)}, u32[]{:S(2)}, u32[]{:S(2)}) collective-permute-start(f32[4,8,256]{2,1,0:T(8,128)S(1)} %maximum_select_fusion.2), channel_id=1, source_target_pairs={{0,4},{1,5},{2,6},{3,7},{4,0},{5,1},{6,2},{7,3},{8,12},{9,13},{10,... | collective-permute-start | bytes 98312 | tf_op jit(solution)/shard_map/ppermute | solution.py:54
  37.3 12.3 %collective-permute-start.5 = (f32[8,8,256]{2,1,0:T(8,128)S(1)}, f32[8,8,256]{2,1,0:T(8,128)S(1)}, u32[]{:S(2)}, u32[]{:S(2)}) collective-permute-start(f32[8,8,256]{2,1,0:T(8,128)S(1)} %maximum_select_fusion.1), channel_id=1, source_target_pairs={{0,8},{1,9},{2,10},{3,11},{4,12},{5,13},{6,14},{7,15},{8,0},{9,1},... | collective-permute-start | bytes 196616 | tf_op jit(solution)/shard_map/ppermute | solution.py:54
  60.7 1.8 %copy-start.12 = (pred[128]{0:T(512)(128)(4,1)S(1)}, pred[128]{0:T(512)(128)(4,1)}, u32[]{:S(2)}) copy-start(pred[128]{0:T(512)(128)(4,1)} %constant.259.clone) | copy-start | bytes 388
  60.8 1.8 %copy-start.13 = (pred[128]{0:T(512)(128)(4,1)S(1)}, pred[128]{0:T(512)(128)(4,1)}, u32[]{:S(2)}) copy-start(pred[128]{0:T(512)(128)(4,1)} %constant.260.clone) | copy-start | bytes 388
  60.8 1.8 %copy-start.14 = (pred[128]{0:T(512)(128)(4,1)S(1)}, pred[128]{0:T(512)(128)(4,1)}, u32[]{:S(2)}) copy-start(pred[128]{0:T(512)(128)(4,1)} %constant.261.clone) | copy-start | bytes 388
  60.8 1.8 %copy-start.15 = (pred[128]{0:T(512)(128)(4,1)S(1)}, pred[128]{0:T(512)(128)(4,1)}, u32[]{:S(2)}) copy-start(pred[128]{0:T(512)(128)(4,1)} %constant.262.clone) | copy-start | bytes 388
  60.8 1.8 %copy-start.16 = (pred[128]{0:T(512)(128)(4,1)S(1)}, pred[128]{0:T(512)(128)(4,1)}, u32[]{:S(2)}) copy-start(pred[128]{0:T(512)(128)(4,1)} %constant.263.clone) | copy-start | bytes 388
  60.8 1.8 %copy-start.17 = (pred[128]{0:T(512)(128)(4,1)S(1)}, pred[128]{0:T(512)(128)(4,1)}, u32[]{:S(2)}) copy-start(pred[128]{0:T(512)(128)(4,1)} %constant.264.clone) | copy-start | bytes 388
  60.9 2.2 %copy-start.3 = (pred[128]{0:T(512)(128)(4,1)S(1)}, pred[128]{0:T(512)(128)(4,1)}, u32[]{:S(2)}) copy-start(pred[128]{0:T(512)(128)(4,1)} %constant.267.clone) | copy-start | bytes 388
  60.9 2.2 %copy-start.4 = (pred[128]{0:T(512)(128)(4,1)S(1)}, pred[128]{0:T(512)(128)(4,1)}, u32[]{:S(2)}) copy-start(pred[128]{0:T(512)(128)(4,1)} %constant.268.clone) | copy-start | bytes 388
  60.9 2.2 %copy-start.5 = (pred[128]{0:T(512)(128)(4,1)S(1)}, pred[128]{0:T(512)(128)(4,1)}, u32[]{:S(2)}) copy-start(pred[128]{0:T(512)(128)(4,1)} %constant.269.clone) | copy-start | bytes 388
  60.9 2.2 %copy-start.6 = (pred[128]{0:T(512)(128)(4,1)S(1)}, pred[128]{0:T(512)(128)(4,1)}, u32[]{:S(2)}) copy-start(pred[128]{0:T(512)(128)(4,1)} %constant.270.clone) | copy-start | bytes 388
  60.9 2.2 %copy-start.7 = (pred[128]{0:T(512)(128)(4,1)S(1)}, pred[128]{0:T(512)(128)(4,1)}, u32[]{:S(2)}) copy-start(pred[128]{0:T(512)(128)(4,1)} %constant.271.clone) | copy-start | bytes 388
  60.9 2.2 %copy-start.8 = (pred[128]{0:T(512)(128)(4,1)S(1)}, pred[128]{0:T(512)(128)(4,1)}, u32[]{:S(2)}) copy-start(pred[128]{0:T(512)(128)(4,1)} %constant.272.clone) | copy-start | bytes 388
  60.9 2.2 %copy-start.9 = (pred[128]{0:T(512)(128)(4,1)S(1)}, pred[128]{0:T(512)(128)(4,1)}, u32[]{:S(2)}) copy-start(pred[128]{0:T(512)(128)(4,1)} %constant.274.clone) | copy-start | bytes 388
  61.0 2.2 %copy-start.10 = (pred[128]{0:T(512)(128)(4,1)S(1)}, pred[128]{0:T(512)(128)(4,1)}, u32[]{:S(2)}) copy-start(pred[128]{0:T(512)(128)(4,1)} %constant.275.clone) | copy-start | bytes 388
  61.0 2.1 %copy-start.11 = (pred[128]{0:T(512)(128)(4,1)S(1)}, pred[128]{0:T(512)(128)(4,1)}, u32[]{:S(2)}) copy-start(pred[128]{0:T(512)(128)(4,1)} %constant.287.clone) | copy-start | bytes 388
  61.4 2.1 %copy-start.1 = (pred[128]{0:T(512)(128)(4,1)S(1)}, pred[128]{0:T(512)(128)(4,1)}, u32[]{:S(2)}) copy-start(pred[128]{0:T(512)(128)(4,1)} %constant.276.clone) | copy-start | bytes 388
  61.5 2.1 %copy-start.2 = (pred[128]{0:T(512)(128)(4,1)S(1)}, pred[128]{0:T(512)(128)(4,1)}, u32[]{:S(2)}) copy-start(pred[128]{0:T(512)(128)(4,1)} %constant.277.clone) | copy-start | bytes 388
  78.2 15.8 %copy-start = (f32[16,56,128]{2,0,1:T(8,128)S(1)}, f32[16,56,128]{2,0,1:T(8,128)}, u32[]{:S(2)}) copy-start(f32[16,56,128]{2,0,1:T(8,128)} %copy.155) | copy-start | bytes 1376260
  (6 other events, 10.4 us)

commit v3 on v2

--- a/solution.py
+++ b/solution.py
@@ -81,14 +81,17 @@
 
 def toeplitz_rhs(kernels):
     nt = kernels.shape[0]
-    kt = jnp.transpose(kernels, (1, 2, 0, 3)).reshape(TS * TS, nt * TS)
-    spread = jnp.pad(kt, ((0, 0), (ZB - 1, TS + ZB - ZB)))
-    lanes = np.arange(nt * ZB) % ZB
-    pieces = []
-    for w in range(TS + ZB):
-        keep = (lanes + w - (ZB - 1) >= 0) & (lanes + w - (ZB - 1) < TS)
-        pieces.append(jnp.where(jnp.asarray(keep)[None], spread[:, w: w + nt * ZB], 0.0))
-    rhs = jnp.stack(pieces, axis=1)
+    per = nt // FIELDS
+    kt = kernels.reshape(FIELDS, per, TS, TS, TS)
+    kt = jnp.transpose(kt, (2, 3, 1, 0, 4)).reshape(TS * TS, TS * nt)
+    dims = (TS + ZB, nt, TS, nt, ZB)
+    w = lax.broadcasted_iota(jnp.int32, dims, 0)
+    t = lax.broadcasted_iota(jnp.int32, dims, 1)
+    c = lax.broadcasted_iota(jnp.int32, dims, 2)
+    t2 = lax.broadcasted_iota(jnp.int32, dims, 3)
+    zl = lax.broadcasted_iota(jnp.int32, dims, 4)
+    shift = ((w - zl == c) & (t == t2)).astype(jnp.float32).reshape(TS + ZB, TS * nt, nt * ZB)
+    rhs = jnp.einsum("rk,wkn->rwn", kt, shift, precision=lax.Precision.HIGHEST)
     return rhs.reshape(TS, 1, TS * (TS + ZB), nt * ZB)
 
 
@@ -111,10 +114,6 @@
     )(padded_t)
 
 
-def reorder(values, order):
-    return jnp.concatenate([values[i: i + 1] for i in order])
-
-
 def local(volume, bank, orient, bank_id, counts):
     rows_x = volume.shape[0]
     half = TS // 2
@@ -126,8 +125,7 @@
     blocks = BZ // ZB
     planes = gather_planes(bank, "gx")
     per = nt // FIELDS
-    order = [k * per + p for p in range(per) for k in range(FIELDS)]
-    kernels = rotated_kernels(planes, reorder(orient, order), reorder(bank_id, order))
+    kernels = rotated_kernels(planes, orient, bank_id)
     rhs = toeplitz_rhs(kernels)
     field_in = extended(grid, (("gx", 0),), half)
     padded = jnp.pad(field_in, ((0, 0), (half, TS - half), (half, TS - half)))
@@ -151,10 +149,10 @@
         "xyn,ym->xmn", energy, band_table(pos_y, jnp.arange(BY, dtype=jnp.int32), len_y)
     )
     energy = contract("xmn,xl->lmn", energy, band_table(pos_x, out_x, len_x))
-    energy = jnp.transpose(jnp.flip(energy.reshape(rows_x, BY, blocks, ZB), axis=3), (0, 2, 1, 3))
+    energy = jnp.transpose(energy.reshape(rows_x, BY, blocks, ZB), (0, 2, 1, 3))
     energy = jnp.tile(energy.reshape(rows_x, blocks * BY, ZB), (1, 1, nt))
     scores = numer / jnp.sqrt(energy + epsilon)
-    weights = reorder(counts, order).astype(jnp.float32)
+    weights = jnp.transpose(counts.astype(jnp.float32).reshape(FIELDS, per)).reshape(nt)
     weighted = jnp.repeat(weights, ZB)[None, None] * jnp.exp(sharpness * scores)
     half_lanes = FIELDS * ZB
     grouped = weighted[:, :, :half_lanes]
@@ -165,7 +163,7 @@
         totals = totals + weights[p * FIELDS:(p + 1) * FIELDS]
     fields = jnp.log(grouped / jnp.repeat(totals, ZB)[None, None])
     fields = fields.reshape(rows_x, blocks, BY, FIELDS, ZB)
-    fields = jnp.transpose(jnp.flip(fields, axis=4), (3, 0, 2, 1, 4))
+    fields = jnp.transpose(fields, (3, 0, 2, 1, 4))
     return fields.reshape(FIELDS, rows_x, BY * BZ)
 
 

time: 105 us -> 70 us (0.67)
  local copies, waits for them, and re-layouts: 54.8 us -> 23.8 us
  starting transfers between devices: 14.9 us -> 12.8 us
    concatenate x3 -> x0, local copies, waits for them, and re-layouts: 15.3 us -> none  [reorder(): return jnp.concatenate([values[i:i + 1] for i in order])]
    another operation x2 -> x0, local copies, waits for them, and re-layouts: 12.8 us -> none  [toeplitz_rhs(): rhs = jnp.stack(pieces, axis=1)]
    slice x3 -> x0, local copies, waits for them, and re-layouts: 4.91 us -> none  [reorder(): return jnp.concatenate([values[i:i + 1] for i in order])]
    rev x2 -> x0, local copies, waits for them, and re-layouts: 4.62 us -> none  [the longest x1 4.43 us: local(): fields = jnp.transpose(jnp.flip(fields, axis=4), (3, 0, 2, 1, 4))]
    and x0 -> x1, local copies, waits for them, and re-layouts: none -> 3.68 us  [toeplitz_rhs(): (w - zl == c) & (t == t2)]
    select_n x4 -> x0, other arithmetic: 2.84 us -> none  [toeplitz_rhs(): jnp.where(jnp.asarray(keep)[None], spread[:, w:w + nt * ZB], 0.0)]
    dot_general x1, local copies, waits for them, and re-layouts: 0.02 us -> 2.43 us  [toeplitz_rhs(): rhs = jnp.einsum('rk,wkn->rwn', kt, shift, precision=lax.Precision.HIGHEST)]
    conv_general_dilated x1, matrix products: 15.6 us -> 13.2 us  [local(): lax.conv_general_dilated(cols, rhs, (1, 1), 'VALID', dimension_numbers=la...]
  transfers between devices with their start and end apart: 6 -> 6, of which waited for: 2 -> 1; matrix products, arithmetic and copies ran while one was open for 26% -> 19% of each run, Pallas kernels for 6% -> 10%
where the time goes in v3:
time: 70 us; the launch traced here: 69.5 us
  local copies, waits for them, and re-layouts  23.8 us (34%)
  matrix products  15.8 us (23%)
  starting transfers between devices  12.8 us (18%)
  other arithmetic  8.52 us (12%)
  Pallas kernels  6.61 us (9%)
  waiting for transfers between devices  1.54 us (2%)
    conv_general_dilated x1, matrix products, local(): lax.conv_general_dilated(cols, rhs, (1, 1), 'VALID', dimension_numbers=la...  13.2 us
    ppermute x4, starting transfers between devices, gather_planes(): other = lax.ppermute(held, axis, pairs)  9.54 us
    pallas_call x1, Pallas kernels, im2col(): pl.pallas_call(im2col_kernel, out_shape=jax.ShapeDtypeStruct((blocks, BY,...  6.61 us
    and x1, local copies, waits for them, and re-layouts, toeplitz_rhs(): (w - zl == c) & (t == t2)  3.68 us
    transpose x1, local copies, waits for them, and re-layouts, local(): fields = jnp.transpose(fields, (3, 0, 2, 1, 4))  2.58 us
    dot_general x1, local copies, waits for them, and re-layouts, toeplitz_rhs(): rhs = jnp.einsum('rk,wkn->rwn', kt, shift, precision=lax.Precision.HIGHEST)  2.43 us
    reshape x1, local copies, waits for them, and re-layouts, local(): fields = fields.reshape(rows_x, blocks, BY, FIELDS, ZB)  2.05 us
    ppermute x1, starting transfers between devices, extended(): before = lax.ppermute(last, axis, up)  1.96 us
  transfers between devices with their start and end apart: 6, of which 1 were waited for; matrix products, arithmetic and copies ran while one was open for 19% of the time, Pallas kernels for 10%

profile of v3, /device:TPU:0, one launch (start us, length us, event | category | flops | bytes accessed | tf_op | source)
XLA Modules:
  0.0 69.5 jit_solution(200320595596910823)
XLA Ops:
  0.5 0.8 %fusion.63 = (f32[8,896]{1,0:T(8,128)S(1)}, f32[8,896]{1,0:T(8,128)S(1)}) fusion(f32[16,896]{1,0:T(8,128)} %param.5), kind=kLoop, calls=%fused_computation.141 | loop fusion | bytes 114688 | tf_op jit(solution)/shard_map/slice | solution.py:27
  1.3 2.0 %collective-permute-start = (f32[8,8,112]{2,0,1:T(8,128)S(1)}, f32[8,8,112]{2,0,1:T(8,128)S(1)}, u32[]{:S(2)}, u32[]{:S(2)}) collective-permute-start(f32[8,8,112]{2,0,1:T(8,128)S(1)} %copy.65), channel_id=1, source_target_pairs={{0,1},{1,2},{2,3},{3,4},{4,5},{5,6},{6,7},{7,8},{8,9},{9,10},{10,1... | collective-permute-start | bytes 86024 | tf_op jit(solution)/shard_map/ppermute | solution.py:28
  3.4 1.3 %collective-permute-start.1 = (f32[8,8,112]{2,0,1:T(8,128)S(1)}, f32[8,8,112]{2,0,1:T(8,128)S(1)}, u32[]{:S(2)}, u32[]{:S(2)}) collective-permute-start(f32[8,8,112]{2,0,1:T(8,128)S(1)} %copy.66), channel_id=1, source_target_pairs={{1,0},{2,1},{3,2},{4,3},{5,4},{6,5},{7,6},{8,7},{9,8},{10,9},{11,1... | collective-permute-start | bytes 86024 | tf_op jit(solution)/shard_map/ppermute | solution.py:29
  4.7 1.0 %fusion = pred[32,8,16,8,16]{0,4,3,2,1:T(8,128)(4,1)S(1)} fusion(), kind=kLoop, calls=%fused_computation.2 | loop fusion | flops 2097152 | bytes 524288 | tf_op jit(solution)/shard_map/and | solution.py:93
  8.0 0.8 %maximum_select_fusion.3 = f32[2,8,256]{2,1,0:T(8,128)S(1)} fusion(f32[1,8,256]{2,1,0:T(8,128)S(1)} %collective-permute-done.2, f32[1,8,256]{2,1,0:T(8,128)} %bitcast.70, pred[]{:T(512)S(6)} %eq.109), kind=kLoop, calls=%fused_computation.58 | loop fusion | flops 12288 | bytes 32769 | tf_op jit(solution)/shard_map/jit(_where)/select_n | solution.py:56
  8.8 4.8 %collective-permute-start.3 = (f32[2,8,256]{2,1,0:T(8,128)S(1)}, f32[2,8,256]{2,1,0:T(8,128)S(1)}, u32[]{:S(2)}, u32[]{:S(2)}) collective-permute-start(f32[2,8,256]{2,1,0:T(8,128)S(1)} %maximum_select_fusion.3), channel_id=1, source_target_pairs={{0,2},{1,3},{2,0},{3,1},{4,6},{5,7},{6,4},{7,5},{8,10},{9,11},{10,... | collective-permute-start | bytes 49160 | tf_op jit(solution)/shard_map/ppermute | solution.py:54
  13.6 0.9 %reshape.175 = f32[16,8,112]{2,1,0:T(8,128)S(1)} reshape(f32[16,896]{1,0:T(8,128)} %param.5) | data formatting | bytes 114688 | tf_op jit(solution)/shard_map/reshape | solution.py:121
  14.6 3.7 %copy.95 = pred[32,128,128]{2,1,0:T(32,128)(4,1)} copy(pred[32,128,128]{0,2,1:T(8,128)(4,1)S(1)} %bitcast.62) | data formatting | bytes 1048576 | tf_op jit(solution)/shard_map/and | solution.py:93
  18.7 1.6 %collective-permute-start.4 = (f32[4,8,256]{2,1,0:T(8,128)S(1)}, f32[4,8,256]{2,1,0:T(8,128)S(1)}, u32[]{:S(2)}, u32[]{:S(2)}) collective-permute-start(f32[4,8,256]{2,1,0:T(8,128)S(1)} %maximum_select_fusion.2), channel_id=1, source_target_pairs={{0,4},{1,5},{2,6},{3,7},{4,0},{5,1},{6,2},{7,3},{8,12},{9,13},{10,... | collective-permute-start | bytes 98312 | tf_op jit(solution)/shard_map/ppermute | solution.py:54
  21.1 1.5 %collective-permute-done.4 = f32[4,8,256]{2,1,0:T(8,128)S(1)} collective-permute-done((f32[4,8,256]{2,1,0:T(8,128)S(1)}, f32[4,8,256]{2,1,0:T(8,128)S(1)}, u32[]{:S(2)}, u32[]{:S(2)}) %collective-permute-start.4) | collective-permute-done | bytes 32800 | tf_op jit(solution)/shard_map/ppermute | solution.py:54
  22.7 2.7 %collective-permute-start.5 = (f32[8,8,256]{2,1,0:T(8,128)S(1)}, f32[8,8,256]{2,1,0:T(8,128)S(1)}, u32[]{:S(2)}, u32[]{:S(2)}) collective-permute-start(f32[8,8,256]{2,1,0:T(8,128)S(1)} %maximum_select_fusion.1), channel_id=1, source_target_pairs={{0,8},{1,9},{2,10},{3,11},{4,12},{5,13},{6,14},{7,15},{8,0},{9,1},... | collective-permute-start | bytes 196616 | tf_op jit(solution)/shard_map/ppermute | solution.py:54
  25.3 0.9 %slice_bitcast_fusion.p_ref = f32[24,31,128]{2,1,0:T(8,128)} fusion(f32[32,8,112]{2,0,1:T(8,128)S(1)} %constant_dynamic-update-slice_fusion), kind=kLoop, calls=%fused_computation.27 | loop fusion | bytes 495616 | tf_op jit(solution)/shard_map/transpose | solution.py:132
  26.2 6.6 %shard_map.55 = f32[7,8,31,512]{3,2,1,0:T(8,128)} custom-call(f32[24,31,128]{2,1,0:T(8,128)} %slice_bitcast_fusion.p_ref), custom_call_target="tpu_custom_call" | custom-call | tf_op jit(solution)/shard_map/pallas_call | solution.py:109
  33.3 1.1 %copy.105 = f32[16,56,128]{2,0,1:T(8,128)} copy(f32[16,56,128]{1,2,0:T(8,128)S(1)} %bitcast.64) | data formatting | bytes 917504 | tf_op jit(solution)/shard_map/sqrt | solution.py:154
  36.4 0.9 %select_add_fusion = f32[8,16,16,16]{2,3,1,0:T(8,128)S(1)} fusion(f32[16,16,16]{1,2,0:T(8,128)S(1)} %copy.82, f32[16,16,16]{1,2,0:T(8,128)S(1)} %copy.80, f32[16,16,16]{1,2,0:T(8,128)S(1)} %copy.78, f32[16,16,16]{1,2,0:T(8,128)S(1)} %copy.76, f32[16,16,16]{1,2,0:T(8,128)S(1)} %copy.74, f32[16,16,16]{1,2,0:T(8,128)S(1)} %copy.72, f32[16,16,16]{1,2,0:T(8,128)S(1)} %copy.70, ...), kind=kLoop, calls=%fused_computation.16 | loop fusion | flops 491520 | bytes 262208 | tf_op jit(solution)/shard_map/add | solution.py:66
  38.9 0.7 copy.84
  40.0 1.3 %bitcast_add_fusion.3 = f32[8,16,16,16]{1,3,2,0:T(8,128)} fusion(f32[8,16,16,16]{2,3,1,0:T(8,128)S(1)} %broadcast_select_fusion.1, f32[8,16,16,16]{1,2,3,0:T(8,128)S(1)} %copy.86, f32[8,16,16,16]{1,3,2,0:T(8,128)S(1)} %copy.84, pred[8]{0:T(512)(128)(4,1)S(1)} %get-tuple-element.40, pred[8]{0:T(512)(128)(4,1)S(1)} %get-tuple-element.39, ...), kind=kLoop, calls=%fused_computation.12 | loop fusion | flops 163840 | bytes 524312 | tf_op jit(solution)/shard_map/add | solution.py:75
  41.3 1.5 %copy.89 = f32[8,16,16,16]{3,1,2,0:T(8,128)S(1)} copy(f32[8,16,16,16]{1,3,2,0:T(8,128)} %bitcast_add_fusion.3) | data formatting | bytes 262144 | tf_op jit(solution)/shard_map/add | solution.py:75
  45.4 1.8 %fusion.64 = f32[256,32,128]{2,0,1:T(8,128)S(1)} fusion(f32[256,128,1]{0,1,2:T(8,128)S(1)} %reshape.205, pred[32,128,128]{2,1,0:T(32,128)(4,1)S(1)} %copy-done.1), kind=kOutput, calls=%fused_computation.142 | convolution fusion | flops 1610612736 | bytes 4849664 | tf_op jit(solution)/shard_map/rk,wkn->rwn/dot_general | solution.py:94
  47.2 2.4 %copy.96 = f32[256,32,128]{2,1,0:T(8,128)S(1)} copy(f32[256,32,128]{2,0,1:T(8,128)S(1)} %fusion.64) | data formatting | bytes 8388608 | tf_op jit(solution)/shard_map/rk,wkn->rwn/dot_general | solution.py:94
  49.7 13.2 %fusion.1 = f32[16,8,7,128]{3,1,2,0:T(8,128)S(1)} fusion(f32[16,1,512,128]{3,2,1,0:T(8,128)S(1)} %bitcast.60, f32[8,7,31,512]{3,2,1,0:T(8,128)S(1)} %bitcast.59), kind=kOutput, calls=%fused_computation.3 | convolution fusion | flops 5637144576 | bytes 8208384 | tf_op jit(solution)/shard_map/conv_general_dilated | solution.py:134
  63.5 2.1 %reshape.181 = f32[16,7,8,4,16]{4,3,2,1,0:T(4,128)} reshape(f32[16,56,64]{2,1,0:T(8,128)S(1)} %copy.106) | data formatting | bytes 458752 | tf_op jit(solution)/shard_map/reshape | solution.py:165
  65.6 2.6 %copy.107 = f32[4,16,8,7,16]{4,3,2,1,0:T(8,128)S(1)} copy(f32[4,16,8,7,16]{4,0,2,3,1:T(4,128)} %bitcast.63) | data formatting | bytes 458752 | tf_op jit(solution)/shard_map/transpose | solution.py:166
  68.1 1.4 %reshape.182 = f32[4,16,896]{2,1,0:T(8,128)} reshape(f32[4,16,8,7,16]{4,3,2,1,0:T(8,128)S(1)} %copy.107) | data formatting | bytes 458752 | tf_op jit(solution)/shard_map/reshape | solution.py:167
  (81 shorter events, 11.5 us)
Async XLA Ops:
  0.0 8.0 %collective-permute-start.2 = (f32[1,8,256]{2,1,0:T(8,128)}, f32[1,8,256]{2,1,0:T(8,128)S(1)}, u32[]{:S(2)}, u32[]{:S(2)}) collective-permute-start(f32[1,8,256]{2,1,0:T(8,128)} %bitcast.69), channel_id=1, source_target_pairs={{0,1},{1,0},{2,3},{3,2},{4,5},{5,4},{6,7},{7,6},{8,9},{9,8},{10,11... | collective-permute-start | bytes 24584 | tf_op jit(solution)/shard_map/ppermute | solution.py:54
  1.3 19.0 %collective-permute-start = (f32[8,8,112]{2,0,1:T(8,128)S(1)}, f32[8,8,112]{2,0,1:T(8,128)S(1)}, u32[]{:S(2)}, u32[]{:S(2)}) collective-permute-start(f32[8,8,112]{2,0,1:T(8,128)S(1)} %copy.65), channel_id=1, source_target_pairs={{0,1},{1,2},{2,3},{3,4},{4,5},{5,6},{6,7},{7,8},{8,9},{9,10},{10,1... | collective-permute-start | bytes 86024 | tf_op jit(solution)/shard_map/ppermute | solution.py:28
  3.4 17.0 %collective-permute-start.1 = (f32[8,8,112]{2,0,1:T(8,128)S(1)}, f32[8,8,112]{2,0,1:T(8,128)S(1)}, u32[]{:S(2)}, u32[]{:S(2)}) collective-permute-start(f32[8,8,112]{2,0,1:T(8,128)S(1)} %copy.66), channel_id=1, source_target_pairs={{1,0},{2,1},{3,2},{4,3},{5,4},{6,5},{7,6},{8,7},{9,8},{10,9},{11,1... | collective-permute-start | bytes 86024 | tf_op jit(solution)/shard_map/ppermute | solution.py:29
  8.8 9.9 %collective-permute-start.3 = (f32[2,8,256]{2,1,0:T(8,128)S(1)}, f32[2,8,256]{2,1,0:T(8,128)S(1)}, u32[]{:S(2)}, u32[]{:S(2)}) collective-permute-start(f32[2,8,256]{2,1,0:T(8,128)S(1)} %maximum_select_fusion.3), channel_id=1, source_target_pairs={{0,2},{1,3},{2,0},{3,1},{4,6},{5,7},{6,4},{7,5},{8,10},{9,11},{10,... | collective-permute-start | bytes 49160 | tf_op jit(solution)/shard_map/ppermute | solution.py:54
  18.7 4.0 %collective-permute-start.4 = (f32[4,8,256]{2,1,0:T(8,128)S(1)}, f32[4,8,256]{2,1,0:T(8,128)S(1)}, u32[]{:S(2)}, u32[]{:S(2)}) collective-permute-start(f32[4,8,256]{2,1,0:T(8,128)S(1)} %maximum_select_fusion.2), channel_id=1, source_target_pairs={{0,4},{1,5},{2,6},{3,7},{4,0},{5,1},{6,2},{7,3},{8,12},{9,13},{10,... | collective-permute-start | bytes 98312 | tf_op jit(solution)/shard_map/ppermute | solution.py:54
  22.7 11.8 %collective-permute-start.5 = (f32[8,8,256]{2,1,0:T(8,128)S(1)}, f32[8,8,256]{2,1,0:T(8,128)S(1)}, u32[]{:S(2)}, u32[]{:S(2)}) collective-permute-start(f32[8,8,256]{2,1,0:T(8,128)S(1)} %maximum_select_fusion.1), channel_id=1, source_target_pairs={{0,8},{1,9},{2,10},{3,11},{4,12},{5,13},{6,14},{7,15},{8,0},{9,1},... | collective-permute-start | bytes 196616 | tf_op jit(solution)/shard_map/ppermute | solution.py:54
  43.1 2.3 %copy-start.1 = (pred[32,128,128]{2,1,0:T(32,128)(4,1)S(1)}, pred[32,128,128]{2,1,0:T(32,128)(4,1)}, u32[]{:S(2)}) copy-start(pred[32,128,128]{2,1,0:T(32,128)(4,1)} %copy.95) | copy-start | bytes 1572868
  47.2 2.4 %copy-start = (f32[7,8,31,512]{3,2,1,0:T(8,128)S(1)}, f32[7,8,31,512]{3,2,1,0:T(8,128)}, u32[]{:S(2)}) copy-start(f32[7,8,31,512]{3,2,1,0:T(8,128)} %shard_map.55) | copy-start | bytes 10665988
  49.7 13.4 %copy-start.2 = (f32[16,56,128]{2,0,1:T(8,128)S(1)}, f32[16,56,128]{2,0,1:T(8,128)}, u32[]{:S(2)}) copy-start(f32[16,56,128]{2,0,1:T(8,128)} %copy.105) | copy-start | bytes 1376260

commit v4 on v3

--- a/solution.py
+++ b/solution.py
@@ -50,11 +50,19 @@
     held = bank[None]
     step = 1
     while step < size:
-        pairs = [(i, i ^ step) for i in range(size)]
-        other = lax.ppermute(held, axis, pairs)
-        low = (me // step) % 2 == 0
-        held = jnp.where(low, jnp.concatenate([held, other], 0), jnp.concatenate([other, held], 0))
-        step *= 2
+        radix = min(4, size // step)
+        digit = (me // step) % radix
+        blocks = [held] + [
+            lax.ppermute(held, axis, [(i, i ^ (s * step)) for i in range(size)]) for s in range(1, radix)
+        ]
+        placed = []
+        for d in range(radix):
+            value = jnp.zeros_like(held)
+            for s in range(radix):
+                value = value + jnp.where((digit ^ s) == d, blocks[s], 0.0)
+            placed.append(value)
+        held = jnp.concatenate(placed, 0)
+        step *= radix
     return held
 
 
@@ -84,13 +92,11 @@
     per = nt // FIELDS
     kt = kernels.reshape(FIELDS, per, TS, TS, TS)
     kt = jnp.transpose(kt, (2, 3, 1, 0, 4)).reshape(TS * TS, TS * nt)
-    dims = (TS + ZB, nt, TS, nt, ZB)
+    dims = (TS + ZB, TS * nt, nt * ZB)
     w = lax.broadcasted_iota(jnp.int32, dims, 0)
-    t = lax.broadcasted_iota(jnp.int32, dims, 1)
-    c = lax.broadcasted_iota(jnp.int32, dims, 2)
-    t2 = lax.broadcasted_iota(jnp.int32, dims, 3)
-    zl = lax.broadcasted_iota(jnp.int32, dims, 4)
-    shift = ((w - zl == c) & (t == t2)).astype(jnp.float32).reshape(TS + ZB, TS * nt, nt * ZB)
+    k = lax.broadcasted_iota(jnp.int32, dims, 1)
+    n = lax.broadcasted_iota(jnp.int32, dims, 2)
+    shift = ((w - n % ZB == k % TS) & (k // TS == n // ZB)).astype(jnp.float32)
     rhs = jnp.einsum("rk,wkn->rwn", kt, shift, precision=lax.Precision.HIGHEST)
     return rhs.reshape(TS, 1, TS * (TS + ZB), nt * ZB)
 
@@ -111,6 +117,7 @@
         out_shape=jax.ShapeDtypeStruct((blocks, BY, rows, TS * (TS + ZB)), jnp.float32),
         in_specs=[pl.BlockSpec(memory_space=pltpu.VMEM)],
         out_specs=pl.BlockSpec(memory_space=pltpu.VMEM),
+        cost_estimate=pl.CostEstimate(flops=0, transcendentals=0, bytes_accessed=4 * blocks * BY * rows * TS * (TS + ZB)),
     )(padded_t)
 
 

time: 70 us -> 65.3 us (0.933)
  local copies, waits for them, and re-layouts: 23.8 us -> 20.1 us
  waiting for transfers between devices: 1.54 us -> 0.02 us
  starting transfers between devices: 12.8 us -> 14 us
  other arithmetic: 8.52 us -> 7.57 us
    and x1 -> x0, local copies, waits for them, and re-layouts: 3.68 us -> none  [toeplitz_rhs(): (w - zl == c) & (t == t2)]
    ppermute x4 -> x6, waiting for transfers between devices: 1.54 us -> 0.02 us  [gather_planes(): lax.ppermute(held, axis, [(i, i ^ s * step) for i in range(size)])]
    ppermute x4 -> x6, starting transfers between devices: 9.54 us -> 10.7 us  [gather_planes(): lax.ppermute(held, axis, [(i, i ^ s * step) for i in range(size)])]
    and x1, other arithmetic: 0.98 us -> 0.01 us  [toeplitz_rhs(): shift = ((w - n % ZB == k % TS) & (k // TS == n // ZB)).astype(jnp.float32)]
    select_n x4 -> x0, other arithmetic: 0.8 us -> none  [gather_planes(): jnp.where(low, jnp.concatenate([held, other], 0), jnp.concatenate([other,...]
    add x0 -> x4, other arithmetic: none -> 0.79 us  [gather_planes(): value = value + jnp.where(digit ^ s == d, blocks[s], 0.0)]
  transfers between devices with their start and end apart: 6 -> 8, of which waited for: 1 -> 0; matrix products, arithmetic and copies ran while one was open for 19% -> 13% of each run, Pallas kernels for 10% -> 10%
where the time goes in v4:
time: 65.3 us; the launch traced here: 64.8 us
  local copies, waits for them, and re-layouts  20.1 us (31%)
  matrix products  15.9 us (24%)
  starting transfers between devices  14 us (21%)
  other arithmetic  7.57 us (12%)
  Pallas kernels  6.61 us (10%)
    conv_general_dilated x1, matrix products, local(): lax.conv_general_dilated(cols, rhs, (1, 1), 'VALID', dimension_numbers=la...  13.2 us
    ppermute x6, starting transfers between devices, gather_planes(): lax.ppermute(held, axis, [(i, i ^ s * step) for i in range(size)])  10.7 us
    pallas_call x1, Pallas kernels, im2col(): pl.pallas_call(im2col_kernel, out_shape=jax.ShapeDtypeStruct((blocks, BY,...  6.61 us
    transpose x1, local copies, waits for them, and re-layouts, local(): fields = jnp.transpose(fields, (3, 0, 2, 1, 4))  2.58 us
    dot_general x1, local copies, waits for them, and re-layouts, toeplitz_rhs(): rhs = jnp.einsum('rk,wkn->rwn', kt, shift, precision=lax.Precision.HIGHEST)  2.43 us
    reshape x1, local copies, waits for them, and re-layouts, local(): fields = fields.reshape(rows_x, blocks, BY, FIELDS, ZB)  2.05 us
    ppermute x1, starting transfers between devices, extended(): before = lax.ppermute(last, axis, up)  1.99 us
    dot_general x1, matrix products, toeplitz_rhs(): rhs = jnp.einsum('rk,wkn->rwn', kt, shift, precision=lax.Precision.HIGHEST)  1.96 us
  transfers between devices with their start and end apart: 8, of which 0 were waited for; matrix products, arithmetic and copies ran while one was open for 13% of the time, Pallas kernels for 10%

profile of v4, /device:TPU:0, one launch (start us, length us, event | category | flops | bytes accessed | tf_op | source)
XLA Modules:
  0.0 64.8 jit_solution(4668158370562036650)
XLA Ops:
  0.5 2.5 %collective-permute-start.3 = (f32[1,8,256]{2,1,0:T(8,128)}, f32[1,8,256]{2,1,0:T(8,128)S(1)}, u32[]{:S(2)}, u32[]{:S(2)}) collective-permute-start(f32[1,8,256]{2,1,0:T(8,128)} %bitcast.91), channel_id=1, source_target_pairs={{0,2},{1,3},{2,0},{3,1},{4,6},{5,7},{6,4},{7,5},{8,10},{9,11},{10,... | collective-permute-start | bytes 24584 | tf_op jit(solution)/shard_map/ppermute | solution.py:56
  3.1 0.8 %fusion.85 = (f32[8,896]{1,0:T(8,128)S(1)}, f32[8,896]{1,0:T(8,128)S(1)}) fusion(f32[16,896]{1,0:T(8,128)} %param.5), kind=kLoop, calls=%fused_computation.175 | loop fusion | bytes 114688 | tf_op jit(solution)/shard_map/slice | solution.py:27
  3.9 2.0 %collective-permute-start = (f32[8,8,112]{2,0,1:T(8,128)S(1)}, f32[8,8,112]{2,0,1:T(8,128)S(1)}, u32[]{:S(2)}, u32[]{:S(2)}) collective-permute-start(f32[8,8,112]{2,0,1:T(8,128)S(1)} %copy.64), channel_id=1, source_target_pairs={{0,1},{1,2},{2,3},{3,4},{4,5},{5,6},{6,7},{7,8},{8,9},{9,10},{10,1... | collective-permute-start | bytes 86024 | tf_op jit(solution)/shard_map/ppermute | solution.py:28
  6.0 1.3 %collective-permute-start.1 = (f32[8,8,112]{2,0,1:T(8,128)S(1)}, f32[8,8,112]{2,0,1:T(8,128)S(1)}, u32[]{:S(2)}, u32[]{:S(2)}) collective-permute-start(f32[8,8,112]{2,0,1:T(8,128)S(1)} %copy.65), channel_id=1, source_target_pairs={{1,0},{2,1},{3,2},{4,3},{5,4},{6,5},{7,6},{8,7},{9,8},{10,9},{11,1... | collective-permute-start | bytes 86024 | tf_op jit(solution)/shard_map/ppermute | solution.py:29
  7.4 0.7 %broadcast_compare_fusion.10 = (pred[8]{0:T(512)(128)(4,1)S(1)}, pred[8]{0:T(512)(128)(4,1)S(1)}, pred[8]{0:T(512)(128)(4,1)S(1)}, pred[8]{0:T(512)(128)(4,1)S(1...) fusion(s32[8]{0:T(128)} %param.8), kind=kLoop, calls=%fused_computation.158 | loop fusion | flops 64 | bytes 96 | tf_op jit(solution)/shard_map/eq | solution.py:74
  8.0 0.7 %broadcast_compare_fusion.1 = (pred[8]{0:T(512)(128)(4,1)S(1)}, s32[8]{0:T(128)S(1)}, pred[8]{0:T(512)(128)(4,1)S(1)}, s32[8]{0:T(128)S(1)}) fusion(s32[8]{0:T(128)} %param.7), kind=kLoop, calls=%fused_computation.149 | loop fusion | flops 376 | bytes 112 | tf_op jit(solution)/shard_map/eq | solution.py:83
  8.7 0.7 %convert_element_type.4 = f32[8]{0:T(128)S(1)} convert(s32[8]{0:T(128)} %param.9) | non-fusion elementwise | flops 8 | bytes 64 | tf_op jit(solution)/shard_map/convert_element_type | solution.py:162
  9.8 0.9 %reshape.122 = f32[16,8,112]{2,1,0:T(8,128)S(1)} reshape(f32[16,896]{1,0:T(8,128)} %param.5) | data formatting | bytes 114688 | tf_op jit(solution)/shard_map/reshape | solution.py:128
  11.2 0.7 %fusion.48 = (f32[1,8,256]{2,1,0:T(8,128)S(1)}, f32[1,8,256]{2,1,0:T(8,128)S(1)}, f32[1,8,256]{2,1,0:T(8,128)S(1)}) fusion(f32[1,8,256]{2,1,0:T(8,128)S(1)} %collective-permute-done.4, f32[1,8,256]{2,1,0:T(8,128)S(1)} %collective-permute-done.3, f32[1,8,256]{2,1,0:T(8,128)S(1)} %collective-permute-done.2, f32[8,256]{1,0:T(8,128)} %param.6, pred[]{:T(512)S(6)} %eq.179, ...), kind=kLoop, calls=%fused_computation.92 | loop fusion | flops 43008 | bytes 57356 | tf_op jit(solution)/shard_map/add | solution.py:62
  12.0 5.0 %collective-permute-start.5 = (f32[4,8,256]{2,1,0:T(8,128)S(1)}, f32[4,8,256]{2,1,0:T(8,128)S(1)}, u32[]{:S(2)}, u32[]{:S(2)}) collective-permute-start(f32[4,8,256]{2,1,0:T(8,128)S(1)} %pad_maximum_fusion.1), channel_id=1, source_target_pairs={{0,4},{1,5},{2,6},{3,7},{4,0},{5,1},{6,2},{7,3},{8,12},{9,13},{10,... | collective-permute-start | bytes 98312 | tf_op jit(solution)/shard_map/ppermute | solution.py:56
  17.0 2.6 %collective-permute-start.6 = (f32[4,8,256]{2,1,0:T(8,128)S(1)}, f32[4,8,256]{2,1,0:T(8,128)S(1)}, u32[]{:S(2)}, u32[]{:S(2)}) collective-permute-start(f32[4,8,256]{2,1,0:T(8,128)S(1)} %pad_maximum_fusion.1), channel_id=1, source_target_pairs={{0,8},{1,9},{2,10},{3,11},{4,12},{5,13},{6,14},{7,15},{8,0},{9,1},... | collective-permute-start | bytes 98312 | tf_op jit(solution)/shard_map/ppermute | solution.py:56
  20.4 0.9 %slice_bitcast_fusion.p_ref = f32[24,31,128]{2,1,0:T(8,128)} fusion(f32[32,8,112]{2,0,1:T(8,128)S(1)} %constant_dynamic-update-slice_fusion), kind=kLoop, calls=%fused_computation.40 | loop fusion | bytes 495616 | tf_op jit(solution)/shard_map/transpose | solution.py:139
  21.3 6.6 %shard_map.55 = f32[7,8,31,512]{3,2,1,0:T(8,128)} custom-call(f32[24,31,128]{2,1,0:T(8,128)} %slice_bitcast_fusion.p_ref), custom_call_target="tpu_custom_call" | custom-call | bytes 3555328 | tf_op jit(solution)/shard_map/pallas_call | solution.py:115
  28.4 1.1 %copy.103 = f32[16,56,128]{2,0,1:T(8,128)} copy(f32[16,56,128]{1,2,0:T(8,128)S(1)} %bitcast.85) | data formatting | bytes 917504 | tf_op jit(solution)/shard_map/sqrt | solution.py:161
  31.6 0.9 %select_add_fusion = f32[8,16,16,16]{2,3,1,0:T(8,128)S(1)} fusion(f32[16,16,16]{1,2,0:T(8,128)S(1)} %copy.81, f32[16,16,16]{1,2,0:T(8,128)S(1)} %copy.79, f32[16,16,16]{1,2,0:T(8,128)S(1)} %copy.77, f32[16,16,16]{1,2,0:T(8,128)S(1)} %copy.75, f32[16,16,16]{1,2,0:T(8,128)S(1)} %copy.73, f32[16,16,16]{1,2,0:T(8,128)S(1)} %copy.71, f32[16,16,16]{1,2,0:T(8,128)S(1)} %copy.69, ...), kind=kLoop, calls=%fused_computation.25 | loop fusion | flops 491520 | bytes 262208 | tf_op jit(solution)/shard_map/add | solution.py:74
  34.1 0.7 %copy.83 = f32[8,16,16,16]{1,3,2,0:T(8,128)S(1)} copy(f32[8,16,16,16]{2,3,1,0:T(8,128)S(1)} %broadcast_select_fusion.1) | data formatting | bytes 262144 | tf_op jit(solution)/shard_map/jit(_where)/select_n | solution.py:78
  35.2 1.3 %bitcast_add_fusion.3 = f32[8,16,16,16]{1,3,2,0:T(8,128)} fusion(f32[8,16,16,16]{2,3,1,0:T(8,128)S(1)} %broadcast_select_fusion.1, f32[8,16,16,16]{1,2,3,0:T(8,128)S(1)} %copy.85, f32[8,16,16,16]{1,3,2,0:T(8,128)S(1)} %copy.83, pred[8]{0:T(512)(128)(4,1)S(1)} %get-tuple-element.47, pred[8]{0:T(512)(128)(4,1)S(1)} %get-tuple-element.46, ...), kind=kLoop, calls=%fused_computation.13 | loop fusion | flops 163840 | bytes 524312 | tf_op jit(solution)/shard_map/add | solution.py:83
  36.5 1.5 %copy.88 = f32[8,16,16,16]{3,1,2,0:T(8,128)S(1)} copy(f32[8,16,16,16]{1,3,2,0:T(8,128)} %bitcast_add_fusion.3) | data formatting | bytes 262144 | tf_op jit(solution)/shard_map/add | solution.py:83
  40.6 2.0 %fusion.3 = f32[256,32,128]{2,0,1:T(8,128)S(1)} fusion(f32[256,128,1]{0,1,2:T(8,128)S(1)} %reshape.152, s32[128]{0:T(128)S(1)} %get-tuple-element.52, s32[128]{0:T(128)S(1)} %get-tuple-element.54, s32[128]{0:T(128)S(1)} %get-tuple-element.53, s32[128]{0:T(128)S(1)} %get-tuple-element.55, pred[128]{0:T(512)(128)(4,1)S(1)} %get-tuple-element.50, ...), kind=kOutput, calls=%fused_computation.5 | convolution fusion | flops 1614807040 | bytes 4327680 | tf_op jit(solution)/shard_map/rk,wkn->rwn/dot_general | solution.py:100
  42.5 2.4 %copy.94 = f32[256,32,128]{2,1,0:T(8,128)S(1)} copy(f32[256,32,128]{2,0,1:T(8,128)S(1)} %fusion.3) | data formatting | bytes 8388608 | tf_op jit(solution)/shard_map/rk,wkn->rwn/dot_general | solution.py:100
  45.0 13.2 %fusion = f32[16,8,7,128]{3,1,2,0:T(8,128)S(1)} fusion(f32[16,1,512,128]{3,2,1,0:T(8,128)S(1)} %bitcast.82, f32[8,7,31,512]{3,2,1,0:T(8,128)S(1)} %bitcast.81), kind=kOutput, calls=%fused_computation | convolution fusion | flops 5637144576 | bytes 8208384 | tf_op jit(solution)/shard_map/conv_general_dilated | solution.py:141
  58.8 2.1 %reshape.128 = f32[16,7,8,4,16]{4,3,2,1,0:T(4,128)} reshape(f32[16,56,64]{2,1,0:T(8,128)S(1)} %copy.104) | data formatting | bytes 458752 | tf_op jit(solution)/shard_map/reshape | solution.py:172
  60.9 2.6 %copy.105 = f32[4,16,8,7,16]{4,3,2,1,0:T(8,128)S(1)} copy(f32[4,16,8,7,16]{4,0,2,3,1:T(4,128)} %bitcast.84) | data formatting | bytes 458752 | tf_op jit(solution)/shard_map/transpose | solution.py:173
  63.4 1.4 %reshape.129 = f32[4,16,896]{2,1,0:T(8,128)} reshape(f32[4,16,8,7,16]{4,3,2,1,0:T(8,128)S(1)} %copy.105) | data formatting | bytes 458752 | tf_op jit(solution)/shard_map/reshape | solution.py:174
  (86 shorter events, 9.8 us)
Async XLA Ops:
  0.0 11.2 %collective-permute-start.2 = (f32[1,8,256]{2,1,0:T(8,128)}, f32[1,8,256]{2,1,0:T(8,128)S(1)}, u32[]{:S(2)}, u32[]{:S(2)}) collective-permute-start(f32[1,8,256]{2,1,0:T(8,128)} %bitcast.90), channel_id=1, source_target_pairs={{0,1},{1,0},{2,3},{3,2},{4,5},{5,4},{6,7},{7,6},{8,9},{9,8},{10,11... | collective-permute-start | bytes 24584 | tf_op jit(solution)/shard_map/ppermute | solution.py:56
  0.5 10.7 %collective-permute-start.3 = (f32[1,8,256]{2,1,0:T(8,128)}, f32[1,8,256]{2,1,0:T(8,128)S(1)}, u32[]{:S(2)}, u32[]{:S(2)}) collective-permute-start(f32[1,8,256]{2,1,0:T(8,128)} %bitcast.91), channel_id=1, source_target_pairs={{0,2},{1,3},{2,0},{3,1},{4,6},{5,7},{6,4},{7,5},{8,10},{9,11},{10,... | collective-permute-start | bytes 24584 | tf_op jit(solution)/shard_map/ppermute | solution.py:56
  2.9 8.3 %collective-permute-start.4 = (f32[1,8,256]{2,1,0:T(8,128)}, f32[1,8,256]{2,1,0:T(8,128)S(1)}, u32[]{:S(2)}, u32[]{:S(2)}) collective-permute-start(f32[1,8,256]{2,1,0:T(8,128)} %bitcast.92), channel_id=1, source_target_pairs={{0,3},{1,2},{2,1},{3,0},{4,7},{5,6},{6,5},{7,4},{8,11},{9,10},{10,... | collective-permute-start | bytes 24584 | tf_op jit(solution)/shard_map/ppermute | solution.py:56
  3.9 15.7 %collective-permute-start = (f32[8,8,112]{2,0,1:T(8,128)S(1)}, f32[8,8,112]{2,0,1:T(8,128)S(1)}, u32[]{:S(2)}, u32[]{:S(2)}) collective-permute-start(f32[8,8,112]{2,0,1:T(8,128)S(1)} %copy.64), channel_id=1, source_target_pairs={{0,1},{1,2},{2,3},{3,4},{4,5},{5,6},{6,7},{7,8},{8,9},{9,10},{10,1... | collective-permute-start | bytes 86024 | tf_op jit(solution)/shard_map/ppermute | solution.py:28
  6.0 13.6 %collective-permute-start.1 = (f32[8,8,112]{2,0,1:T(8,128)S(1)}, f32[8,8,112]{2,0,1:T(8,128)S(1)}, u32[]{:S(2)}, u32[]{:S(2)}) collective-permute-start(f32[8,8,112]{2,0,1:T(8,128)S(1)} %copy.65), channel_id=1, source_target_pairs={{1,0},{2,1},{3,2},{4,3},{5,4},{6,5},{7,6},{8,7},{9,8},{10,9},{11,1... | collective-permute-start | bytes 86024 | tf_op jit(solution)/shard_map/ppermute | solution.py:29
  12.0 17.6 %collective-permute-start.5 = (f32[4,8,256]{2,1,0:T(8,128)S(1)}, f32[4,8,256]{2,1,0:T(8,128)S(1)}, u32[]{:S(2)}, u32[]{:S(2)}) collective-permute-start(f32[4,8,256]{2,1,0:T(8,128)S(1)} %pad_maximum_fusion.1), channel_id=1, source_target_pairs={{0,4},{1,5},{2,6},{3,7},{4,0},{5,1},{6,2},{7,3},{8,12},{9,13},{10,... | collective-permute-start | bytes 98312 | tf_op jit(solution)/shard_map/ppermute | solution.py:56
  17.0 12.5 %collective-permute-start.6 = (f32[4,8,256]{2,1,0:T(8,128)S(1)}, f32[4,8,256]{2,1,0:T(8,128)S(1)}, u32[]{:S(2)}, u32[]{:S(2)}) collective-permute-start(f32[4,8,256]{2,1,0:T(8,128)S(1)} %pad_maximum_fusion.1), channel_id=1, source_target_pairs={{0,8},{1,9},{2,10},{3,11},{4,12},{5,13},{6,14},{7,15},{8,0},{9,1},... | collective-permute-start | bytes 98312 | tf_op jit(solution)/shard_map/ppermute | solution.py:56
  19.6 10.0 %collective-permute-start.7 = (f32[4,8,256]{2,1,0:T(8,128)S(1)}, f32[4,8,256]{2,1,0:T(8,128)S(1)}, u32[]{:S(2)}, u32[]{:S(2)}) collective-permute-start(f32[4,8,256]{2,1,0:T(8,128)S(1)} %pad_maximum_fusion.1), channel_id=1, source_target_pairs={{0,12},{1,13},{2,14},{3,15},{4,8},{5,9},{6,10},{7,11},{8,4},{9,5},... | collective-permute-start | bytes 98312 | tf_op jit(solution)/shard_map/ppermute | solution.py:56
  42.5 2.4 %copy-start = (f32[7,8,31,512]{3,2,1,0:T(8,128)S(1)}, f32[7,8,31,512]{3,2,1,0:T(8,128)}, u32[]{:S(2)}) copy-start(f32[7,8,31,512]{3,2,1,0:T(8,128)} %shard_map.55) | copy-start | bytes 10665988
  45.0 13.4 %copy-start.1 = (f32[16,56,128]{2,0,1:T(8,128)S(1)}, f32[16,56,128]{2,0,1:T(8,128)}, u32[]{:S(2)}) copy-start(f32[16,56,128]{2,0,1:T(8,128)} %copy.103) | copy-start | bytes 1376260

commit v5 on v4

--- a/solution.py
+++ b/solution.py
@@ -68,10 +68,9 @@
 
 def rotated_kernels(planes, orient, bank_id):
     count = planes.shape[1]
-    picked = jnp.zeros((orient.shape[0], TS, TS, TS), jnp.float32)
-    for m in range(count):
-        base = planes[:, m, :].reshape(TS, TS, TS)
-        picked = picked + jnp.where(expand(bank_id == m), base[None], 0.0)
+    choice = (bank_id[:, None] == jnp.arange(count, dtype=jnp.int32)[None, :]).astype(jnp.float32)
+    picked = jnp.einsum("tm,amv->tav", choice, planes, precision=lax.Precision.HIGHEST)
+    picked = picked.reshape(orient.shape[0], TS, TS, TS)
     flips = orient % 8
     for axis_num in range(3):
         bit = (flips // 2**axis_num) % 2 == 1
@@ -90,15 +89,18 @@
 def toeplitz_rhs(kernels):
     nt = kernels.shape[0]
     per = nt // FIELDS
-    kt = kernels.reshape(FIELDS, per, TS, TS, TS)
-    kt = jnp.transpose(kt, (2, 3, 1, 0, 4)).reshape(TS * TS, TS * nt)
     dims = (TS + ZB, TS * nt, nt * ZB)
     w = lax.broadcasted_iota(jnp.int32, dims, 0)
     k = lax.broadcasted_iota(jnp.int32, dims, 1)
     n = lax.broadcasted_iota(jnp.int32, dims, 2)
     shift = ((w - n % ZB == k % TS) & (k // TS == n // ZB)).astype(jnp.float32)
-    rhs = jnp.einsum("rk,wkn->rwn", kt, shift, precision=lax.Precision.HIGHEST)
-    return rhs.reshape(TS, 1, TS * (TS + ZB), nt * ZB)
+    pairs = kernels.reshape(FIELDS, per, TS // 2, 2, TS, TS)
+    halves = []
+    for e in range(2):
+        kt = jnp.transpose(pairs[:, :, :, e], (2, 3, 1, 0, 4)).reshape(TS * TS // 2, TS * nt)
+        halves.append(jnp.einsum("rk,wkn->rwn", kt, shift, precision=lax.Precision.HIGHEST))
+    rhs = jnp.concatenate(halves, axis=-1)
+    return rhs.reshape(TS // 2, 1, TS * (TS + ZB), 2 * nt * ZB)
 
 
 def im2col_kernel(p_ref, o_ref):
@@ -138,11 +140,12 @@
     padded = jnp.pad(field_in, ((0, 0), (half, TS - half), (half, TS - half)))
     cols = im2col(jnp.transpose(padded[: len_x - 1], (1, 0, 2)), blocks)
     cols = cols.reshape(1, blocks * BY, len_x - 1, TS * (TS + ZB))
-    numer = lax.conv_general_dilated(
-        cols, rhs, (1, 1), "VALID",
+    both = lax.conv_general_dilated(
+        cols, rhs, (1, 1), "VALID", rhs_dilation=(2, 1),
         dimension_numbers=lax.ConvDimensionNumbers((0, 3, 2, 1), (3, 2, 0, 1), (0, 3, 1, 2)),
         precision=lax.Precision.HIGH,
     )
+    numer = both[:, :rows_x, :, : nt * ZB] + both[:, 1:, :, nt * ZB:]
     numer = numer.reshape(rows_x, blocks * BY, nt * ZB)
     pos_x = jnp.arange(len_x, dtype=jnp.int32)
     out_x = jnp.arange(rows_x, dtype=jnp.int32)

time: 65.3 us -> 74.5 us (1.14)
  other arithmetic: 7.57 us -> 13.8 us
  local copies, waits for them, and re-layouts: 20.1 us -> 25.3 us
  matrix products: 15.9 us -> 13.6 us
    concatenate x0 -> x1, local copies, waits for them, and re-layouts: none -> 5.49 us  [toeplitz_rhs(): rhs = jnp.concatenate(halves, axis=-1)]
    conv_general_dilated x1, matrix products: 13.2 us -> 10.5 us  [local(): lax.conv_general_dilated(cols, rhs, (1, 1), 'VALID', rhs_dilation=(2, 1),...]
    add x2, other arithmetic: 1.55 us -> 4.02 us  [rotated_kernels(): rotated + jnp.where(expand(order_row == row), jnp.transpose(picked, perm)...]
    select_n x3, other arithmetic: 0.64 us -> 3.08 us  [rotated_kernels(): picked = jnp.where(expand(bit), jnp.flip(picked, axis=axis_num + 1), picked)]
    concatenate x0 -> x1, other arithmetic: none -> 2.44 us  [toeplitz_rhs(): rhs = jnp.concatenate(halves, axis=-1)]
    dot_general x1 -> x0, local copies, waits for them, and re-layouts: 2.43 us -> none  [toeplitz_rhs(): rhs = jnp.einsum('rk,wkn->rwn', kt, shift, precision=lax.Precision.HIGHEST)]
    unnamed x0 -> x2, matrix products: none -> 2 us
    dot_general x1, matrix products: 1.96 us -> 0.25 us  [rotated_kernels(): jnp.einsum('tm,amv->tav', choice, planes, precision=lax.Precision.HIGHEST)]
  transfers between devices with their start and end apart: 8 -> 8, of which waited for: 0 -> 0; matrix products, arithmetic and copies ran while one was open for 13% -> 10% of each run, Pallas kernels for 10% -> 9%
where the time goes in v5:
time: 74.5 us; the launch traced here: 73.8 us
  local copies, waits for them, and re-layouts  25.3 us (34%)
  starting transfers between devices  14 us (19%)
  other arithmetic  13.8 us (19%)
  matrix products  13.6 us (18%)
  Pallas kernels  6.62 us (9%)
    ppermute x6, starting transfers between devices, gather_planes(): lax.ppermute(held, axis, [(i, i ^ s * step) for i in range(size)])  10.7 us
    conv_general_dilated x1, matrix products, local(): lax.conv_general_dilated(cols, rhs, (1, 1), 'VALID', rhs_dilation=(2, 1),...  10.5 us
    pallas_call x1, Pallas kernels, im2col(): pl.pallas_call(im2col_kernel, out_shape=jax.ShapeDtypeStruct((blocks, BY,...  6.62 us
    concatenate x1, local copies, waits for them, and re-layouts, toeplitz_rhs(): rhs = jnp.concatenate(halves, axis=-1)  5.49 us
    add x2, other arithmetic, rotated_kernels(): rotated + jnp.where(expand(order_row == row), jnp.transpose(picked, perm)...  4.02 us
    select_n x3, other arithmetic, rotated_kernels(): picked = jnp.where(expand(bit), jnp.flip(picked, axis=axis_num + 1), picked)  3.08 us
    transpose x1, local copies, waits for them, and re-layouts, local(): fields = jnp.transpose(fields, (3, 0, 2, 1, 4))  2.58 us
    add x1, local copies, waits for them, and re-layouts, rotated_kernels(): rotated + jnp.where(expand(order_row == row), jnp.transpose(picked, perm)...  2.53 us
  transfers between devices with their start and end apart: 8, of which 0 were waited for; matrix products, arithmetic and copies ran while one was open for 10% of the time, Pallas kernels for 9%

profile of v5, /device:TPU:0, one launch (start us, length us, event | category | flops | bytes accessed | tf_op | source)
XLA Modules:
  0.0 73.8 jit_solution(5828780706190057311)
XLA Ops:
  0.5 2.5 %collective-permute-start.3 = (f32[1,8,256]{2,1,0:T(8,128)}, f32[1,8,256]{2,1,0:T(8,128)S(1)}, u32[]{:S(2)}, u32[]{:S(2)}) collective-permute-start(f32[1,8,256]{2,1,0:T(8,128)} %bitcast.113), channel_id=1, source_target_pairs={{0,2},{1,3},{2,0},{3,1},{4,6},{5,7},{6,4},{7,5},{8,10},{9,11},{10,... | collective-permute-start | bytes 24584 | tf_op jit(solution)/shard_map/ppermute | solution.py:56
  3.9 2.0 %collective-permute-start = (f32[8,8,112]{2,0,1:T(8,128)S(1)}, f32[8,8,112]{2,0,1:T(8,128)S(1)}, u32[]{:S(2)}, u32[]{:S(2)}) collective-permute-start(f32[8,8,112]{2,0,1:T(8,128)S(1)} %copy.21), channel_id=1, source_target_pairs={{0,1},{1,2},{2,3},{3,4},{4,5},{5,6},{6,7},{7,8},{8,9},{9,10},{10,1... | collective-permute-start | bytes 86024 | tf_op jit(solution)/shard_map/ppermute | solution.py:28
  6.0 1.3 %collective-permute-start.1 = (f32[8,8,112]{2,0,1:T(8,128)S(1)}, f32[8,8,112]{2,0,1:T(8,128)S(1)}, u32[]{:S(2)}, u32[]{:S(2)}) collective-permute-start(f32[8,8,112]{2,0,1:T(8,128)S(1)} %copy.22), channel_id=1, source_target_pairs={{1,0},{2,1},{3,2},{4,3},{5,4},{6,5},{7,6},{8,7},{9,8},{10,9},{11,1... | collective-permute-start | bytes 86024 | tf_op jit(solution)/shard_map/ppermute | solution.py:29
  9.6 0.9 %reshape.113 = f32[16,8,112]{2,1,0:T(8,128)S(1)} reshape(f32[16,896]{1,0:T(8,128)} %param.5) | data formatting | bytes 114688 | tf_op jit(solution)/shard_map/reshape | solution.py:130
  11.7 5.0 %collective-permute-start.5 = (f32[4,8,256]{2,1,0:T(8,128)S(1)}, f32[4,8,256]{2,1,0:T(8,128)S(1)}, u32[]{:S(2)}, u32[]{:S(2)}) collective-permute-start(f32[4,8,256]{2,1,0:T(8,128)S(1)} %pad_maximum_fusion.1), channel_id=1, source_target_pairs={{0,4},{1,5},{2,6},{3,7},{4,0},{5,1},{6,2},{7,3},{8,12},{9,13},{10,... | collective-permute-start | bytes 98312 | tf_op jit(solution)/shard_map/ppermute | solution.py:56
  16.8 2.6 %collective-permute-start.6 = (f32[4,8,256]{2,1,0:T(8,128)S(1)}, f32[4,8,256]{2,1,0:T(8,128)S(1)}, u32[]{:S(2)}, u32[]{:S(2)}) collective-permute-start(f32[4,8,256]{2,1,0:T(8,128)S(1)} %pad_maximum_fusion.1), channel_id=1, source_target_pairs={{0,8},{1,9},{2,10},{3,11},{4,12},{5,13},{6,14},{7,15},{8,0},{9,1},... | collective-permute-start | bytes 98312 | tf_op jit(solution)/shard_map/ppermute | solution.py:56
  20.3 0.9 %slice_bitcast_fusion.2.p_ref = f32[24,31,128]{2,1,0:T(8,128)} fusion(f32[32,8,112]{2,0,1:T(8,128)S(1)} %constant_dynamic-update-slice_fusion), kind=kLoop, calls=%fused_computation.29 | loop fusion | bytes 495616 | tf_op jit(solution)/shard_map/transpose | solution.py:141
  21.1 6.6 %shard_map.55 = f32[7,8,31,512]{3,2,1,0:T(8,128)} custom-call(f32[24,31,128]{2,1,0:T(8,128)} %slice_bitcast_fusion.2.p_ref), custom_call_target="tpu_custom_call" | custom-call | bytes 3555328 | tf_op jit(solution)/shard_map/pallas_call | solution.py:117
  29.9 1.3 %rev.13 = f32[8,16,16,16]{2,3,1,0:T(8,128)} reverse(f32[8,16,16,16]{2,3,1,0:T(8,128)S(1)} %reverse_select_fusion), dimensions={2} | reverse | bytes 262144 | tf_op jit(solution)/shard_map/jit(_flip)/rev | solution.py:77
  31.2 1.5 %broadcast_select_fusion = f32[8,16,16,16]{2,3,1,0:T(8,128)S(1)} fusion(f32[8,16,16,16]{2,3,1,0:T(8,128)} %rev.13, pred[8]{0:T(512)(128)(4,1)S(1)} %get-tuple-element.29, f32[8,16,16,16]{2,3,1,0:T(8,128)S(1)} %copy.24, pred[8]{0:T(512)(128)(4,1)S(1)} %get-tuple-element.30), kind=kLoop, calls=%fused_computation.18 | loop fusion | flops 65536 | bytes 393232 | tf_op jit(solution)/shard_map/jit(_where)/select_n | solution.py:77
  32.7 1.1 %rev.14 = f32[8,16,16,16]{2,3,1,0:T(8,128)} reverse(f32[8,16,16,16]{2,3,1,0:T(8,128)S(1)} %broadcast_select_fusion), dimensions={3} | reverse | bytes 262144 | tf_op jit(solution)/shard_map/jit(_flip)/rev | solution.py:77
  33.8 1.4 %broadcast_select_fusion.1 = f32[8,16,16,16]{2,3,1,0:T(8,128)S(1)} fusion(f32[8,16,16,16]{2,3,1,0:T(8,128)} %rev.14, f32[8,16,16,16]{2,3,1,0:T(8,128)S(1)} %broadcast_select_fusion, pred[8]{0:T(512)(128)(4,1)S(1)} %get-tuple-element.27), kind=kLoop, calls=%fused_computation.19 | loop fusion | flops 32768 | bytes 393224 | tf_op jit(solution)/shard_map/jit(_where)/select_n | solution.py:77
  35.2 1.6 %copy.26 = f32[8,16,16,16]{1,3,2,0:T(8,128)} copy(f32[8,16,16,16]{2,3,1,0:T(8,128)S(1)} %broadcast_select_fusion.1) | data formatting | bytes 262144 | tf_op jit(solution)/shard_map/jit(_where)/select_n | solution.py:77
  37.3 2.5 %bitcast_add_fusion.3 = f32[8,16,16,16]{1,3,2,0:T(8,128)} fusion(f32[8,16,16,16]{2,3,1,0:T(8,128)S(1)} %broadcast_select_fusion.1, f32[8,16,16,16]{1,2,3,0:T(8,128)S(1)} %copy.28, f32[8,16,16,16]{1,3,2,0:T(8,128)} %copy.26, pred[8]{0:T(512)(128)(4,1)S(1)} %get-tuple-element.33, pred[8]{0:T(512)(128)(4,1)S(1)} %get-tuple-element.32, ...), kind=kLoop, calls=%fused_computation.12 | loop fusion | flops 163840 | bytes 524312 | tf_op jit(solution)/shard_map/add | solution.py:82
  39.8 2.5 %copy.31 = f32[8,16,16,16]{3,1,2,0:T(8,128)} copy(f32[8,16,16,16]{1,3,2,0:T(8,128)} %bitcast_add_fusion.3) | data formatting | bytes 262144 | tf_op jit(solution)/shard_map/add | solution.py:82
  42.4 1.5 %bitcast_add_fusion.1 = f32[8,16,16,16]{3,1,2,0:T(8,128)S(1)} fusion(f32[8,16,16,16]{3,1,2,0:T(8,128)} %copy.31, f32[8,16,16,16]{1,2,3,0:T(8,128)S(1)} %copy.28, f32[8,16,16,16]{2,3,1,0:T(8,128)S(1)} %broadcast_select_fusion.1, pred[8]{0:T(512)(128)(4,1)S(1)} %get-tuple-element.34, pred[8]{0:T(512)(128)(4,1)S(1)} %get-tuple-element.35), kind=kLoop, calls=%fused_computation.10 | loop fusion | flops 131072 | bytes 524304 | tf_op jit(solution)/shard_map/add | solution.py:82
  46.7 1.0 %fusion.86 = f32[128,4096]{0,1:S(1)} fusion(f32[128,128]{1,0:T(8,128)S(1)} %reshape.117, pred[128,4096]{0,1:T(32,128)(4,1)S(1)} %bitcast.105), kind=kOutput, calls=%fused_computation.162 | convolution fusion | flops 805306368 | bytes 2686976
  47.7 1.0 %fusion.87 = f32[128,4096]{0,1:S(1)} fusion(f32[128,128]{1,0:T(8,128)S(1)} %reshape.118, pred[128,4096]{0,1:T(32,128)(4,1)S(1)} %bitcast.106), kind=kOutput, calls=%fused_computation.163 | convolution fusion | flops 805306368 | bytes 2686976
  48.7 2.4 %pad_maximum_fusion = f32[128,32,256]{0,2,1:T(8,128)} fusion(f32[128,32,128]{0,2,1:T(8,128)S(1)} %bitcast.103, f32[128,32,128]{0,2,1:T(8,128)S(1)} %bitcast.102), kind=kLoop, calls=%fused_computation | loop fusion | flops 1048576 | bytes 8388608 | tf_op jit(solution)/shard_map/concatenate | solution.py:102
  51.2 5.5 %copy.37 = f32[128,32,256]{2,1,0:T(8,128)} copy(f32[128,32,256]{0,2,1:T(8,128)} %pad_maximum_fusion) | data formatting | bytes 8388608 | tf_op jit(solution)/shard_map/concatenate | solution.py:102
  56.7 10.5 %fusion = f32[17,8,7,256]{3,1,2,0:T(8,128)S(1)} fusion(f32[8,1,512,256]{3,2,1,0:T(8,128)} %bitcast.100, f32[8,7,31,512]{3,2,1,0:T(8,128)} %bitcast.99), kind=kOutput, calls=%fused_computation.1 | convolution fusion | flops 5989466112 | bytes 8724480 | tf_op jit(solution)/shard_map/conv_general_dilated | solution.py:143
  67.8 2.1 %reshape.121 = f32[16,7,8,4,16]{4,3,2,1,0:T(4,128)} reshape(f32[16,56,64]{2,1,0:T(8,128)S(1)} %copy.45) | data formatting | bytes 458752 | tf_op jit(solution)/shard_map/reshape | solution.py:175
  69.9 2.6 %copy.46 = f32[4,16,8,7,16]{4,3,2,1,0:T(8,128)S(1)} copy(f32[4,16,8,7,16]{4,0,2,3,1:T(4,128)} %bitcast.104) | data formatting | bytes 458752 | tf_op jit(solution)/shard_map/transpose | solution.py:176
  72.4 1.4 %reshape.122 = f32[4,16,896]{2,1,0:T(8,128)} reshape(f32[4,16,8,7,16]{4,3,2,1,0:T(8,128)S(1)} %copy.46) | data formatting | bytes 458752 | tf_op jit(solution)/shard_map/reshape | solution.py:177
  (74 shorter events, 11.6 us)
Async XLA Ops:
  0.0 11.0 %collective-permute-start.2 = (f32[1,8,256]{2,1,0:T(8,128)}, f32[1,8,256]{2,1,0:T(8,128)S(1)}, u32[]{:S(2)}, u32[]{:S(2)}) collective-permute-start(f32[1,8,256]{2,1,0:T(8,128)} %bitcast.112), channel_id=1, source_target_pairs={{0,1},{1,0},{2,3},{3,2},{4,5},{5,4},{6,7},{7,6},{8,9},{9,8},{10,11... | collective-permute-start | bytes 24584 | tf_op jit(solution)/shard_map/ppermute | solution.py:56
  0.5 10.5 %collective-permute-start.3 = (f32[1,8,256]{2,1,0:T(8,128)}, f32[1,8,256]{2,1,0:T(8,128)S(1)}, u32[]{:S(2)}, u32[]{:S(2)}) collective-permute-start(f32[1,8,256]{2,1,0:T(8,128)} %bitcast.113), channel_id=1, source_target_pairs={{0,2},{1,3},{2,0},{3,1},{4,6},{5,7},{6,4},{7,5},{8,10},{9,11},{10,... | collective-permute-start | bytes 24584 | tf_op jit(solution)/shard_map/ppermute | solution.py:56
  2.9 8.0 %collective-permute-start.4 = (f32[1,8,256]{2,1,0:T(8,128)}, f32[1,8,256]{2,1,0:T(8,128)S(1)}, u32[]{:S(2)}, u32[]{:S(2)}) collective-permute-start(f32[1,8,256]{2,1,0:T(8,128)} %bitcast.114), channel_id=1, source_target_pairs={{0,3},{1,2},{2,1},{3,0},{4,7},{5,6},{6,5},{7,4},{8,11},{9,10},{10,... | collective-permute-start | bytes 24584 | tf_op jit(solution)/shard_map/ppermute | solution.py:56
  3.9 15.4 %collective-permute-start = (f32[8,8,112]{2,0,1:T(8,128)S(1)}, f32[8,8,112]{2,0,1:T(8,128)S(1)}, u32[]{:S(2)}, u32[]{:S(2)}) collective-permute-start(f32[8,8,112]{2,0,1:T(8,128)S(1)} %copy.21), channel_id=1, source_target_pairs={{0,1},{1,2},{2,3},{3,4},{4,5},{5,6},{6,7},{7,8},{8,9},{9,10},{10,1... | collective-permute-start | bytes 86024 | tf_op jit(solution)/shard_map/ppermute | solution.py:28
  6.0 13.4 %collective-permute-start.1 = (f32[8,8,112]{2,0,1:T(8,128)S(1)}, f32[8,8,112]{2,0,1:T(8,128)S(1)}, u32[]{:S(2)}, u32[]{:S(2)}) collective-permute-start(f32[8,8,112]{2,0,1:T(8,128)S(1)} %copy.22), channel_id=1, source_target_pairs={{1,0},{2,1},{3,2},{4,3},{5,4},{6,5},{7,6},{8,7},{9,8},{10,9},{11,1... | collective-permute-start | bytes 86024 | tf_op jit(solution)/shard_map/ppermute | solution.py:29
  11.7 17.0 %collective-permute-start.5 = (f32[4,8,256]{2,1,0:T(8,128)S(1)}, f32[4,8,256]{2,1,0:T(8,128)S(1)}, u32[]{:S(2)}, u32[]{:S(2)}) collective-permute-start(f32[4,8,256]{2,1,0:T(8,128)S(1)} %pad_maximum_fusion.1), channel_id=1, source_target_pairs={{0,4},{1,5},{2,6},{3,7},{4,0},{5,1},{6,2},{7,3},{8,12},{9,13},{10,... | collective-permute-start | bytes 98312 | tf_op jit(solution)/shard_map/ppermute | solution.py:56
  16.8 11.9 %collective-permute-start.6 = (f32[4,8,256]{2,1,0:T(8,128)S(1)}, f32[4,8,256]{2,1,0:T(8,128)S(1)}, u32[]{:S(2)}, u32[]{:S(2)}) collective-permute-start(f32[4,8,256]{2,1,0:T(8,128)S(1)} %pad_maximum_fusion.1), channel_id=1, source_target_pairs={{0,8},{1,9},{2,10},{3,11},{4,12},{5,13},{6,14},{7,15},{8,0},{9,1},... | collective-permute-start | bytes 98312 | tf_op jit(solution)/shard_map/ppermute | solution.py:56
  19.4 9.3 %collective-permute-start.7 = (f32[4,8,256]{2,1,0:T(8,128)S(1)}, f32[4,8,256]{2,1,0:T(8,128)S(1)}, u32[]{:S(2)}, u32[]{:S(2)}) collective-permute-start(f32[4,8,256]{2,1,0:T(8,128)S(1)} %pad_maximum_fusion.1), channel_id=1, source_target_pairs={{0,12},{1,13},{2,14},{3,15},{4,8},{5,9},{6,10},{7,11},{8,4},{9,5},... | collective-permute-start | bytes 98312 | tf_op jit(solution)/shard_map/ppermute | solution.py:56
  27.9 0.8 %copy-start = (s32[8]{0:T(128)S(1)}, s32[8]{0:T(128)}, u32[]{:S(2)}) copy-start(s32[8]{0:T(128)} %param.8) | copy-start | bytes 100

commit v6 on v4

--- a/solution.py
+++ b/solution.py
@@ -90,15 +90,15 @@
 def toeplitz_rhs(kernels):
     nt = kernels.shape[0]
     per = nt // FIELDS
-    kt = kernels.reshape(FIELDS, per, TS, TS, TS)
-    kt = jnp.transpose(kt, (2, 3, 1, 0, 4)).reshape(TS * TS, TS * nt)
-    dims = (TS + ZB, TS * nt, nt * ZB)
+    dims = (TS + ZB, 2 * TS * nt, 2 * nt * ZB)
     w = lax.broadcasted_iota(jnp.int32, dims, 0)
     k = lax.broadcasted_iota(jnp.int32, dims, 1)
     n = lax.broadcasted_iota(jnp.int32, dims, 2)
     shift = ((w - n % ZB == k % TS) & (k // TS == n // ZB)).astype(jnp.float32)
+    pairs = kernels.reshape(FIELDS, per, TS // 2, 2, TS, TS)
+    kt = jnp.transpose(pairs, (2, 4, 3, 1, 0, 5)).reshape(TS * TS // 2, 2 * TS * nt)
     rhs = jnp.einsum("rk,wkn->rwn", kt, shift, precision=lax.Precision.HIGHEST)
-    return rhs.reshape(TS, 1, TS * (TS + ZB), nt * ZB)
+    return rhs.reshape(TS // 2, 1, TS * (TS + ZB), 2 * nt * ZB)
 
 
 def im2col_kernel(p_ref, o_ref):
@@ -138,11 +138,12 @@
     padded = jnp.pad(field_in, ((0, 0), (half, TS - half), (half, TS - half)))
     cols = im2col(jnp.transpose(padded[: len_x - 1], (1, 0, 2)), blocks)
     cols = cols.reshape(1, blocks * BY, len_x - 1, TS * (TS + ZB))
-    numer = lax.conv_general_dilated(
-        cols, rhs, (1, 1), "VALID",
+    both = lax.conv_general_dilated(
+        cols, rhs, (1, 1), "VALID", rhs_dilation=(2, 1),
         dimension_numbers=lax.ConvDimensionNumbers((0, 3, 2, 1), (3, 2, 0, 1), (0, 3, 1, 2)),
         precision=lax.Precision.HIGH,
     )
+    numer = both[:, :rows_x, :, : nt * ZB] + both[:, 1:, :, nt * ZB:]
     numer = numer.reshape(rows_x, blocks * BY, nt * ZB)
     pos_x = jnp.arange(len_x, dtype=jnp.int32)
     out_x = jnp.arange(rows_x, dtype=jnp.int32)

time: 65.3 us -> 60.9 us (0.933)
  matrix products: 15.9 us -> 11.7 us
    conv_general_dilated x1, matrix products: 13.2 us -> 8.07 us  [local(): lax.conv_general_dilated(cols, rhs, (1, 1), 'VALID', rhs_dilation=(2, 1),...]
    dot_general x1, matrix products: 1.96 us -> 2.85 us  [toeplitz_rhs(): rhs = jnp.einsum('rk,wkn->rwn', kt, shift, precision=lax.Precision.HIGHEST)]
  transfers between devices with their start and end apart: 8 -> 8, of which waited for: 0 -> 0; matrix products, arithmetic and copies ran while one was open for 13% -> 14% of each run, Pallas kernels for 10% -> 11%
where the time goes in v6:
time: 60.9 us; the launch traced here: 60.5 us
  local copies, waits for them, and re-layouts  19.9 us (33%)
  starting transfers between devices  14 us (23%)
  matrix products  11.7 us (19%)
  other arithmetic  7.7 us (13%)
  Pallas kernels  6.61 us (11%)
  between operations  0.62 us (1%)
    ppermute x6, starting transfers between devices, gather_planes(): lax.ppermute(held, axis, [(i, i ^ s * step) for i in range(size)])  10.7 us
    conv_general_dilated x1, matrix products, local(): lax.conv_general_dilated(cols, rhs, (1, 1), 'VALID', rhs_dilation=(2, 1),...  8.07 us
    pallas_call x1, Pallas kernels, im2col(): pl.pallas_call(im2col_kernel, out_shape=jax.ShapeDtypeStruct((blocks, BY,...  6.61 us
    dot_general x1, matrix products, toeplitz_rhs(): rhs = jnp.einsum('rk,wkn->rwn', kt, shift, precision=lax.Precision.HIGHEST)  2.85 us
    transpose x1, local copies, waits for them, and re-layouts, local(): fields = jnp.transpose(fields, (3, 0, 2, 1, 4))  2.58 us
    dot_general x1, local copies, waits for them, and re-layouts, toeplitz_rhs(): rhs = jnp.einsum('rk,wkn->rwn', kt, shift, precision=lax.Precision.HIGHEST)  2.43 us
    reshape x1, local copies, waits for them, and re-layouts, local(): fields = fields.reshape(rows_x, blocks, BY, FIELDS, ZB)  2.05 us
    ppermute x1, starting transfers between devices, extended(): before = lax.ppermute(last, axis, up)  1.99 us
  transfers between devices with their start and end apart: 8, of which 0 were waited for; matrix products, arithmetic and copies ran while one was open for 14% of the time, Pallas kernels for 11%

profile of v6, /device:TPU:0, one launch (start us, length us, event | category | flops | bytes accessed | tf_op | source)
XLA Modules:
  0.0 60.5 jit_solution(2551382930175301731)
XLA Ops:
  0.5 2.5 %collective-permute-start.3 = (f32[1,8,256]{2,1,0:T(8,128)}, f32[1,8,256]{2,1,0:T(8,128)S(1)}, u32[]{:S(2)}, u32[]{:S(2)}) collective-permute-start(f32[1,8,256]{2,1,0:T(8,128)} %bitcast.91), channel_id=1, source_target_pairs={{0,2},{1,3},{2,0},{3,1},{4,6},{5,7},{6,4},{7,5},{8,10},{9,11},{10,... | collective-permute-start | bytes 24584 | tf_op jit(solution)/shard_map/ppermute | solution.py:56
  3.1 0.8 %fusion.87 = (f32[8,896]{1,0:T(8,128)S(1)}, f32[8,896]{1,0:T(8,128)S(1)}) fusion(f32[16,896]{1,0:T(8,128)} %param.5), kind=kLoop, calls=%fused_computation.177 | loop fusion | bytes 114688 | tf_op jit(solution)/shard_map/slice | solution.py:27
  3.9 2.0 %collective-permute-start = (f32[8,8,112]{2,0,1:T(8,128)S(1)}, f32[8,8,112]{2,0,1:T(8,128)S(1)}, u32[]{:S(2)}, u32[]{:S(2)}) collective-permute-start(f32[8,8,112]{2,0,1:T(8,128)S(1)} %copy.64), channel_id=1, source_target_pairs={{0,1},{1,2},{2,3},{3,4},{4,5},{5,6},{6,7},{7,8},{8,9},{9,10},{10,1... | collective-permute-start | bytes 86024 | tf_op jit(solution)/shard_map/ppermute | solution.py:28
  6.0 1.3 %collective-permute-start.1 = (f32[8,8,112]{2,0,1:T(8,128)S(1)}, f32[8,8,112]{2,0,1:T(8,128)S(1)}, u32[]{:S(2)}, u32[]{:S(2)}) collective-permute-start(f32[8,8,112]{2,0,1:T(8,128)S(1)} %copy.65), channel_id=1, source_target_pairs={{1,0},{2,1},{3,2},{4,3},{5,4},{6,5},{7,6},{8,7},{9,8},{10,9},{11,1... | collective-permute-start | bytes 86024 | tf_op jit(solution)/shard_map/ppermute | solution.py:29
  7.4 0.7 %broadcast_compare_fusion.10 = (pred[8]{0:T(512)(128)(4,1)S(1)}, pred[8]{0:T(512)(128)(4,1)S(1)}, pred[8]{0:T(512)(128)(4,1)S(1)}, pred[8]{0:T(512)(128)(4,1)S(1...) fusion(s32[8]{0:T(128)} %param.8), kind=kLoop, calls=%fused_computation.160 | loop fusion | flops 64 | bytes 96 | tf_op jit(solution)/shard_map/eq | solution.py:74
  8.0 0.7 %broadcast_compare_fusion.1 = (pred[8]{0:T(512)(128)(4,1)S(1)}, s32[8]{0:T(128)S(1)}, pred[8]{0:T(512)(128)(4,1)S(1)}, s32[8]{0:T(128)S(1)}) fusion(s32[8]{0:T(128)} %param.7), kind=kLoop, calls=%fused_computation.151 | loop fusion | flops 376 | bytes 112 | tf_op jit(solution)/shard_map/eq | solution.py:83
  8.7 0.7 %convert_element_type.4 = f32[8]{0:T(128)S(1)} convert(s32[8]{0:T(128)} %param.9) | non-fusion elementwise | flops 8 | bytes 64 | tf_op jit(solution)/shard_map/convert_element_type | solution.py:163
  9.8 0.9 %reshape.122 = f32[16,8,112]{2,1,0:T(8,128)S(1)} reshape(f32[16,896]{1,0:T(8,128)} %param.5) | data formatting | bytes 114688 | tf_op jit(solution)/shard_map/reshape | solution.py:128
  11.2 0.7 %fusion.48 = (f32[1,8,256]{2,1,0:T(8,128)S(1)}, f32[1,8,256]{2,1,0:T(8,128)S(1)}, f32[1,8,256]{2,1,0:T(8,128)S(1)}) fusion(f32[1,8,256]{2,1,0:T(8,128)S(1)} %collective-permute-done.4, f32[1,8,256]{2,1,0:T(8,128)S(1)} %collective-permute-done.3, f32[1,8,256]{2,1,0:T(8,128)S(1)} %collective-permute-done.2, f32[8,256]{1,0:T(8,128)} %param.6, pred[]{:T(512)S(6)} %eq.179, ...), kind=kLoop, calls=%fused_computation.93 | loop fusion | flops 43008 | bytes 57356 | tf_op jit(solution)/shard_map/add | solution.py:62
  12.0 5.0 %collective-permute-start.5 = (f32[4,8,256]{2,1,0:T(8,128)S(1)}, f32[4,8,256]{2,1,0:T(8,128)S(1)}, u32[]{:S(2)}, u32[]{:S(2)}) collective-permute-start(f32[4,8,256]{2,1,0:T(8,128)S(1)} %pad_maximum_fusion.1), channel_id=1, source_target_pairs={{0,4},{1,5},{2,6},{3,7},{4,0},{5,1},{6,2},{7,3},{8,12},{9,13},{10,... | collective-permute-start | bytes 98312 | tf_op jit(solution)/shard_map/ppermute | solution.py:56
  17.0 2.6 %collective-permute-start.6 = (f32[4,8,256]{2,1,0:T(8,128)S(1)}, f32[4,8,256]{2,1,0:T(8,128)S(1)}, u32[]{:S(2)}, u32[]{:S(2)}) collective-permute-start(f32[4,8,256]{2,1,0:T(8,128)S(1)} %pad_maximum_fusion.1), channel_id=1, source_target_pairs={{0,8},{1,9},{2,10},{3,11},{4,12},{5,13},{6,14},{7,15},{8,0},{9,1},... | collective-permute-start | bytes 98312 | tf_op jit(solution)/shard_map/ppermute | solution.py:56
  20.4 0.9 %slice_bitcast_fusion.p_ref = f32[24,31,128]{2,1,0:T(8,128)} fusion(f32[32,8,112]{2,0,1:T(8,128)S(1)} %constant_dynamic-update-slice_fusion), kind=kLoop, calls=%fused_computation.41 | loop fusion | bytes 495616 | tf_op jit(solution)/shard_map/transpose | solution.py:139
  21.3 6.6 %shard_map.55 = f32[7,8,31,512]{3,2,1,0:T(8,128)} custom-call(f32[24,31,128]{2,1,0:T(8,128)} %slice_bitcast_fusion.p_ref), custom_call_target="tpu_custom_call" | custom-call | bytes 3555328 | tf_op jit(solution)/shard_map/pallas_call | solution.py:115
  28.4 1.1 %copy.103 = f32[16,56,128]{2,0,1:T(8,128)} copy(f32[16,56,128]{1,2,0:T(8,128)S(1)} %bitcast.85) | data formatting | bytes 917504 | tf_op jit(solution)/shard_map/sqrt | solution.py:162
  31.6 0.9 %select_add_fusion = f32[8,16,16,16]{2,3,1,0:T(8,128)S(1)} fusion(f32[16,16,16]{1,2,0:T(8,128)S(1)} %copy.81, f32[16,16,16]{1,2,0:T(8,128)S(1)} %copy.79, f32[16,16,16]{1,2,0:T(8,128)S(1)} %copy.77, f32[16,16,16]{1,2,0:T(8,128)S(1)} %copy.75, f32[16,16,16]{1,2,0:T(8,128)S(1)} %copy.73, f32[16,16,16]{1,2,0:T(8,128)S(1)} %copy.71, f32[16,16,16]{1,2,0:T(8,128)S(1)} %copy.69, ...), kind=kLoop, calls=%fused_computation.29 | loop fusion | flops 491520 | bytes 262208 | tf_op jit(solution)/shard_map/add | solution.py:74
  34.1 0.7 %copy.83 = f32[8,16,16,16]{1,3,2,0:T(8,128)S(1)} copy(f32[8,16,16,16]{2,3,1,0:T(8,128)S(1)} %broadcast_select_fusion.1) | data formatting | bytes 262144 | tf_op jit(solution)/shard_map/jit(_where)/select_n | solution.py:78
  35.2 1.3 %bitcast_add_fusion.3 = f32[8,16,16,16]{1,3,2,0:T(8,128)} fusion(f32[8,16,16,16]{2,3,1,0:T(8,128)S(1)} %broadcast_select_fusion.1, f32[8,16,16,16]{1,2,3,0:T(8,128)S(1)} %copy.85, f32[8,16,16,16]{1,3,2,0:T(8,128)S(1)} %copy.83, pred[8]{0:T(512)(128)(4,1)S(1)} %get-tuple-element.47, pred[8]{0:T(512)(128)(4,1)S(1)} %get-tuple-element.46, ...), kind=kLoop, calls=%fused_computation.25 | loop fusion | flops 163840 | bytes 524312 | tf_op jit(solution)/shard_map/add | solution.py:83
  36.5 1.5 %copy.88 = f32[8,16,16,16]{3,1,2,0:T(8,128)S(1)} copy(f32[8,16,16,16]{1,3,2,0:T(8,128)} %bitcast_add_fusion.3) | data formatting | bytes 262144 | tf_op jit(solution)/shard_map/add | solution.py:83
  40.4 2.9 %fusion.1 = f32[128,32,256]{2,0,1:T(8,128)S(1)} fusion(f32[128,256,1]{0,1,2:T(8,128)S(1)} %reshape.152, s32[256]{0:T(256)S(1)} %get-tuple-element.52, s32[256]{0:T(256)S(1)} %get-tuple-element.55, s32[256]{0:T(256)S(1)} %get-tuple-element.53, s32[256]{0:T(256)S(1)} %get-tuple-element.54, pred[256]{0:T(512)(128)(4,1)S(1)} %get-tuple-element.50, ...), kind=kOutput, calls=%fused_computation.3 | convolution fusion | flops 3238002688 | bytes 4329984 | tf_op jit(solution)/shard_map/rk,wkn->rwn/dot_general | solution.py:100
  43.3 2.4 %copy.94 = f32[128,32,256]{2,1,0:T(8,128)S(1)} copy(f32[128,32,256]{2,0,1:T(8,128)S(1)} %fusion.1) | data formatting | bytes 8388608 | tf_op jit(solution)/shard_map/rk,wkn->rwn/dot_general | solution.py:100
  45.7 8.1 %fusion.15 = f32[17,8,7,256]{3,1,2,0:T(8,128)S(1)} fusion(f32[8,1,512,256]{3,2,1,0:T(8,128)S(1)} %bitcast.82, f32[8,7,31,512]{3,2,1,0:T(8,128)S(1)} %bitcast.81), kind=kOutput, calls=%fused_computation.16 | convolution fusion | flops 5989466112 | bytes 8724480 | tf_op jit(solution)/shard_map/conv_general_dilated | solution.py:141
  54.4 2.1 %reshape.128 = f32[16,7,8,4,16]{4,3,2,1,0:T(4,128)} reshape(f32[16,56,64]{2,1,0:T(8,128)S(1)} %copy.104) | data formatting | bytes 458752 | tf_op jit(solution)/shard_map/reshape | solution.py:173
  56.5 2.6 %copy.105 = f32[4,16,8,7,16]{4,3,2,1,0:T(8,128)S(1)} copy(f32[4,16,8,7,16]{4,0,2,3,1:T(4,128)} %bitcast.84) | data formatting | bytes 458752 | tf_op jit(solution)/shard_map/transpose | solution.py:174
  59.1 1.4 %reshape.129 = f32[4,16,896]{2,1,0:T(8,128)} reshape(f32[4,16,8,7,16]{4,3,2,1,0:T(8,128)S(1)} %copy.105) | data formatting | bytes 458752 | tf_op jit(solution)/shard_map/reshape | solution.py:175
  (87 shorter events, 9.7 us)
Async XLA Ops:
  0.0 11.2 %collective-permute-start.2 = (f32[1,8,256]{2,1,0:T(8,128)}, f32[1,8,256]{2,1,0:T(8,128)S(1)}, u32[]{:S(2)}, u32[]{:S(2)}) collective-permute-start(f32[1,8,256]{2,1,0:T(8,128)} %bitcast.90), channel_id=1, source_target_pairs={{0,1},{1,0},{2,3},{3,2},{4,5},{5,4},{6,7},{7,6},{8,9},{9,8},{10,11... | collective-permute-start | bytes 24584 | tf_op jit(solution)/shard_map/ppermute | solution.py:56
  0.5 10.7 %collective-permute-start.3 = (f32[1,8,256]{2,1,0:T(8,128)}, f32[1,8,256]{2,1,0:T(8,128)S(1)}, u32[]{:S(2)}, u32[]{:S(2)}) collective-permute-start(f32[1,8,256]{2,1,0:T(8,128)} %bitcast.91), channel_id=1, source_target_pairs={{0,2},{1,3},{2,0},{3,1},{4,6},{5,7},{6,4},{7,5},{8,10},{9,11},{10,... | collective-permute-start | bytes 24584 | tf_op jit(solution)/shard_map/ppermute | solution.py:56
  2.9 8.3 %collective-permute-start.4 = (f32[1,8,256]{2,1,0:T(8,128)}, f32[1,8,256]{2,1,0:T(8,128)S(1)}, u32[]{:S(2)}, u32[]{:S(2)}) collective-permute-start(f32[1,8,256]{2,1,0:T(8,128)} %bitcast.92), channel_id=1, source_target_pairs={{0,3},{1,2},{2,1},{3,0},{4,7},{5,6},{6,5},{7,4},{8,11},{9,10},{10,... | collective-permute-start | bytes 24584 | tf_op jit(solution)/shard_map/ppermute | solution.py:56
  3.9 15.7 %collective-permute-start = (f32[8,8,112]{2,0,1:T(8,128)S(1)}, f32[8,8,112]{2,0,1:T(8,128)S(1)}, u32[]{:S(2)}, u32[]{:S(2)}) collective-permute-start(f32[8,8,112]{2,0,1:T(8,128)S(1)} %copy.64), channel_id=1, source_target_pairs={{0,1},{1,2},{2,3},{3,4},{4,5},{5,6},{6,7},{7,8},{8,9},{9,10},{10,1... | collective-permute-start | bytes 86024 | tf_op jit(solution)/shard_map/ppermute | solution.py:28
  6.0 13.6 %collective-permute-start.1 = (f32[8,8,112]{2,0,1:T(8,128)S(1)}, f32[8,8,112]{2,0,1:T(8,128)S(1)}, u32[]{:S(2)}, u32[]{:S(2)}) collective-permute-start(f32[8,8,112]{2,0,1:T(8,128)S(1)} %copy.65), channel_id=1, source_target_pairs={{1,0},{2,1},{3,2},{4,3},{5,4},{6,5},{7,6},{8,7},{9,8},{10,9},{11,1... | collective-permute-start | bytes 86024 | tf_op jit(solution)/shard_map/ppermute | solution.py:29
  12.0 17.6 %collective-permute-start.5 = (f32[4,8,256]{2,1,0:T(8,128)S(1)}, f32[4,8,256]{2,1,0:T(8,128)S(1)}, u32[]{:S(2)}, u32[]{:S(2)}) collective-permute-start(f32[4,8,256]{2,1,0:T(8,128)S(1)} %pad_maximum_fusion.1), channel_id=1, source_target_pairs={{0,4},{1,5},{2,6},{3,7},{4,0},{5,1},{6,2},{7,3},{8,12},{9,13},{10,... | collective-permute-start | bytes 98312 | tf_op jit(solution)/shard_map/ppermute | solution.py:56
  17.0 12.5 %collective-permute-start.6 = (f32[4,8,256]{2,1,0:T(8,128)S(1)}, f32[4,8,256]{2,1,0:T(8,128)S(1)}, u32[]{:S(2)}, u32[]{:S(2)}) collective-permute-start(f32[4,8,256]{2,1,0:T(8,128)S(1)} %pad_maximum_fusion.1), channel_id=1, source_target_pairs={{0,8},{1,9},{2,10},{3,11},{4,12},{5,13},{6,14},{7,15},{8,0},{9,1},... | collective-permute-start | bytes 98312 | tf_op jit(solution)/shard_map/ppermute | solution.py:56
  19.6 10.0 %collective-permute-start.7 = (f32[4,8,256]{2,1,0:T(8,128)S(1)}, f32[4,8,256]{2,1,0:T(8,128)S(1)}, u32[]{:S(2)}, u32[]{:S(2)}) collective-permute-start(f32[4,8,256]{2,1,0:T(8,128)S(1)} %pad_maximum_fusion.1), channel_id=1, source_target_pairs={{0,12},{1,13},{2,14},{3,15},{4,8},{5,9},{6,10},{7,11},{8,4},{9,5},... | collective-permute-start | bytes 98312 | tf_op jit(solution)/shard_map/ppermute | solution.py:56
  43.3 2.4 %copy-start = (f32[7,8,31,512]{3,2,1,0:T(8,128)S(1)}, f32[7,8,31,512]{3,2,1,0:T(8,128)}, u32[]{:S(2)}) copy-start(f32[7,8,31,512]{3,2,1,0:T(8,128)} %shard_map.55) | copy-start | bytes 10665988
  45.7 8.2 %copy-start.1 = (f32[16,56,128]{2,0,1:T(8,128)S(1)}, f32[16,56,128]{2,0,1:T(8,128)}, u32[]{:S(2)}) copy-start(f32[16,56,128]{2,0,1:T(8,128)} %copy.103) | copy-start | bytes 1376260

commit v7 on v6

--- a/solution.py
+++ b/solution.py
@@ -121,6 +121,34 @@
     )(padded_t)
 
 
+def post_kernel(both_ref, energy_ref, wl_ref, tl_ref, o_ref):
+    rows = o_ref.shape[1]
+    lanes = wl_ref.shape[-1]
+    half_lanes = tl_ref.shape[-1]
+    numer = both_ref[:, 0:rows, 0:lanes] + both_ref[:, 1:rows + 1, lanes:2 * lanes]
+    scores = numer / jnp.sqrt(energy_ref[...] + epsilon)
+    weighted = wl_ref[...] * jnp.exp(sharpness * scores)
+    grouped = weighted[:, :, 0:half_lanes]
+    for p in range(1, lanes // half_lanes):
+        grouped = grouped + weighted[:, :, p * half_lanes:(p + 1) * half_lanes]
+    fields = jnp.log(grouped / tl_ref[...])
+    blocks = both_ref.shape[0] // BY
+    for k in range(o_ref.shape[0]):
+        for zb in range(blocks):
+            for y in range(BY):
+                at = y * BZ + zb * ZB
+                o_ref[k, :, at:at + ZB] = fields[zb * BY + y, :, k * ZB:(k + 1) * ZB]
+
+
+def post(both, energy, wl, tl, rows_x):
+    return pl.pallas_call(
+        post_kernel,
+        out_shape=jax.ShapeDtypeStruct((FIELDS, rows_x, BY * BZ), jnp.float32),
+        in_specs=[pl.BlockSpec(memory_space=pltpu.VMEM)] * 4,
+        out_specs=pl.BlockSpec(memory_space=pltpu.VMEM),
+    )(both, energy, wl, tl)
+
+
 def local(volume, bank, orient, bank_id, counts):
     rows_x = volume.shape[0]
     half = TS // 2
@@ -140,11 +168,9 @@
     cols = cols.reshape(1, blocks * BY, len_x - 1, TS * (TS + ZB))
     both = lax.conv_general_dilated(
         cols, rhs, (1, 1), "VALID", rhs_dilation=(2, 1),
-        dimension_numbers=lax.ConvDimensionNumbers((0, 3, 2, 1), (3, 2, 0, 1), (0, 3, 1, 2)),
+        dimension_numbers=lax.ConvDimensionNumbers((0, 3, 2, 1), (3, 2, 0, 1), (0, 3, 2, 1)),
         precision=lax.Precision.HIGH,
     )
-    numer = both[:, :rows_x, :, : nt * ZB] + both[:, 1:, :, nt * ZB:]
-    numer = numer.reshape(rows_x, blocks * BY, nt * ZB)
     pos_x = jnp.arange(len_x, dtype=jnp.int32)
     out_x = jnp.arange(rows_x, dtype=jnp.int32)
     pos_y = half + jnp.arange(BY, dtype=jnp.int32)
@@ -157,22 +183,15 @@
         "xyn,ym->xmn", energy, band_table(pos_y, jnp.arange(BY, dtype=jnp.int32), len_y)
     )
     energy = contract("xmn,xl->lmn", energy, band_table(pos_x, out_x, len_x))
-    energy = jnp.transpose(energy.reshape(rows_x, BY, blocks, ZB), (0, 2, 1, 3))
-    energy = jnp.tile(energy.reshape(rows_x, blocks * BY, ZB), (1, 1, nt))
-    scores = numer / jnp.sqrt(energy + epsilon)
+    energy = jnp.transpose(energy.reshape(rows_x, BY, blocks, ZB), (2, 1, 0, 3))
+    energy = jnp.tile(energy.reshape(blocks * BY, rows_x, ZB), (1, 1, nt))
     weights = jnp.transpose(counts.astype(jnp.float32).reshape(FIELDS, per)).reshape(nt)
-    weighted = jnp.repeat(weights, ZB)[None, None] * jnp.exp(sharpness * scores)
-    half_lanes = FIELDS * ZB
-    grouped = weighted[:, :, :half_lanes]
-    for p in range(1, per):
-        grouped = grouped + weighted[:, :, p * half_lanes:(p + 1) * half_lanes]
     totals = weights[:FIELDS]
     for p in range(1, per):
         totals = totals + weights[p * FIELDS:(p + 1) * FIELDS]
-    fields = jnp.log(grouped / jnp.repeat(totals, ZB)[None, None])
-    fields = fields.reshape(rows_x, blocks, BY, FIELDS, ZB)
-    fields = jnp.transpose(fields, (3, 0, 2, 1, 4))
-    return fields.reshape(FIELDS, rows_x, BY * BZ)
+    wl = jnp.repeat(weights, ZB)[None, None]
+    tl = jnp.repeat(totals, ZB)[None, None]
+    return post(both[0], energy, wl, tl, rows_x)
 
 
 def solution(mesh):

time: 60.9 us -> 91.6 us (1.50)
  matrix products: 11.7 us -> 43.3 us
  local copies, waits for them, and re-layouts: 19.9 us -> 16.4 us
  Pallas kernels: 6.61 us -> 9.6 us
    conv_general_dilated x1, matrix products: 8.07 us -> 39.7 us  [local(): lax.conv_general_dilated(cols, rhs, (1, 1), 'VALID', rhs_dilation=(2, 1),...]
    reshape x2 -> x1, local copies, waits for them, and re-layouts: 3.45 us -> 0.17 us  [local(): energy = jnp.transpose(energy.reshape(rows_x, BY, blocks, ZB), (2, 1, 0, 3))]
    pallas_call x0 -> x1, Pallas kernels: none -> 2.99 us  [post(): pl.pallas_call(post_kernel, out_shape=jax.ShapeDtypeStruct((FIELDS, rows_...]
    another operation x1 -> x5, local copies, waits for them, and re-layouts: 0.1 us -> 2.7 us  [the longest x3 1.41 us: local(): energy = jnp.tile(energy.reshape(blocks * BY, rows_x, ZB), (1, 1, nt))]
    transpose x1, local copies, waits for them, and re-layouts: 2.58 us -> 0.27 us  [local(): energy = jnp.transpose(energy.reshape(rows_x, BY, blocks, ZB), (2, 1, 0, 3))]
    sqrt x5 -> x0, local copies, waits for them, and re-layouts: 1.54 us -> none  [local(): scores = numer / jnp.sqrt(energy + epsilon)]
    conv_general_dilated x0 -> x1, local copies, waits for them, and re-layouts: none -> 1.42 us  [local(): lax.conv_general_dilated(cols, rhs, (1, 1), 'VALID', rhs_dilation=(2, 1),...]
  transfers between devices with their start and end apart: 8 -> 8, of which waited for: 0 -> 0; matrix products, arithmetic and copies ran while one was open for 14% -> 11% of each run, Pallas kernels for 11% -> 7%
where the time goes in v7:
time: 91.6 us; the launch traced here: 91.2 us
  matrix products  43.3 us (47%)
  local copies, waits for them, and re-layouts  16.4 us (18%)
  starting transfers between devices  14 us (15%)
  Pallas kernels  9.6 us (10%)
  other arithmetic  7.36 us (8%)
    conv_general_dilated x1, matrix products, local(): lax.conv_general_dilated(cols, rhs, (1, 1), 'VALID', rhs_dilation=(2, 1),...  39.7 us
    ppermute x6, starting transfers between devices, gather_planes(): lax.ppermute(held, axis, [(i, i ^ s * step) for i in range(size)])  10.7 us
    pallas_call x1, Pallas kernels, im2col(): pl.pallas_call(im2col_kernel, out_shape=jax.ShapeDtypeStruct((blocks, BY,...  6.61 us
    pallas_call x1, Pallas kernels, post(): pl.pallas_call(post_kernel, out_shape=jax.ShapeDtypeStruct((FIELDS, rows_...  2.99 us
    dot_general x1, matrix products, toeplitz_rhs(): rhs = jnp.einsum('rk,wkn->rwn', kt, shift, precision=lax.Precision.HIGHEST)  2.85 us
    dot_general x1, local copies, waits for them, and re-layouts, toeplitz_rhs(): rhs = jnp.einsum('rk,wkn->rwn', kt, shift, precision=lax.Precision.HIGHEST)  2.43 us
    ppermute x1, starting transfers between devices, extended(): before = lax.ppermute(last, axis, up)  1.99 us
  transfers between devices with their start and end apart: 8, of which 0 were waited for; matrix products, arithmetic and copies ran while one was open for 11% of the time, Pallas kernels for 7%

profile of v7, /device:TPU:0, one launch (start us, length us, event | category | flops | bytes accessed | tf_op | source)
XLA Modules:
  0.0 91.2 jit_solution(14292969865969509129)
XLA Ops:
  0.5 2.5 %collective-permute-start.3 = (f32[1,8,256]{2,1,0:T(8,128)}, f32[1,8,256]{2,1,0:T(8,128)S(1)}, u32[]{:S(2)}, u32[]{:S(2)}) collective-permute-start(f32[1,8,256]{2,1,0:T(8,128)} %bitcast.83), channel_id=1, source_target_pairs={{0,2},{1,3},{2,0},{3,1},{4,6},{5,7},{6,4},{7,5},{8,10},{9,11},{10,... | collective-permute-start | bytes 24584 | tf_op jit(solution)/shard_map/ppermute | solution.py:56
  3.1 0.8 fusion.82
  3.9 2.0 %collective-permute-start = (f32[8,8,112]{2,0,1:T(8,128)S(1)}, f32[8,8,112]{2,0,1:T(8,128)S(1)}, u32[]{:S(2)}, u32[]{:S(2)}) collective-permute-start(f32[8,8,112]{2,0,1:T(8,128)S(1)} %copy.62), channel_id=1, source_target_pairs={{0,1},{1,2},{2,3},{3,4},{4,5},{5,6},{6,7},{7,8},{8,9},{9,10},{10,1... | collective-permute-start | bytes 86024 | tf_op jit(solution)/shard_map/ppermute | solution.py:28
  6.0 1.3 %collective-permute-start.1 = (f32[8,8,112]{2,0,1:T(8,128)S(1)}, f32[8,8,112]{2,0,1:T(8,128)S(1)}, u32[]{:S(2)}, u32[]{:S(2)}) collective-permute-start(f32[8,8,112]{2,0,1:T(8,128)S(1)} %copy.63), channel_id=1, source_target_pairs={{1,0},{2,1},{3,2},{4,3},{5,4},{6,5},{7,6},{8,7},{9,8},{10,9},{11,1... | collective-permute-start | bytes 86024 | tf_op jit(solution)/shard_map/ppermute | solution.py:29
  7.4 0.7 broadcast_compare_fusion.10
  8.0 0.7 broadcast_compare_fusion.1
  8.7 0.7 convert_element_type.4
  9.8 0.9 reshape.103
  11.6 0.7 broadcast_in_dim_reshape.7.tl_ref
  12.4 0.7 fusion.43
  13.1 5.0 %collective-permute-start.5 = (f32[4,8,256]{2,1,0:T(8,128)S(1)}, f32[4,8,256]{2,1,0:T(8,128)S(1)}, u32[]{:S(2)}, u32[]{:S(2)}) collective-permute-start(f32[4,8,256]{2,1,0:T(8,128)S(1)} %pad_maximum_fusion.1), channel_id=1, source_target_pairs={{0,4},{1,5},{2,6},{3,7},{4,0},{5,1},{6,2},{7,3},{8,12},{9,13},{10,... | collective-permute-start | bytes 98312 | tf_op jit(solution)/shard_map/ppermute | solution.py:56
  18.1 2.6 %collective-permute-start.6 = (f32[4,8,256]{2,1,0:T(8,128)S(1)}, f32[4,8,256]{2,1,0:T(8,128)S(1)}, u32[]{:S(2)}, u32[]{:S(2)}) collective-permute-start(f32[4,8,256]{2,1,0:T(8,128)S(1)} %pad_maximum_fusion.1), channel_id=1, source_target_pairs={{0,8},{1,9},{2,10},{3,11},{4,12},{5,13},{6,14},{7,15},{8,0},{9,1},... | collective-permute-start | bytes 98312 | tf_op jit(solution)/shard_map/ppermute | solution.py:56
  21.5 0.9 slice_bitcast_fusion.p_ref
  22.4 6.6 %shard_map.55 = f32[7,8,31,512]{3,2,1,0:T(8,128)} custom-call(f32[24,31,128]{2,1,0:T(8,128)} %slice_bitcast_fusion.p_ref), custom_call_target="tpu_custom_call" | custom-call | bytes 3555328 | tf_op jit(solution)/shard_map/pallas_call | solution.py:115
  29.8 1.1 %copy.102.energy_ref = f32[56,16,128]{2,1,0:T(8,128)} copy(f32[56,16,128]{0,2,1:T(8,128)S(1)} %bitcast.76) | data formatting | bytes 917504 | tf_op jit(solution)/shard_map/tile | solution.py:187
  32.9 0.9 select_add_fusion
  35.4 0.7 copy.81
  36.5 1.3 %bitcast_add_fusion.3 = f32[8,16,16,16]{1,3,2,0:T(8,128)} fusion(f32[8,16,16,16]{2,3,1,0:T(8,128)S(1)} %broadcast_select_fusion.1, f32[8,16,16,16]{1,2,3,0:T(8,128)S(1)} %copy.83, f32[8,16,16,16]{1,3,2,0:T(8,128)S(1)} %copy.81, pred[8]{0:T(512)(128)(4,1)S(1)} %get-tuple-element.47, pred[8]{0:T(512)(128)(4,1)S(1)} %get-tuple-element.46, ...), kind=kLoop, calls=%fused_computation.24 | loop fusion | flops 163840 | bytes 524312 | tf_op jit(solution)/shard_map/add | solution.py:83
  37.8 1.5 %copy.86 = f32[8,16,16,16]{3,1,2,0:T(8,128)S(1)} copy(f32[8,16,16,16]{1,3,2,0:T(8,128)} %bitcast_add_fusion.3) | data formatting | bytes 262144 | tf_op jit(solution)/shard_map/add | solution.py:83
  41.7 2.9 %fusion.1 = f32[128,32,256]{2,0,1:T(8,128)S(1)} fusion(f32[128,256,1]{0,1,2:T(8,128)S(1)} %reshape.117, s32[256]{0:T(256)S(1)} %get-tuple-element.52, s32[256]{0:T(256)S(1)} %get-tuple-element.55, s32[256]{0:T(256)S(1)} %get-tuple-element.53, s32[256]{0:T(256)S(1)} %get-tuple-element.54, pred[256]{0:T(512)(128)(4,1)S(1)} %get-tuple-element.50, ...), kind=kOutput, calls=%fused_computation.3 | convolution fusion | flops 3238002688 | bytes 4329984 | tf_op jit(solution)/shard_map/rk,wkn->rwn/dot_general | solution.py:100
  44.6 2.4 %copy.92 = f32[128,32,256]{2,1,0:T(8,128)S(1)} copy(f32[128,32,256]{2,0,1:T(8,128)S(1)} %fusion.1) | data formatting | bytes 8388608 | tf_op jit(solution)/shard_map/rk,wkn->rwn/dot_general | solution.py:100
  47.0 39.7 %fusion.15 = f32[1,56,17,256]{3,0,1,2:T(1,128)S(1)} fusion(f32[8,1,512,256]{3,2,1,0:T(8,128)S(1)} %bitcast.75, f32[1,56,31,512]{3,2,1,0:T(8,128)S(1)} %bitcast.77), kind=kOutput, calls=%fused_computation.16 | convolution fusion | flops 5989466112 | bytes 8724480 | tf_op jit(solution)/shard_map/conv_general_dilated | solution.py:169
  86.8 1.4 %copy.118 = f32[1,56,17,256]{3,2,1,0:T(8,128)} copy(f32[1,56,17,256]{3,0,1,2:T(1,128)S(1)} %fusion.15) | data formatting | bytes 1949696 | tf_op jit(solution)/shard_map/conv_general_dilated | solution.py:169
  88.2 3.0 %shard_map.56 = f32[4,16,896]{2,1,0:T(8,128)} custom-call(f32[56,17,256]{2,1,0:T(8,128)} %bitcast.74, f32[56,16,128]{2,1,0:T(8,128)} %copy.102.energy_ref, f32[1,1,128]{2,1,0:T(1,128)} %broadcast_in_dim_reshape.6.wl_ref, f32[1,1,64]{2,1,0:T(1,128)} %broadcast_in_dim_reshape.7.tl_ref), custom_call_target="tpu_custom_call" | custom-call | tf_op jit(solution)/shard_map/pallas_call | solution.py:144
  (79 shorter events, 9.8 us)
Async XLA Ops:
  0.0 12.3 %collective-permute-start.2 = (f32[1,8,256]{2,1,0:T(8,128)}, f32[1,8,256]{2,1,0:T(8,128)S(1)}, u32[]{:S(2)}, u32[]{:S(2)}) collective-permute-start(f32[1,8,256]{2,1,0:T(8,128)} %bitcast.82), channel_id=1, source_target_pairs={{0,1},{1,0},{2,3},{3,2},{4,5},{5,4},{6,7},{7,6},{8,9},{9,8},{10,11... | collective-permute-start | bytes 24584 | tf_op jit(solution)/shard_map/ppermute | solution.py:56
  0.5 11.9 %collective-permute-start.3 = (f32[1,8,256]{2,1,0:T(8,128)}, f32[1,8,256]{2,1,0:T(8,128)S(1)}, u32[]{:S(2)}, u32[]{:S(2)}) collective-permute-start(f32[1,8,256]{2,1,0:T(8,128)} %bitcast.83), channel_id=1, source_target_pairs={{0,2},{1,3},{2,0},{3,1},{4,6},{5,7},{6,4},{7,5},{8,10},{9,11},{10,... | collective-permute-start | bytes 24584 | tf_op jit(solution)/shard_map/ppermute | solution.py:56
  2.9 9.4 %collective-permute-start.4 = (f32[1,8,256]{2,1,0:T(8,128)}, f32[1,8,256]{2,1,0:T(8,128)S(1)}, u32[]{:S(2)}, u32[]{:S(2)}) collective-permute-start(f32[1,8,256]{2,1,0:T(8,128)} %bitcast.84), channel_id=1, source_target_pairs={{0,3},{1,2},{2,1},{3,0},{4,7},{5,6},{6,5},{7,4},{8,11},{9,10},{10,... | collective-permute-start | bytes 24584 | tf_op jit(solution)/shard_map/ppermute | solution.py:56
  3.9 16.8 %collective-permute-start = (f32[8,8,112]{2,0,1:T(8,128)S(1)}, f32[8,8,112]{2,0,1:T(8,128)S(1)}, u32[]{:S(2)}, u32[]{:S(2)}) collective-permute-start(f32[8,8,112]{2,0,1:T(8,128)S(1)} %copy.62), channel_id=1, source_target_pairs={{0,1},{1,2},{2,3},{3,4},{4,5},{5,6},{6,7},{7,8},{8,9},{9,10},{10,1... | collective-permute-start | bytes 86024 | tf_op jit(solution)/shard_map/ppermute | solution.py:28
  6.0 14.7 %collective-permute-start.1 = (f32[8,8,112]{2,0,1:T(8,128)S(1)}, f32[8,8,112]{2,0,1:T(8,128)S(1)}, u32[]{:S(2)}, u32[]{:S(2)}) collective-permute-start(f32[8,8,112]{2,0,1:T(8,128)S(1)} %copy.63), channel_id=1, source_target_pairs={{1,0},{2,1},{3,2},{4,3},{5,4},{6,5},{7,6},{8,7},{9,8},{10,9},{11,1... | collective-permute-start | bytes 86024 | tf_op jit(solution)/shard_map/ppermute | solution.py:29
  13.1 17.8 %collective-permute-start.5 = (f32[4,8,256]{2,1,0:T(8,128)S(1)}, f32[4,8,256]{2,1,0:T(8,128)S(1)}, u32[]{:S(2)}, u32[]{:S(2)}) collective-permute-start(f32[4,8,256]{2,1,0:T(8,128)S(1)} %pad_maximum_fusion.1), channel_id=1, source_target_pairs={{0,4},{1,5},{2,6},{3,7},{4,0},{5,1},{6,2},{7,3},{8,12},{9,13},{10,... | collective-permute-start | bytes 98312 | tf_op jit(solution)/shard_map/ppermute | solution.py:56
  18.1 12.8 %collective-permute-start.6 = (f32[4,8,256]{2,1,0:T(8,128)S(1)}, f32[4,8,256]{2,1,0:T(8,128)S(1)}, u32[]{:S(2)}, u32[]{:S(2)}) collective-permute-start(f32[4,8,256]{2,1,0:T(8,128)S(1)} %pad_maximum_fusion.1), channel_id=1, source_target_pairs={{0,8},{1,9},{2,10},{3,11},{4,12},{5,13},{6,14},{7,15},{8,0},{9,1},... | collective-permute-start | bytes 98312 | tf_op jit(solution)/shard_map/ppermute | solution.py:56
  20.7 10.2 %collective-permute-start.7 = (f32[4,8,256]{2,1,0:T(8,128)S(1)}, f32[4,8,256]{2,1,0:T(8,128)S(1)}, u32[]{:S(2)}, u32[]{:S(2)}) collective-permute-start(f32[4,8,256]{2,1,0:T(8,128)S(1)} %pad_maximum_fusion.1), channel_id=1, source_target_pairs={{0,12},{1,13},{2,14},{3,15},{4,8},{5,9},{6,10},{7,11},{8,4},{9,5},... | collective-permute-start | bytes 98312 | tf_op jit(solution)/shard_map/ppermute | solution.py:56
  44.6 2.4 %copy-start = (f32[7,8,31,512]{3,2,1,0:T(8,128)S(1)}, f32[7,8,31,512]{3,2,1,0:T(8,128)}, u32[]{:S(2)}) copy-start(f32[7,8,31,512]{3,2,1,0:T(8,128)} %shard_map.55) | copy-start | bytes 10665988

commit v8 on v7

--- a/solution.py
+++ b/solution.py
@@ -121,23 +121,23 @@
     )(padded_t)
 
 
-def post_kernel(both_ref, energy_ref, wl_ref, tl_ref, o_ref):
+def post_kernel(both_ref, energy_ref, wl_ref, tl_ref, o_ref, fields_ref):
     rows = o_ref.shape[1]
     lanes = wl_ref.shape[-1]
     half_lanes = tl_ref.shape[-1]
-    numer = both_ref[:, 0:rows, 0:lanes] + both_ref[:, 1:rows + 1, lanes:2 * lanes]
+    numer = both_ref[0:rows, :, 0:lanes] + both_ref[1:rows + 1, :, lanes:2 * lanes]
     scores = numer / jnp.sqrt(energy_ref[...] + epsilon)
     weighted = wl_ref[...] * jnp.exp(sharpness * scores)
     grouped = weighted[:, :, 0:half_lanes]
     for p in range(1, lanes // half_lanes):
         grouped = grouped + weighted[:, :, p * half_lanes:(p + 1) * half_lanes]
-    fields = jnp.log(grouped / tl_ref[...])
-    blocks = both_ref.shape[0] // BY
+    fields_ref[...] = jnp.log(grouped / tl_ref[...])
+    blocks = both_ref.shape[1] // BY
     for k in range(o_ref.shape[0]):
         for zb in range(blocks):
             for y in range(BY):
                 at = y * BZ + zb * ZB
-                o_ref[k, :, at:at + ZB] = fields[zb * BY + y, :, k * ZB:(k + 1) * ZB]
+                o_ref[k, :, at:at + ZB] = fields_ref[:, zb * BY + y, k * ZB:(k + 1) * ZB]
 
 
 def post(both, energy, wl, tl, rows_x):
@@ -146,6 +146,7 @@
         out_shape=jax.ShapeDtypeStruct((FIELDS, rows_x, BY * BZ), jnp.float32),
         in_specs=[pl.BlockSpec(memory_space=pltpu.VMEM)] * 4,
         out_specs=pl.BlockSpec(memory_space=pltpu.VMEM),
+        scratch_shapes=[pltpu.VMEM((rows_x, both.shape[1], tl.shape[-1]), jnp.float32)],
     )(both, energy, wl, tl)
 
 
@@ -168,7 +169,7 @@
     cols = cols.reshape(1, blocks * BY, len_x - 1, TS * (TS + ZB))
     both = lax.conv_general_dilated(
         cols, rhs, (1, 1), "VALID", rhs_dilation=(2, 1),
-        dimension_numbers=lax.ConvDimensionNumbers((0, 3, 2, 1), (3, 2, 0, 1), (0, 3, 2, 1)),
+        dimension_numbers=lax.ConvDimensionNumbers((0, 3, 2, 1), (3, 2, 0, 1), (0, 3, 1, 2)),
         precision=lax.Precision.HIGH,
     )
     pos_x = jnp.arange(len_x, dtype=jnp.int32)
@@ -183,8 +184,8 @@
         "xyn,ym->xmn", energy, band_table(pos_y, jnp.arange(BY, dtype=jnp.int32), len_y)
     )
     energy = contract("xmn,xl->lmn", energy, band_table(pos_x, out_x, len_x))
-    energy = jnp.transpose(energy.reshape(rows_x, BY, blocks, ZB), (2, 1, 0, 3))
-    energy = jnp.tile(energy.reshape(blocks * BY, rows_x, ZB), (1, 1, nt))
+    energy = jnp.transpose(energy.reshape(rows_x, BY, blocks, ZB), (0, 2, 1, 3))
+    energy = jnp.tile(energy.reshape(rows_x, blocks * BY, ZB), (1, 1, nt))
     weights = jnp.transpose(counts.astype(jnp.float32).reshape(FIELDS, per)).reshape(nt)
     totals = weights[:FIELDS]
     for p in range(1, per):

time: 91.6 us -> 91.3 us (level)
    conv_general_dilated x1 -> x0, local copies, waits for them, and re-layouts: 1.42 us -> none  [local(): lax.conv_general_dilated(cols, rhs, (1, 1), 'VALID', rhs_dilation=(2, 1),...]
    unnamed x4 -> x5, local copies, waits for them, and re-layouts: 0.02 us -> 1.05 us
where the time goes in v8:
time: 91.3 us; the launch traced here: 90.9 us
  matrix products  43.3 us (47%)
  local copies, waits for them, and re-layouts  15.7 us (17%)
  starting transfers between devices  14 us (15%)
  Pallas kernels  9.96 us (11%)
  other arithmetic  7.36 us (8%)
    conv_general_dilated x1, matrix products, local(): lax.conv_general_dilated(cols, rhs, (1, 1), 'VALID', rhs_dilation=(2, 1),...  39.7 us
    ppermute x6, starting transfers between devices, gather_planes(): lax.ppermute(held, axis, [(i, i ^ s * step) for i in range(size)])  10.7 us
    pallas_call x1, Pallas kernels, im2col(): pl.pallas_call(im2col_kernel, out_shape=jax.ShapeDtypeStruct((blocks, BY,...  6.61 us
    pallas_call x1, Pallas kernels, post(): pl.pallas_call(post_kernel, out_shape=jax.ShapeDtypeStruct((FIELDS, rows_...  3.35 us
    dot_general x1, matrix products, toeplitz_rhs(): rhs = jnp.einsum('rk,wkn->rwn', kt, shift, precision=lax.Precision.HIGHEST)  2.85 us
    dot_general x1, local copies, waits for them, and re-layouts, toeplitz_rhs(): rhs = jnp.einsum('rk,wkn->rwn', kt, shift, precision=lax.Precision.HIGHEST)  2.43 us
    ppermute x1, starting transfers between devices, extended(): before = lax.ppermute(last, axis, up)  1.99 us
  transfers between devices with their start and end apart: 8, of which 0 were waited for; matrix products, arithmetic and copies ran while one was open for 11% of the time, Pallas kernels for 7%

profile of v8, /device:TPU:0, one launch (start us, length us, event | category | flops | bytes accessed | tf_op | source)
XLA Modules:
  0.0 90.9 jit_solution(12055035580254063666)
XLA Ops:
  0.5 2.5 %collective-permute-start.3 = (f32[1,8,256]{2,1,0:T(8,128)}, f32[1,8,256]{2,1,0:T(8,128)S(1)}, u32[]{:S(2)}, u32[]{:S(2)}) collective-permute-start(f32[1,8,256]{2,1,0:T(8,128)} %bitcast.85), channel_id=1, source_target_pairs={{0,2},{1,3},{2,0},{3,1},{4,6},{5,7},{6,4},{7,5},{8,10},{9,11},{10,... | collective-permute-start | bytes 24584 | tf_op jit(solution)/shard_map/ppermute | solution.py:56
  3.1 0.8 fusion.82
  3.9 2.0 %collective-permute-start = (f32[8,8,112]{2,0,1:T(8,128)S(1)}, f32[8,8,112]{2,0,1:T(8,128)S(1)}, u32[]{:S(2)}, u32[]{:S(2)}) collective-permute-start(f32[8,8,112]{2,0,1:T(8,128)S(1)} %copy.60), channel_id=1, source_target_pairs={{0,1},{1,2},{2,3},{3,4},{4,5},{5,6},{6,7},{7,8},{8,9},{9,10},{10,1... | collective-permute-start | bytes 86024 | tf_op jit(solution)/shard_map/ppermute | solution.py:28
  6.0 1.3 %collective-permute-start.1 = (f32[8,8,112]{2,0,1:T(8,128)S(1)}, f32[8,8,112]{2,0,1:T(8,128)S(1)}, u32[]{:S(2)}, u32[]{:S(2)}) collective-permute-start(f32[8,8,112]{2,0,1:T(8,128)S(1)} %copy.61), channel_id=1, source_target_pairs={{1,0},{2,1},{3,2},{4,3},{5,4},{6,5},{7,6},{8,7},{9,8},{10,9},{11,1... | collective-permute-start | bytes 86024 | tf_op jit(solution)/shard_map/ppermute | solution.py:29
  7.4 0.7 broadcast_compare_fusion.10
  8.0 0.7 broadcast_compare_fusion.1
  8.7 0.7 convert_element_type.4
  9.8 0.9 reshape.103
  11.6 0.7 broadcast_in_dim_reshape.7.tl_ref
  12.4 0.7 fusion.43
  13.1 5.0 %collective-permute-start.5 = (f32[4,8,256]{2,1,0:T(8,128)S(1)}, f32[4,8,256]{2,1,0:T(8,128)S(1)}, u32[]{:S(2)}, u32[]{:S(2)}) collective-permute-start(f32[4,8,256]{2,1,0:T(8,128)S(1)} %pad_maximum_fusion.1), channel_id=1, source_target_pairs={{0,4},{1,5},{2,6},{3,7},{4,0},{5,1},{6,2},{7,3},{8,12},{9,13},{10,... | collective-permute-start | bytes 98312 | tf_op jit(solution)/shard_map/ppermute | solution.py:56
  18.1 2.6 %collective-permute-start.6 = (f32[4,8,256]{2,1,0:T(8,128)S(1)}, f32[4,8,256]{2,1,0:T(8,128)S(1)}, u32[]{:S(2)}, u32[]{:S(2)}) collective-permute-start(f32[4,8,256]{2,1,0:T(8,128)S(1)} %pad_maximum_fusion.1), channel_id=1, source_target_pairs={{0,8},{1,9},{2,10},{3,11},{4,12},{5,13},{6,14},{7,15},{8,0},{9,1},... | collective-permute-start | bytes 98312 | tf_op jit(solution)/shard_map/ppermute | solution.py:56
  21.5 0.9 slice_bitcast_fusion.p_ref
  22.4 6.6 %shard_map.55 = f32[7,8,31,512]{3,2,1,0:T(8,128)} custom-call(f32[24,31,128]{2,1,0:T(8,128)} %slice_bitcast_fusion.p_ref), custom_call_target="tpu_custom_call" | custom-call | bytes 3555328 | tf_op jit(solution)/shard_map/pallas_call | solution.py:115
  29.5 1.1 %copy.99.energy_ref = f32[16,56,128]{2,1,0:T(8,128)} copy(f32[16,56,128]{1,2,0:T(8,128)S(1)} %bitcast.77) | data formatting | bytes 917504 | tf_op jit(solution)/shard_map/tile | solution.py:188
  32.7 0.9 select_add_fusion
  35.1 0.7 copy.79
  36.3 1.3 %bitcast_add_fusion.3 = f32[8,16,16,16]{1,3,2,0:T(8,128)} fusion(f32[8,16,16,16]{2,3,1,0:T(8,128)S(1)} %broadcast_select_fusion.1, f32[8,16,16,16]{1,2,3,0:T(8,128)S(1)} %copy.81, f32[8,16,16,16]{1,3,2,0:T(8,128)S(1)} %copy.79, pred[8]{0:T(512)(128)(4,1)S(1)} %get-tuple-element.47, pred[8]{0:T(512)(128)(4,1)S(1)} %get-tuple-element.46, ...), kind=kLoop, calls=%fused_computation.23 | loop fusion | flops 163840 | bytes 524312 | tf_op jit(solution)/shard_map/add | solution.py:83
  37.6 1.5 %copy.84 = f32[8,16,16,16]{3,1,2,0:T(8,128)S(1)} copy(f32[8,16,16,16]{1,3,2,0:T(8,128)} %bitcast_add_fusion.3) | data formatting | bytes 262144 | tf_op jit(solution)/shard_map/add | solution.py:83
  41.5 2.8 %fusion.1 = f32[128,32,256]{2,0,1:T(8,128)S(1)} fusion(f32[128,256,1]{0,1,2:T(8,128)S(1)} %reshape.117, s32[256]{0:T(256)S(1)} %get-tuple-element.52, s32[256]{0:T(256)S(1)} %get-tuple-element.55, s32[256]{0:T(256)S(1)} %get-tuple-element.53, s32[256]{0:T(256)S(1)} %get-tuple-element.54, pred[256]{0:T(512)(128)(4,1)S(1)} %get-tuple-element.50, ...), kind=kOutput, calls=%fused_computation.3 | convolution fusion | flops 3238002688 | bytes 4329984 | tf_op jit(solution)/shard_map/rk,wkn->rwn/dot_general | solution.py:100
  44.4 2.4 %copy.90 = f32[128,32,256]{2,1,0:T(8,128)S(1)} copy(f32[128,32,256]{2,0,1:T(8,128)S(1)} %fusion.1) | data formatting | bytes 8388608 | tf_op jit(solution)/shard_map/rk,wkn->rwn/dot_general | solution.py:100
  46.8 39.7 %fusion.15 = f32[1,17,56,256]{3,0,2,1:T(1,128)S(1)} fusion(f32[8,1,512,256]{3,2,1,0:T(8,128)S(1)} %bitcast.76, f32[1,56,31,512]{3,2,1,0:T(8,128)S(1)} %bitcast.79), kind=kOutput, calls=%fused_computation.16 | convolution fusion | flops 5989466112 | bytes 8724480 | tf_op jit(solution)/shard_map/conv_general_dilated | solution.py:170
  86.5 1.0 %copy.117 = f32[1,17,56,256]{3,2,0,1:T(8,128)} copy(f32[1,17,56,256]{3,0,2,1:T(1,128)S(1)} %fusion.15) | data formatting | bytes 1949696
  87.5 3.4 %shard_map.56 = f32[4,16,896]{2,1,0:T(8,128)} custom-call(f32[17,56,256]{2,1,0:T(8,128)} %bitcast.78, f32[16,56,128]{2,1,0:T(8,128)} %copy.99.energy_ref, f32[1,1,128]{2,1,0:T(1,128)} %broadcast_in_dim_reshape.6.wl_ref, f32[1,1,64]{2,1,0:T(1,128)} %broadcast_in_dim_reshape.7.tl_ref), custom_call_target="tpu_custom_call" | custom-call | tf_op jit(solution)/shard_map/pallas_call | solution.py:144
  (79 shorter events, 9.5 us)
Async XLA Ops:
  0.0 12.3 %collective-permute-start.2 = (f32[1,8,256]{2,1,0:T(8,128)}, f32[1,8,256]{2,1,0:T(8,128)S(1)}, u32[]{:S(2)}, u32[]{:S(2)}) collective-permute-start(f32[1,8,256]{2,1,0:T(8,128)} %bitcast.84), channel_id=1, source_target_pairs={{0,1},{1,0},{2,3},{3,2},{4,5},{5,4},{6,7},{7,6},{8,9},{9,8},{10,11... | collective-permute-start | bytes 24584 | tf_op jit(solution)/shard_map/ppermute | solution.py:56
  0.5 11.9 %collective-permute-start.3 = (f32[1,8,256]{2,1,0:T(8,128)}, f32[1,8,256]{2,1,0:T(8,128)S(1)}, u32[]{:S(2)}, u32[]{:S(2)}) collective-permute-start(f32[1,8,256]{2,1,0:T(8,128)} %bitcast.85), channel_id=1, source_target_pairs={{0,2},{1,3},{2,0},{3,1},{4,6},{5,7},{6,4},{7,5},{8,10},{9,11},{10,... | collective-permute-start | bytes 24584 | tf_op jit(solution)/shard_map/ppermute | solution.py:56
  2.9 9.4 %collective-permute-start.4 = (f32[1,8,256]{2,1,0:T(8,128)}, f32[1,8,256]{2,1,0:T(8,128)S(1)}, u32[]{:S(2)}, u32[]{:S(2)}) collective-permute-start(f32[1,8,256]{2,1,0:T(8,128)} %bitcast.86), channel_id=1, source_target_pairs={{0,3},{1,2},{2,1},{3,0},{4,7},{5,6},{6,5},{7,4},{8,11},{9,10},{10,... | collective-permute-start | bytes 24584 | tf_op jit(solution)/shard_map/ppermute | solution.py:56
  3.9 16.8 %collective-permute-start = (f32[8,8,112]{2,0,1:T(8,128)S(1)}, f32[8,8,112]{2,0,1:T(8,128)S(1)}, u32[]{:S(2)}, u32[]{:S(2)}) collective-permute-start(f32[8,8,112]{2,0,1:T(8,128)S(1)} %copy.60), channel_id=1, source_target_pairs={{0,1},{1,2},{2,3},{3,4},{4,5},{5,6},{6,7},{7,8},{8,9},{9,10},{10,1... | collective-permute-start | bytes 86024 | tf_op jit(solution)/shard_map/ppermute | solution.py:28
  6.0 14.7 %collective-permute-start.1 = (f32[8,8,112]{2,0,1:T(8,128)S(1)}, f32[8,8,112]{2,0,1:T(8,128)S(1)}, u32[]{:S(2)}, u32[]{:S(2)}) collective-permute-start(f32[8,8,112]{2,0,1:T(8,128)S(1)} %copy.61), channel_id=1, source_target_pairs={{1,0},{2,1},{3,2},{4,3},{5,4},{6,5},{7,6},{8,7},{9,8},{10,9},{11,1... | collective-permute-start | bytes 86024 | tf_op jit(solution)/shard_map/ppermute | solution.py:29
  13.1 17.6 %collective-permute-start.5 = (f32[4,8,256]{2,1,0:T(8,128)S(1)}, f32[4,8,256]{2,1,0:T(8,128)S(1)}, u32[]{:S(2)}, u32[]{:S(2)}) collective-permute-start(f32[4,8,256]{2,1,0:T(8,128)S(1)} %pad_maximum_fusion.1), channel_id=1, source_target_pairs={{0,4},{1,5},{2,6},{3,7},{4,0},{5,1},{6,2},{7,3},{8,12},{9,13},{10,... | collective-permute-start | bytes 98312 | tf_op jit(solution)/shard_map/ppermute | solution.py:56
  18.1 12.5 %collective-permute-start.6 = (f32[4,8,256]{2,1,0:T(8,128)S(1)}, f32[4,8,256]{2,1,0:T(8,128)S(1)}, u32[]{:S(2)}, u32[]{:S(2)}) collective-permute-start(f32[4,8,256]{2,1,0:T(8,128)S(1)} %pad_maximum_fusion.1), channel_id=1, source_target_pairs={{0,8},{1,9},{2,10},{3,11},{4,12},{5,13},{6,14},{7,15},{8,0},{9,1},... | collective-permute-start | bytes 98312 | tf_op jit(solution)/shard_map/ppermute | solution.py:56
  20.7 9.9 %collective-permute-start.7 = (f32[4,8,256]{2,1,0:T(8,128)S(1)}, f32[4,8,256]{2,1,0:T(8,128)S(1)}, u32[]{:S(2)}, u32[]{:S(2)}) collective-permute-start(f32[4,8,256]{2,1,0:T(8,128)S(1)} %pad_maximum_fusion.1), channel_id=1, source_target_pairs={{0,12},{1,13},{2,14},{3,15},{4,8},{5,9},{6,10},{7,11},{8,4},{9,5},... | collective-permute-start | bytes 98312 | tf_op jit(solution)/shard_map/ppermute | solution.py:56
  44.3 2.4 %copy-start = (f32[7,8,31,512]{3,2,1,0:T(8,128)S(1)}, f32[7,8,31,512]{3,2,1,0:T(8,128)}, u32[]{:S(2)}) copy-start(f32[7,8,31,512]{3,2,1,0:T(8,128)} %shard_map.55) | copy-start | bytes 10665988

commit v9 on v8

--- a/solution.py
+++ b/solution.py
@@ -125,19 +125,19 @@
     rows = o_ref.shape[1]
     lanes = wl_ref.shape[-1]
     half_lanes = tl_ref.shape[-1]
-    numer = both_ref[0:rows, :, 0:lanes] + both_ref[1:rows + 1, :, lanes:2 * lanes]
+    numer = both_ref[0:rows, :, :, 0:lanes] + both_ref[1:rows + 1, :, :, lanes:2 * lanes]
     scores = numer / jnp.sqrt(energy_ref[...] + epsilon)
     weighted = wl_ref[...] * jnp.exp(sharpness * scores)
-    grouped = weighted[:, :, 0:half_lanes]
+    grouped = weighted[..., 0:half_lanes]
     for p in range(1, lanes // half_lanes):
-        grouped = grouped + weighted[:, :, p * half_lanes:(p + 1) * half_lanes]
+        grouped = grouped + weighted[..., p * half_lanes:(p + 1) * half_lanes]
     fields_ref[...] = jnp.log(grouped / tl_ref[...])
-    blocks = both_ref.shape[1] // BY
+    blocks = both_ref.shape[2]
     for k in range(o_ref.shape[0]):
         for zb in range(blocks):
             for y in range(BY):
                 at = y * BZ + zb * ZB
-                o_ref[k, :, at:at + ZB] = fields_ref[:, zb * BY + y, k * ZB:(k + 1) * ZB]
+                o_ref[k, :, at:at + ZB] = fields_ref[:, y, zb, k * ZB:(k + 1) * ZB]
 
 
 def post(both, energy, wl, tl, rows_x):
@@ -146,7 +146,7 @@
         out_shape=jax.ShapeDtypeStruct((FIELDS, rows_x, BY * BZ), jnp.float32),
         in_specs=[pl.BlockSpec(memory_space=pltpu.VMEM)] * 4,
         out_specs=pl.BlockSpec(memory_space=pltpu.VMEM),
-        scratch_shapes=[pltpu.VMEM((rows_x, both.shape[1], tl.shape[-1]), jnp.float32)],
+        scratch_shapes=[pltpu.VMEM((rows_x, both.shape[1], both.shape[2], tl.shape[-1]), jnp.float32)],
     )(both, energy, wl, tl)
 
 
@@ -166,10 +166,10 @@
     field_in = extended(grid, (("gx", 0),), half)
     padded = jnp.pad(field_in, ((0, 0), (half, TS - half), (half, TS - half)))
     cols = im2col(jnp.transpose(padded[: len_x - 1], (1, 0, 2)), blocks)
-    cols = cols.reshape(1, blocks * BY, len_x - 1, TS * (TS + ZB))
+
     both = lax.conv_general_dilated(
         cols, rhs, (1, 1), "VALID", rhs_dilation=(2, 1),
-        dimension_numbers=lax.ConvDimensionNumbers((0, 3, 2, 1), (3, 2, 0, 1), (0, 3, 1, 2)),
+        dimension_numbers=lax.ConvDimensionNumbers((0, 3, 2, 1), (3, 2, 0, 1), (2, 3, 0, 1)),
         precision=lax.Precision.HIGH,
     )
     pos_x = jnp.arange(len_x, dtype=jnp.int32)
@@ -184,15 +184,14 @@
         "xyn,ym->xmn", energy, band_table(pos_y, jnp.arange(BY, dtype=jnp.int32), len_y)
     )
     energy = contract("xmn,xl->lmn", energy, band_table(pos_x, out_x, len_x))
-    energy = jnp.transpose(energy.reshape(rows_x, BY, blocks, ZB), (0, 2, 1, 3))
-    energy = jnp.tile(energy.reshape(rows_x, blocks * BY, ZB), (1, 1, nt))
+    energy = jnp.tile(energy.reshape(rows_x, BY, blocks, ZB), (1, 1, 1, nt))
     weights = jnp.transpose(counts.astype(jnp.float32).reshape(FIELDS, per)).reshape(nt)
     totals = weights[:FIELDS]
     for p in range(1, per):
         totals = totals + weights[p * FIELDS:(p + 1) * FIELDS]
-    wl = jnp.repeat(weights, ZB)[None, None]
-    tl = jnp.repeat(totals, ZB)[None, None]
-    return post(both[0], energy, wl, tl, rows_x)
+    wl = jnp.repeat(weights, ZB)[None, None, None]
+    tl = jnp.repeat(totals, ZB)[None, None, None]
+    return post(both, energy, wl, tl, rows_x)
 
 
 def solution(mesh):

time: 91.3 us -> 69.5 us (0.76)
  matrix products: 43.3 us -> 17.8 us
  local copies, waits for them, and re-layouts: 15.7 us -> 19.3 us
    conv_general_dilated x1, matrix products: 39.7 us -> 14.2 us  [local(): lax.conv_general_dilated(cols, rhs, (1, 1), 'VALID', rhs_dilation=(2, 1),...]
    another operation x5 -> x7, local copies, waits for them, and re-layouts: 2.64 us -> 7.52 us  [the longest x5 6.24 us: local(): energy = jnp.tile(energy.reshape(rows_x, BY, blocks, ZB), (1, 1, 1, nt))]
    unnamed x5 -> x4, local copies, waits for them, and re-layouts: 1.05 us -> 0.02 us
  transfers between devices with their start and end apart: 8 -> 8, of which waited for: 0 -> 0; matrix products, arithmetic and copies ran while one was open for 11% -> 21% of each run, Pallas kernels for 7% -> 10%
where the time goes in v9:
time: 69.5 us; the launch traced here: 69.1 us
  local copies, waits for them, and re-layouts  19.3 us (28%)
  matrix products  17.8 us (26%)
  starting transfers between devices  14 us (20%)
  Pallas kernels  10.1 us (15%)
  other arithmetic  7.36 us (11%)
    conv_general_dilated x1, matrix products, local(): lax.conv_general_dilated(cols, rhs, (1, 1), 'VALID', rhs_dilation=(2, 1),...  14.2 us
    ppermute x6, starting transfers between devices, gather_planes(): lax.ppermute(held, axis, [(i, i ^ s * step) for i in range(size)])  10.7 us
    pallas_call x1, Pallas kernels, im2col(): pl.pallas_call(im2col_kernel, out_shape=jax.ShapeDtypeStruct((blocks, BY,...  6.61 us
    another operation x5, local copies, waits for them, and re-layouts, local(): energy = jnp.tile(energy.reshape(rows_x, BY, blocks, ZB), (1, 1, 1, nt))  6.24 us
    pallas_call x1, Pallas kernels, post(): pl.pallas_call(post_kernel, out_shape=jax.ShapeDtypeStruct((FIELDS, rows_...  3.47 us
    dot_general x1, matrix products, toeplitz_rhs(): rhs = jnp.einsum('rk,wkn->rwn', kt, shift, precision=lax.Precision.HIGHEST)  2.85 us
    dot_general x1, local copies, waits for them, and re-layouts, toeplitz_rhs(): rhs = jnp.einsum('rk,wkn->rwn', kt, shift, precision=lax.Precision.HIGHEST)  2.43 us
    ppermute x1, starting transfers between devices, extended(): before = lax.ppermute(last, axis, up)  1.99 us
  transfers between devices with their start and end apart: 8, of which 0 were waited for; matrix products, arithmetic and copies ran while one was open for 21% of the time, Pallas kernels for 10%

profile of v9, /device:TPU:0, one launch (start us, length us, event | category | flops | bytes accessed | tf_op | source)
XLA Modules:
  0.0 69.1 jit_solution(4141464086104102477)
XLA Ops:
  0.5 2.5 %collective-permute-start.3 = (f32[1,8,256]{2,1,0:T(8,128)}, f32[1,8,256]{2,1,0:T(8,128)S(1)}, u32[]{:S(2)}, u32[]{:S(2)}) collective-permute-start(f32[1,8,256]{2,1,0:T(8,128)} %bitcast.77), channel_id=1, source_target_pairs={{0,2},{1,3},{2,0},{3,1},{4,6},{5,7},{6,4},{7,5},{8,10},{9,11},{10,... | collective-permute-start | bytes 24584 | tf_op jit(solution)/shard_map/ppermute | solution.py:56
  3.1 0.8 %fusion.82 = (f32[8,896]{1,0:T(8,128)S(1)}, f32[8,896]{1,0:T(8,128)S(1)}) fusion(f32[16,896]{1,0:T(8,128)} %param.5), kind=kLoop, calls=%fused_computation.167 | loop fusion | bytes 114688 | tf_op jit(solution)/shard_map/slice | solution.py:27
  3.9 2.0 %collective-permute-start = (f32[8,8,112]{2,0,1:T(8,128)S(1)}, f32[8,8,112]{2,0,1:T(8,128)S(1)}, u32[]{:S(2)}, u32[]{:S(2)}) collective-permute-start(f32[8,8,112]{2,0,1:T(8,128)S(1)} %copy.60), channel_id=1, source_target_pairs={{0,1},{1,2},{2,3},{3,4},{4,5},{5,6},{6,7},{7,8},{8,9},{9,10},{10,1... | collective-permute-start | bytes 86024 | tf_op jit(solution)/shard_map/ppermute | solution.py:28
  6.0 1.3 %collective-permute-start.1 = (f32[8,8,112]{2,0,1:T(8,128)S(1)}, f32[8,8,112]{2,0,1:T(8,128)S(1)}, u32[]{:S(2)}, u32[]{:S(2)}) collective-permute-start(f32[8,8,112]{2,0,1:T(8,128)S(1)} %copy.61), channel_id=1, source_target_pairs={{1,0},{2,1},{3,2},{4,3},{5,4},{6,5},{7,6},{8,7},{9,8},{10,9},{11,1... | collective-permute-start | bytes 86024 | tf_op jit(solution)/shard_map/ppermute | solution.py:29
  7.4 0.7 broadcast_compare_fusion.10
  8.0 0.7 broadcast_compare_fusion.1
  9.8 0.9 %reshape.97 = f32[16,8,112]{2,1,0:T(8,128)S(1)} reshape(f32[16,896]{1,0:T(8,128)} %param.5) | data formatting | bytes 114688 | tf_op jit(solution)/shard_map/reshape | solution.py:157
  11.0 0.7 broadcast_in_dim_reshape.6.wl_ref
  12.3 0.7 %fusion.43 = (f32[1,8,256]{2,1,0:T(8,128)S(1)}, f32[1,8,256]{2,1,0:T(8,128)S(1)}, f32[1,8,256]{2,1,0:T(8,128)S(1)}) fusion(f32[1,8,256]{2,1,0:T(8,128)S(1)} %collective-permute-done.4, f32[1,8,256]{2,1,0:T(8,128)S(1)} %collective-permute-done.3, f32[1,8,256]{2,1,0:T(8,128)S(1)} %collective-permute-done.2, f32[8,256]{1,0:T(8,128)} %param.6, pred[]{:T(512)S(6)} %eq.179, ...), kind=kLoop, calls=%fused_computation.83 | loop fusion | flops 43008 | bytes 57356 | tf_op jit(solution)/shard_map/add | solution.py:62
  13.1 5.0 %collective-permute-start.5 = (f32[4,8,256]{2,1,0:T(8,128)S(1)}, f32[4,8,256]{2,1,0:T(8,128)S(1)}, u32[]{:S(2)}, u32[]{:S(2)}) collective-permute-start(f32[4,8,256]{2,1,0:T(8,128)S(1)} %pad_maximum_fusion.1), channel_id=1, source_target_pairs={{0,4},{1,5},{2,6},{3,7},{4,0},{5,1},{6,2},{7,3},{8,12},{9,13},{10,... | collective-permute-start | bytes 98312 | tf_op jit(solution)/shard_map/ppermute | solution.py:56
  18.1 2.6 %collective-permute-start.6 = (f32[4,8,256]{2,1,0:T(8,128)S(1)}, f32[4,8,256]{2,1,0:T(8,128)S(1)}, u32[]{:S(2)}, u32[]{:S(2)}) collective-permute-start(f32[4,8,256]{2,1,0:T(8,128)S(1)} %pad_maximum_fusion.1), channel_id=1, source_target_pairs={{0,8},{1,9},{2,10},{3,11},{4,12},{5,13},{6,14},{7,15},{8,0},{9,1},... | collective-permute-start | bytes 98312 | tf_op jit(solution)/shard_map/ppermute | solution.py:56
  21.5 0.9 %slice_bitcast_fusion.p_ref = f32[24,31,128]{2,1,0:T(8,128)} fusion(f32[32,8,112]{2,0,1:T(8,128)S(1)} %constant_dynamic-update-slice_fusion), kind=kLoop, calls=%fused_computation.30 | loop fusion | bytes 495616 | tf_op jit(solution)/shard_map/transpose | solution.py:168
  22.4 6.6 %shard_map.55 = f32[7,8,31,512]{3,2,1,0:T(8,128)} custom-call(f32[24,31,128]{2,1,0:T(8,128)} %slice_bitcast_fusion.p_ref), custom_call_target="tpu_custom_call" | custom-call | bytes 3555328 | tf_op jit(solution)/shard_map/pallas_call | solution.py:115
  29.4 2.3 %tile.11 = f32[16,8,7,8,16]{4,3,1,2,0:T(8,128)} broadcast(f32[16,8,7,16]{3,1,2,0:T(8,128)S(1)} %copy.96), dimensions={0,1,2,4} | broadcast | bytes 516096 | tf_op jit(solution)/shard_map/tile | solution.py:187
  31.8 2.5 %tile.12 = f32[16,8,7,128]{3,1,2,0:T(8,128)S(1)} reshape(f32[16,8,7,8,16]{4,3,1,2,0:T(8,128)} %tile.11) | data formatting | bytes 917504 | tf_op jit(solution)/shard_map/tile | solution.py:187
  34.3 0.9 %copy.98.energy_ref = f32[16,8,7,128]{3,2,1,0:T(8,128)} copy(f32[16,8,7,128]{3,1,2,0:T(8,128)S(1)} %tile.12) | data formatting | bytes 917504 | tf_op jit(solution)/shard_map/tile | solution.py:187
  37.3 0.9 %select_add_fusion = f32[8,16,16,16]{2,3,1,0:T(8,128)S(1)} fusion(f32[16,16,16]{1,2,0:T(8,128)S(1)} %copy.77, f32[16,16,16]{1,2,0:T(8,128)S(1)} %copy.75, f32[16,16,16]{1,2,0:T(8,128)S(1)} %copy.73, f32[16,16,16]{1,2,0:T(8,128)S(1)} %copy.71, f32[16,16,16]{1,2,0:T(8,128)S(1)} %copy.69, f32[16,16,16]{1,2,0:T(8,128)S(1)} %copy.67, f32[16,16,16]{1,2,0:T(8,128)S(1)} %copy.65, ...), kind=kLoop, calls=%fused_computation.27 | loop fusion | flops 491520 | bytes 262208 | tf_op jit(solution)/shard_map/add | solution.py:74
  39.8 0.7 copy.79
  40.9 1.3 %bitcast_add_fusion.3 = f32[8,16,16,16]{1,3,2,0:T(8,128)} fusion(f32[8,16,16,16]{2,3,1,0:T(8,128)S(1)} %broadcast_select_fusion.1, f32[8,16,16,16]{1,2,3,0:T(8,128)S(1)} %copy.81, f32[8,16,16,16]{1,3,2,0:T(8,128)S(1)} %copy.79, pred[8]{0:T(512)(128)(4,1)S(1)} %get-tuple-element.47, pred[8]{0:T(512)(128)(4,1)S(1)} %get-tuple-element.46, ...), kind=kLoop, calls=%fused_computation.23 | loop fusion | flops 163840 | bytes 524312 | tf_op jit(solution)/shard_map/add | solution.py:83
  42.2 1.5 %copy.84 = f32[8,16,16,16]{3,1,2,0:T(8,128)S(1)} copy(f32[8,16,16,16]{1,3,2,0:T(8,128)} %bitcast_add_fusion.3) | data formatting | bytes 262144 | tf_op jit(solution)/shard_map/add | solution.py:83
  46.1 2.9 %fusion.1 = f32[128,32,256]{2,0,1:T(8,128)S(1)} fusion(f32[128,256,1]{0,1,2:T(8,128)S(1)} %reshape.109, s32[256]{0:T(256)S(1)} %get-tuple-element.52, s32[256]{0:T(256)S(1)} %get-tuple-element.55, s32[256]{0:T(256)S(1)} %get-tuple-element.53, s32[256]{0:T(256)S(1)} %get-tuple-element.54, pred[256]{0:T(512)(128)(4,1)S(1)} %get-tuple-element.50, ...), kind=kOutput, calls=%fused_computation.3 | convolution fusion | flops 3238002688 | bytes 4329984 | tf_op jit(solution)/shard_map/rk,wkn->rwn/dot_general | solution.py:100
  49.0 2.4 %copy.90 = f32[128,32,256]{2,1,0:T(8,128)S(1)} copy(f32[128,32,256]{2,0,1:T(8,128)S(1)} %fusion.1) | data formatting | bytes 8388608 | tf_op jit(solution)/shard_map/rk,wkn->rwn/dot_general | solution.py:100
  51.4 14.2 %fusion.15.both_ref = f32[17,8,7,256]{3,2,1,0:T(8,128)} fusion(f32[8,1,512,256]{3,2,1,0:T(8,128)S(1)} %bitcast.72, f32[7,8,31,512]{3,2,1,0:T(8,128)S(1)} %copy-done), kind=kOutput, calls=%fused_computation.16 | convolution fusion | flops 5989466112 | bytes 8724480 | tf_op jit(solution)/shard_map/conv_general_dilated | solution.py:170
  65.6 3.5 %shard_map.56 = f32[4,16,896]{2,1,0:T(8,128)} custom-call(f32[17,8,7,256]{3,2,1,0:T(8,128)} %fusion.15.both_ref, f32[16,8,7,128]{3,2,1,0:T(8,128)} %copy.98.energy_ref, f32[1,1,1,128]{3,2,1,0:T(1,128)} %broadcast_in_dim_reshape.6.wl_ref, f32[1,1,1,64]{3,2,1,0:T(1,128)} %broadcast_in_dim_reshape.7.tl_ref), custom_call_target="tpu_custom_call" | custom-call | tf_op jit(solution)/shard_map/pallas_call | solution.py:144
  (77 shorter events, 10.1 us)
Async XLA Ops:
  0.0 12.3 %collective-permute-start.2 = (f32[1,8,256]{2,1,0:T(8,128)}, f32[1,8,256]{2,1,0:T(8,128)S(1)}, u32[]{:S(2)}, u32[]{:S(2)}) collective-permute-start(f32[1,8,256]{2,1,0:T(8,128)} %bitcast.76), channel_id=1, source_target_pairs={{0,1},{1,0},{2,3},{3,2},{4,5},{5,4},{6,7},{7,6},{8,9},{9,8},{10,11... | collective-permute-start | bytes 24584 | tf_op jit(solution)/shard_map/ppermute | solution.py:56
  0.5 11.9 %collective-permute-start.3 = (f32[1,8,256]{2,1,0:T(8,128)}, f32[1,8,256]{2,1,0:T(8,128)S(1)}, u32[]{:S(2)}, u32[]{:S(2)}) collective-permute-start(f32[1,8,256]{2,1,0:T(8,128)} %bitcast.77), channel_id=1, source_target_pairs={{0,2},{1,3},{2,0},{3,1},{4,6},{5,7},{6,4},{7,5},{8,10},{9,11},{10,... | collective-permute-start | bytes 24584 | tf_op jit(solution)/shard_map/ppermute | solution.py:56
  2.9 9.4 %collective-permute-start.4 = (f32[1,8,256]{2,1,0:T(8,128)}, f32[1,8,256]{2,1,0:T(8,128)S(1)}, u32[]{:S(2)}, u32[]{:S(2)}) collective-permute-start(f32[1,8,256]{2,1,0:T(8,128)} %bitcast.78), channel_id=1, source_target_pairs={{0,3},{1,2},{2,1},{3,0},{4,7},{5,6},{6,5},{7,4},{8,11},{9,10},{10,... | collective-permute-start | bytes 24584 | tf_op jit(solution)/shard_map/ppermute | solution.py:56
  3.9 16.8 %collective-permute-start = (f32[8,8,112]{2,0,1:T(8,128)S(1)}, f32[8,8,112]{2,0,1:T(8,128)S(1)}, u32[]{:S(2)}, u32[]{:S(2)}) collective-permute-start(f32[8,8,112]{2,0,1:T(8,128)S(1)} %copy.60), channel_id=1, source_target_pairs={{0,1},{1,2},{2,3},{3,4},{4,5},{5,6},{6,7},{7,8},{8,9},{9,10},{10,1... | collective-permute-start | bytes 86024 | tf_op jit(solution)/shard_map/ppermute | solution.py:28
  6.0 14.7 %collective-permute-start.1 = (f32[8,8,112]{2,0,1:T(8,128)S(1)}, f32[8,8,112]{2,0,1:T(8,128)S(1)}, u32[]{:S(2)}, u32[]{:S(2)}) collective-permute-start(f32[8,8,112]{2,0,1:T(8,128)S(1)} %copy.61), channel_id=1, source_target_pairs={{1,0},{2,1},{3,2},{4,3},{5,4},{6,5},{7,6},{8,7},{9,8},{10,9},{11,1... | collective-permute-start | bytes 86024 | tf_op jit(solution)/shard_map/ppermute | solution.py:29
  13.1 22.2 %collective-permute-start.5 = (f32[4,8,256]{2,1,0:T(8,128)S(1)}, f32[4,8,256]{2,1,0:T(8,128)S(1)}, u32[]{:S(2)}, u32[]{:S(2)}) collective-permute-start(f32[4,8,256]{2,1,0:T(8,128)S(1)} %pad_maximum_fusion.1), channel_id=1, source_target_pairs={{0,4},{1,5},{2,6},{3,7},{4,0},{5,1},{6,2},{7,3},{8,12},{9,13},{10,... | collective-permute-start | bytes 98312 | tf_op jit(solution)/shard_map/ppermute | solution.py:56
  18.1 17.1 %collective-permute-start.6 = (f32[4,8,256]{2,1,0:T(8,128)S(1)}, f32[4,8,256]{2,1,0:T(8,128)S(1)}, u32[]{:S(2)}, u32[]{:S(2)}) collective-permute-start(f32[4,8,256]{2,1,0:T(8,128)S(1)} %pad_maximum_fusion.1), channel_id=1, source_target_pairs={{0,8},{1,9},{2,10},{3,11},{4,12},{5,13},{6,14},{7,15},{8,0},{9,1},... | collective-permute-start | bytes 98312 | tf_op jit(solution)/shard_map/ppermute | solution.py:56
  20.7 14.5 %collective-permute-start.7 = (f32[4,8,256]{2,1,0:T(8,128)S(1)}, f32[4,8,256]{2,1,0:T(8,128)S(1)}, u32[]{:S(2)}, u32[]{:S(2)}) collective-permute-start(f32[4,8,256]{2,1,0:T(8,128)S(1)} %pad_maximum_fusion.1), channel_id=1, source_target_pairs={{0,12},{1,13},{2,14},{3,15},{4,8},{5,9},{6,10},{7,11},{8,4},{9,5},... | collective-permute-start | bytes 98312 | tf_op jit(solution)/shard_map/ppermute | solution.py:56
  48.9 2.4 %copy-start = (f32[7,8,31,512]{3,2,1,0:T(8,128)S(1)}, f32[7,8,31,512]{3,2,1,0:T(8,128)}, u32[]{:S(2)}) copy-start(f32[7,8,31,512]{3,2,1,0:T(8,128)} %shard_map.55) | copy-start | bytes 10665988

commit v10 on v8

--- a/solution.py
+++ b/solution.py
@@ -125,14 +125,15 @@
     rows = o_ref.shape[1]
     lanes = wl_ref.shape[-1]
     half_lanes = tl_ref.shape[-1]
-    numer = both_ref[0:rows, :, 0:lanes] + both_ref[1:rows + 1, :, lanes:2 * lanes]
+    numer = both_ref[0:rows, :, :, 0:lanes] + both_ref[1:rows + 1, :, :, lanes:2 * lanes]
+    numer = numer.reshape(rows, -1, lanes)
     scores = numer / jnp.sqrt(energy_ref[...] + epsilon)
     weighted = wl_ref[...] * jnp.exp(sharpness * scores)
     grouped = weighted[:, :, 0:half_lanes]
     for p in range(1, lanes // half_lanes):
         grouped = grouped + weighted[:, :, p * half_lanes:(p + 1) * half_lanes]
     fields_ref[...] = jnp.log(grouped / tl_ref[...])
-    blocks = both_ref.shape[1] // BY
+    blocks = both_ref.shape[1]
     for k in range(o_ref.shape[0]):
         for zb in range(blocks):
             for y in range(BY):
@@ -146,7 +147,7 @@
         out_shape=jax.ShapeDtypeStruct((FIELDS, rows_x, BY * BZ), jnp.float32),
         in_specs=[pl.BlockSpec(memory_space=pltpu.VMEM)] * 4,
         out_specs=pl.BlockSpec(memory_space=pltpu.VMEM),
-        scratch_shapes=[pltpu.VMEM((rows_x, both.shape[1], tl.shape[-1]), jnp.float32)],
+        scratch_shapes=[pltpu.VMEM((rows_x, both.shape[1] * both.shape[2], tl.shape[-1]), jnp.float32)],
     )(both, energy, wl, tl)
 
 
@@ -166,10 +167,10 @@
     field_in = extended(grid, (("gx", 0),), half)
     padded = jnp.pad(field_in, ((0, 0), (half, TS - half), (half, TS - half)))
     cols = im2col(jnp.transpose(padded[: len_x - 1], (1, 0, 2)), blocks)
-    cols = cols.reshape(1, blocks * BY, len_x - 1, TS * (TS + ZB))
+
     both = lax.conv_general_dilated(
         cols, rhs, (1, 1), "VALID", rhs_dilation=(2, 1),
-        dimension_numbers=lax.ConvDimensionNumbers((0, 3, 2, 1), (3, 2, 0, 1), (0, 3, 1, 2)),
+        dimension_numbers=lax.ConvDimensionNumbers((0, 3, 2, 1), (3, 2, 0, 1), (1, 3, 0, 2)),
         precision=lax.Precision.HIGH,
     )
     pos_x = jnp.arange(len_x, dtype=jnp.int32)
@@ -192,7 +193,7 @@
         totals = totals + weights[p * FIELDS:(p + 1) * FIELDS]
     wl = jnp.repeat(weights, ZB)[None, None]
     tl = jnp.repeat(totals, ZB)[None, None]
-    return post(both[0], energy, wl, tl, rows_x)
+    return post(both, energy, wl, tl, rows_x)
 
 
 def solution(mesh):

time: 91.3 us -> 66 us (0.72)
  matrix products: 43.3 us -> 17.7 us
    conv_general_dilated x1, matrix products: 39.7 us -> 14.1 us  [local(): lax.conv_general_dilated(cols, rhs, (1, 1), 'VALID', rhs_dilation=(2, 1),...]
    conv_general_dilated x0 -> x1, local copies, waits for them, and re-layouts: none -> 1.28 us  [local(): lax.conv_general_dilated(cols, rhs, (1, 1), 'VALID', rhs_dilation=(2, 1),...]
    unnamed x5 -> x4, local copies, waits for them, and re-layouts: 1.05 us -> 0.02 us
  transfers between devices with their start and end apart: 8 -> 8, of which waited for: 0 -> 0; matrix products, arithmetic and copies ran while one was open for 11% -> 15% of each run, Pallas kernels for 7% -> 10%
where the time goes in v10:
time: 66 us; the launch traced here: 65.6 us
  matrix products  17.7 us (27%)
  local copies, waits for them, and re-layouts  16 us (24%)
  starting transfers between devices  14 us (21%)
  Pallas kernels  9.96 us (15%)
  other arithmetic  7.36 us (11%)
    conv_general_dilated x1, matrix products, local(): lax.conv_general_dilated(cols, rhs, (1, 1), 'VALID', rhs_dilation=(2, 1),...  14.1 us
    ppermute x6, starting transfers between devices, gather_planes(): lax.ppermute(held, axis, [(i, i ^ s * step) for i in range(size)])  10.7 us
    pallas_call x1, Pallas kernels, im2col(): pl.pallas_call(im2col_kernel, out_shape=jax.ShapeDtypeStruct((blocks, BY,...  6.61 us
    pallas_call x1, Pallas kernels, post(): pl.pallas_call(post_kernel, out_shape=jax.ShapeDtypeStruct((FIELDS, rows_...  3.35 us
    dot_general x1, matrix products, toeplitz_rhs(): rhs = jnp.einsum('rk,wkn->rwn', kt, shift, precision=lax.Precision.HIGHEST)  2.85 us
    dot_general x1, local copies, waits for them, and re-layouts, toeplitz_rhs(): rhs = jnp.einsum('rk,wkn->rwn', kt, shift, precision=lax.Precision.HIGHEST)  2.43 us
    ppermute x1, starting transfers between devices, extended(): before = lax.ppermute(last, axis, up)  1.99 us
    add x2, other arithmetic, rotated_kernels(): rotated + jnp.where(expand(order_row == row), jnp.transpose(picked, perm)...  1.55 us
  transfers between devices with their start and end apart: 8, of which 0 were waited for; matrix products, arithmetic and copies ran while one was open for 15% of the time, Pallas kernels for 10%

profile of v10, /device:TPU:0, one launch (start us, length us, event | category | flops | bytes accessed | tf_op | source)
XLA Modules:
  0.0 65.6 jit_solution(13827410012166787275)
XLA Ops:
  0.5 2.5 %collective-permute-start.3 = (f32[1,8,256]{2,1,0:T(8,128)}, f32[1,8,256]{2,1,0:T(8,128)S(1)}, u32[]{:S(2)}, u32[]{:S(2)}) collective-permute-start(f32[1,8,256]{2,1,0:T(8,128)} %bitcast.79), channel_id=1, source_target_pairs={{0,2},{1,3},{2,0},{3,1},{4,6},{5,7},{6,4},{7,5},{8,10},{9,11},{10,... | collective-permute-start | bytes 24584 | tf_op jit(solution)/shard_map/ppermute | solution.py:56
  3.1 0.8 %fusion.82 = (f32[8,896]{1,0:T(8,128)S(1)}, f32[8,896]{1,0:T(8,128)S(1)}) fusion(f32[16,896]{1,0:T(8,128)} %param.5), kind=kLoop, calls=%fused_computation.168 | loop fusion | bytes 114688 | tf_op jit(solution)/shard_map/slice | solution.py:27
  3.9 2.0 %collective-permute-start = (f32[8,8,112]{2,0,1:T(8,128)S(1)}, f32[8,8,112]{2,0,1:T(8,128)S(1)}, u32[]{:S(2)}, u32[]{:S(2)}) collective-permute-start(f32[8,8,112]{2,0,1:T(8,128)S(1)} %copy.62), channel_id=1, source_target_pairs={{0,1},{1,2},{2,3},{3,4},{4,5},{5,6},{6,7},{7,8},{8,9},{9,10},{10,1... | collective-permute-start | bytes 86024 | tf_op jit(solution)/shard_map/ppermute | solution.py:28
  6.0 1.3 %collective-permute-start.1 = (f32[8,8,112]{2,0,1:T(8,128)S(1)}, f32[8,8,112]{2,0,1:T(8,128)S(1)}, u32[]{:S(2)}, u32[]{:S(2)}) collective-permute-start(f32[8,8,112]{2,0,1:T(8,128)S(1)} %copy.63), channel_id=1, source_target_pairs={{1,0},{2,1},{3,2},{4,3},{5,4},{6,5},{7,6},{8,7},{9,8},{10,9},{11,1... | collective-permute-start | bytes 86024 | tf_op jit(solution)/shard_map/ppermute | solution.py:29
  7.4 0.7 %broadcast_compare_fusion.10 = (pred[8]{0:T(512)(128)(4,1)S(1)}, pred[8]{0:T(512)(128)(4,1)S(1)}, pred[8]{0:T(512)(128)(4,1)S(1)}, pred[8]{0:T(512)(128)(4,1)S(1...) fusion(s32[8]{0:T(128)} %param.8), kind=kLoop, calls=%fused_computation.151 | loop fusion | flops 64 | bytes 96 | tf_op jit(solution)/shard_map/eq | solution.py:74
  8.0 0.7 %broadcast_compare_fusion.1 = (pred[8]{0:T(512)(128)(4,1)S(1)}, s32[8]{0:T(128)S(1)}, pred[8]{0:T(512)(128)(4,1)S(1)}, s32[8]{0:T(128)S(1)}) fusion(s32[8]{0:T(128)} %param.7), kind=kLoop, calls=%fused_computation.142 | loop fusion | flops 376 | bytes 112 | tf_op jit(solution)/shard_map/eq | solution.py:83
  8.7 0.7 %convert_element_type.4 = f32[8]{0:T(128)S(1)} convert(s32[8]{0:T(128)} %param.9) | non-fusion elementwise | flops 8 | bytes 64 | tf_op jit(solution)/shard_map/convert_element_type | solution.py:190
  9.8 0.9 %reshape.100 = f32[16,8,112]{2,1,0:T(8,128)S(1)} reshape(f32[16,896]{1,0:T(8,128)} %param.5) | data formatting | bytes 114688 | tf_op jit(solution)/shard_map/reshape | solution.py:158
  11.6 0.7 %broadcast_in_dim_reshape.7.tl_ref = f32[1,1,64]{2,1,0:T(1,128)} reshape(f32[4,16]{1,0:T(4,128)S(1)} %broadcast_in_dim.284) | data formatting | bytes 512 | tf_op jit(solution)/shard_map/broadcast_in_dim;reshape | solution.py:195
  12.4 0.7 %fusion.43 = (f32[1,8,256]{2,1,0:T(8,128)S(1)}, f32[1,8,256]{2,1,0:T(8,128)S(1)}, f32[1,8,256]{2,1,0:T(8,128)S(1)}) fusion(f32[1,8,256]{2,1,0:T(8,128)S(1)} %collective-permute-done.4, f32[1,8,256]{2,1,0:T(8,128)S(1)} %collective-permute-done.3, f32[1,8,256]{2,1,0:T(8,128)S(1)} %collective-permute-done.2, f32[8,256]{1,0:T(8,128)} %param.6, pred[]{:T(512)S(6)} %eq.179, ...), kind=kLoop, calls=%fused_computation.84 | loop fusion | flops 43008 | bytes 57356 | tf_op jit(solution)/shard_map/add | solution.py:62
  13.1 5.0 %collective-permute-start.5 = (f32[4,8,256]{2,1,0:T(8,128)S(1)}, f32[4,8,256]{2,1,0:T(8,128)S(1)}, u32[]{:S(2)}, u32[]{:S(2)}) collective-permute-start(f32[4,8,256]{2,1,0:T(8,128)S(1)} %pad_maximum_fusion.1), channel_id=1, source_target_pairs={{0,4},{1,5},{2,6},{3,7},{4,0},{5,1},{6,2},{7,3},{8,12},{9,13},{10,... | collective-permute-start | bytes 98312 | tf_op jit(solution)/shard_map/ppermute | solution.py:56
  18.1 2.6 %collective-permute-start.6 = (f32[4,8,256]{2,1,0:T(8,128)S(1)}, f32[4,8,256]{2,1,0:T(8,128)S(1)}, u32[]{:S(2)}, u32[]{:S(2)}) collective-permute-start(f32[4,8,256]{2,1,0:T(8,128)S(1)} %pad_maximum_fusion.1), channel_id=1, source_target_pairs={{0,8},{1,9},{2,10},{3,11},{4,12},{5,13},{6,14},{7,15},{8,0},{9,1},... | collective-permute-start | bytes 98312 | tf_op jit(solution)/shard_map/ppermute | solution.py:56
  21.5 0.9 %slice_bitcast_fusion.p_ref = f32[24,31,128]{2,1,0:T(8,128)} fusion(f32[32,8,112]{2,0,1:T(8,128)S(1)} %constant_dynamic-update-slice_fusion), kind=kLoop, calls=%fused_computation.31 | loop fusion | bytes 495616 | tf_op jit(solution)/shard_map/transpose | solution.py:169
  22.4 6.6 %shard_map.55 = f32[7,8,31,512]{3,2,1,0:T(8,128)} custom-call(f32[24,31,128]{2,1,0:T(8,128)} %slice_bitcast_fusion.p_ref), custom_call_target="tpu_custom_call" | custom-call | bytes 3555328 | tf_op jit(solution)/shard_map/pallas_call | solution.py:115
  29.5 1.1 %copy.102.energy_ref = f32[16,56,128]{2,1,0:T(8,128)} copy(f32[16,56,128]{1,2,0:T(8,128)S(1)} %bitcast.73) | data formatting | bytes 917504 | tf_op jit(solution)/shard_map/tile | solution.py:189
  32.7 0.9 %select_add_fusion = f32[8,16,16,16]{2,3,1,0:T(8,128)S(1)} fusion(f32[16,16,16]{1,2,0:T(8,128)S(1)} %copy.79, f32[16,16,16]{1,2,0:T(8,128)S(1)} %copy.77, f32[16,16,16]{1,2,0:T(8,128)S(1)} %copy.75, f32[16,16,16]{1,2,0:T(8,128)S(1)} %copy.73, f32[16,16,16]{1,2,0:T(8,128)S(1)} %copy.71, f32[16,16,16]{1,2,0:T(8,128)S(1)} %copy.69, f32[16,16,16]{1,2,0:T(8,128)S(1)} %copy.67, ...), kind=kLoop, calls=%fused_computation.27 | loop fusion | flops 491520 | bytes 262208 | tf_op jit(solution)/shard_map/add | solution.py:74
  35.1 0.7 %copy.81 = f32[8,16,16,16]{1,3,2,0:T(8,128)S(1)} copy(f32[8,16,16,16]{2,3,1,0:T(8,128)S(1)} %broadcast_select_fusion.1) | data formatting | bytes 262144 | tf_op jit(solution)/shard_map/jit(_where)/select_n | solution.py:78
  36.3 1.3 %bitcast_add_fusion.3 = f32[8,16,16,16]{1,3,2,0:T(8,128)} fusion(f32[8,16,16,16]{2,3,1,0:T(8,128)S(1)} %broadcast_select_fusion.1, f32[8,16,16,16]{1,2,3,0:T(8,128)S(1)} %copy.83, f32[8,16,16,16]{1,3,2,0:T(8,128)S(1)} %copy.81, pred[8]{0:T(512)(128)(4,1)S(1)} %get-tuple-element.47, pred[8]{0:T(512)(128)(4,1)S(1)} %get-tuple-element.46, ...), kind=kLoop, calls=%fused_computation.23 | loop fusion | flops 163840 | bytes 524312 | tf_op jit(solution)/shard_map/add | solution.py:83
  37.6 1.5 %copy.86 = f32[8,16,16,16]{3,1,2,0:T(8,128)S(1)} copy(f32[8,16,16,16]{1,3,2,0:T(8,128)} %bitcast_add_fusion.3) | data formatting | bytes 262144 | tf_op jit(solution)/shard_map/add | solution.py:83
  41.5 2.8 %fusion.1 = f32[128,32,256]{2,0,1:T(8,128)S(1)} fusion(f32[128,256,1]{0,1,2:T(8,128)S(1)} %reshape.113, s32[256]{0:T(256)S(1)} %get-tuple-element.52, s32[256]{0:T(256)S(1)} %get-tuple-element.55, s32[256]{0:T(256)S(1)} %get-tuple-element.53, s32[256]{0:T(256)S(1)} %get-tuple-element.54, pred[256]{0:T(512)(128)(4,1)S(1)} %get-tuple-element.50, ...), kind=kOutput, calls=%fused_computation.3 | convolution fusion | flops 3238002688 | bytes 4329984 | tf_op jit(solution)/shard_map/rk,wkn->rwn/dot_general | solution.py:100
  44.4 2.4 %copy.92 = f32[128,32,256]{2,1,0:T(8,128)S(1)} copy(f32[128,32,256]{2,0,1:T(8,128)S(1)} %fusion.1) | data formatting | bytes 8388608 | tf_op jit(solution)/shard_map/rk,wkn->rwn/dot_general | solution.py:100
  46.8 14.1 %fusion.15 = f32[17,7,8,256]{3,1,2,0:T(8,128)S(1)} fusion(f32[8,1,512,256]{3,2,1,0:T(8,128)S(1)} %bitcast.71, f32[7,8,31,512]{3,2,1,0:T(8,128)S(1)} %copy-done), kind=kOutput, calls=%fused_computation.16 | convolution fusion | flops 5989466112 | bytes 8724480 | tf_op jit(solution)/shard_map/conv_general_dilated | solution.py:171
  60.9 1.3 %copy.101.both_ref = f32[17,7,8,256]{3,2,1,0:T(8,128)} copy(f32[17,7,8,256]{3,1,2,0:T(8,128)S(1)} %fusion.15) | data formatting | bytes 1949696 | tf_op jit(solution)/shard_map/conv_general_dilated | solution.py:171
  62.2 3.4 %shard_map.56 = f32[4,16,896]{2,1,0:T(8,128)} custom-call(f32[17,7,8,256]{3,2,1,0:T(8,128)} %copy.101.both_ref, f32[16,56,128]{2,1,0:T(8,128)} %copy.102.energy_ref, f32[1,1,128]{2,1,0:T(1,128)} %broadcast_in_dim_reshape.6.wl_ref, f32[1,1,64]{2,1,0:T(1,128)} %broadcast_in_dim_reshape.7.tl_ref), custom_call_target="tpu_custom_call" | custom-call | tf_op jit(solution)/shard_map/pallas_call | solution.py:145
  (79 shorter events, 9.5 us)
Async XLA Ops:
  0.0 12.3 %collective-permute-start.2 = (f32[1,8,256]{2,1,0:T(8,128)}, f32[1,8,256]{2,1,0:T(8,128)S(1)}, u32[]{:S(2)}, u32[]{:S(2)}) collective-permute-start(f32[1,8,256]{2,1,0:T(8,128)} %bitcast.78), channel_id=1, source_target_pairs={{0,1},{1,0},{2,3},{3,2},{4,5},{5,4},{6,7},{7,6},{8,9},{9,8},{10,11... | collective-permute-start | bytes 24584 | tf_op jit(solution)/shard_map/ppermute | solution.py:56
  0.5 11.9 %collective-permute-start.3 = (f32[1,8,256]{2,1,0:T(8,128)}, f32[1,8,256]{2,1,0:T(8,128)S(1)}, u32[]{:S(2)}, u32[]{:S(2)}) collective-permute-start(f32[1,8,256]{2,1,0:T(8,128)} %bitcast.79), channel_id=1, source_target_pairs={{0,2},{1,3},{2,0},{3,1},{4,6},{5,7},{6,4},{7,5},{8,10},{9,11},{10,... | collective-permute-start | bytes 24584 | tf_op jit(solution)/shard_map/ppermute | solution.py:56
  2.9 9.4 %collective-permute-start.4 = (f32[1,8,256]{2,1,0:T(8,128)}, f32[1,8,256]{2,1,0:T(8,128)S(1)}, u32[]{:S(2)}, u32[]{:S(2)}) collective-permute-start(f32[1,8,256]{2,1,0:T(8,128)} %bitcast.80), channel_id=1, source_target_pairs={{0,3},{1,2},{2,1},{3,0},{4,7},{5,6},{6,5},{7,4},{8,11},{9,10},{10,... | collective-permute-start | bytes 24584 | tf_op jit(solution)/shard_map/ppermute | solution.py:56
  3.9 16.8 %collective-permute-start = (f32[8,8,112]{2,0,1:T(8,128)S(1)}, f32[8,8,112]{2,0,1:T(8,128)S(1)}, u32[]{:S(2)}, u32[]{:S(2)}) collective-permute-start(f32[8,8,112]{2,0,1:T(8,128)S(1)} %copy.62), channel_id=1, source_target_pairs={{0,1},{1,2},{2,3},{3,4},{4,5},{5,6},{6,7},{7,8},{8,9},{9,10},{10,1... | collective-permute-start | bytes 86024 | tf_op jit(solution)/shard_map/ppermute | solution.py:28
  6.0 14.7 %collective-permute-start.1 = (f32[8,8,112]{2,0,1:T(8,128)S(1)}, f32[8,8,112]{2,0,1:T(8,128)S(1)}, u32[]{:S(2)}, u32[]{:S(2)}) collective-permute-start(f32[8,8,112]{2,0,1:T(8,128)S(1)} %copy.63), channel_id=1, source_target_pairs={{1,0},{2,1},{3,2},{4,3},{5,4},{6,5},{7,6},{8,7},{9,8},{10,9},{11,1... | collective-permute-start | bytes 86024 | tf_op jit(solution)/shard_map/ppermute | solution.py:29
  13.1 17.6 %collective-permute-start.5 = (f32[4,8,256]{2,1,0:T(8,128)S(1)}, f32[4,8,256]{2,1,0:T(8,128)S(1)}, u32[]{:S(2)}, u32[]{:S(2)}) collective-permute-start(f32[4,8,256]{2,1,0:T(8,128)S(1)} %pad_maximum_fusion.1), channel_id=1, source_target_pairs={{0,4},{1,5},{2,6},{3,7},{4,0},{5,1},{6,2},{7,3},{8,12},{9,13},{10,... | collective-permute-start | bytes 98312 | tf_op jit(solution)/shard_map/ppermute | solution.py:56
  18.1 12.5 %collective-permute-start.6 = (f32[4,8,256]{2,1,0:T(8,128)S(1)}, f32[4,8,256]{2,1,0:T(8,128)S(1)}, u32[]{:S(2)}, u32[]{:S(2)}) collective-permute-start(f32[4,8,256]{2,1,0:T(8,128)S(1)} %pad_maximum_fusion.1), channel_id=1, source_target_pairs={{0,8},{1,9},{2,10},{3,11},{4,12},{5,13},{6,14},{7,15},{8,0},{9,1},... | collective-permute-start | bytes 98312 | tf_op jit(solution)/shard_map/ppermute | solution.py:56
  20.7 9.9 %collective-permute-start.7 = (f32[4,8,256]{2,1,0:T(8,128)S(1)}, f32[4,8,256]{2,1,0:T(8,128)S(1)}, u32[]{:S(2)}, u32[]{:S(2)}) collective-permute-start(f32[4,8,256]{2,1,0:T(8,128)S(1)} %pad_maximum_fusion.1), channel_id=1, source_target_pairs={{0,12},{1,13},{2,14},{3,15},{4,8},{5,9},{6,10},{7,11},{8,4},{9,5},... | collective-permute-start | bytes 98312 | tf_op jit(solution)/shard_map/ppermute | solution.py:56
  44.3 2.4 %copy-start = (f32[7,8,31,512]{3,2,1,0:T(8,128)S(1)}, f32[7,8,31,512]{3,2,1,0:T(8,128)}, u32[]{:S(2)}) copy-start(f32[7,8,31,512]{3,2,1,0:T(8,128)} %shard_map.55) | copy-start | bytes 10665988

commit v11 on v6

--- a/solution.py
+++ b/solution.py
@@ -170,9 +170,11 @@
     for p in range(1, per):
         totals = totals + weights[p * FIELDS:(p + 1) * FIELDS]
     fields = jnp.log(grouped / jnp.repeat(totals, ZB)[None, None])
-    fields = fields.reshape(rows_x, blocks, BY, FIELDS, ZB)
-    fields = jnp.transpose(fields, (3, 0, 2, 1, 4))
-    return fields.reshape(FIELDS, rows_x, BY * BZ)
+    planes_out = []
+    for k in range(FIELDS):
+        one = fields[:, :, k * ZB:(k + 1) * ZB].reshape(rows_x, blocks, BY, ZB)
+        planes_out.append(jnp.transpose(one, (0, 2, 1, 3)).reshape(rows_x, BY * BZ))
+    return jnp.stack(planes_out)
 
 
 def solution(mesh):

time: 60.9 us -> 57.9 us (0.951)
  local copies, waits for them, and re-layouts: 19.9 us -> 16.1 us
  other arithmetic: 7.7 us -> 8.4 us
    reshape x2 -> x0, local copies, waits for them, and re-layouts: 3.45 us -> none  [the longest x1 2.05 us: local(): fields = fields.reshape(rows_x, blocks, BY, FIELDS, ZB)]
    transpose x1 -> x4, local copies, waits for them, and re-layouts: 2.58 us -> 1.09 us  [local(): planes_out.append(jnp.transpose(one, (0, 2, 1, 3)).reshape(rows_x, BY * BZ))]
    another operation x0 -> x4, local copies, waits for them, and re-layouts: none -> 0.92 us  [local(): return jnp.stack(planes_out)]
    another operation x0 -> x1, other arithmetic: none -> 0.7 us  [local(): return jnp.stack(planes_out)]
  transfers between devices with their start and end apart: 8 -> 8, of which waited for: 0 -> 0; matrix products, arithmetic and copies ran while one was open for 14% -> 15% of each run, Pallas kernels for 11% -> 12%
where the time goes in v11:
time: 57.9 us; the launch traced here: 57.4 us
  local copies, waits for them, and re-layouts  16.1 us (28%)
  starting transfers between devices  14 us (24%)
  matrix products  11.7 us (20%)
  other arithmetic  8.4 us (15%)
  Pallas kernels  6.61 us (11%)
  between operations  0.63 us (1%)
    ppermute x6, starting transfers between devices, gather_planes(): lax.ppermute(held, axis, [(i, i ^ s * step) for i in range(size)])  10.7 us
    conv_general_dilated x1, matrix products, local(): lax.conv_general_dilated(cols, rhs, (1, 1), 'VALID', rhs_dilation=(2, 1),...  8.07 us
    pallas_call x1, Pallas kernels, im2col(): pl.pallas_call(im2col_kernel, out_shape=jax.ShapeDtypeStruct((blocks, BY,...  6.61 us
    dot_general x1, matrix products, toeplitz_rhs(): rhs = jnp.einsum('rk,wkn->rwn', kt, shift, precision=lax.Precision.HIGHEST)  2.85 us
    dot_general x1, local copies, waits for them, and re-layouts, toeplitz_rhs(): rhs = jnp.einsum('rk,wkn->rwn', kt, shift, precision=lax.Precision.HIGHEST)  2.43 us
    ppermute x1, starting transfers between devices, extended(): before = lax.ppermute(last, axis, up)  1.99 us
    add x2, other arithmetic, rotated_kernels(): rotated + jnp.where(expand(order_row == row), jnp.transpose(picked, perm)...  1.55 us
    add x1, local copies, waits for them, and re-layouts, rotated_kernels(): rotated + jnp.where(expand(order_row == row), jnp.transpose(picked, perm)...  1.55 us
  transfers between devices with their start and end apart: 8, of which 0 were waited for; matrix products, arithmetic and copies ran while one was open for 15% of the time, Pallas kernels for 12%

profile of v11, /device:TPU:0, one launch (start us, length us, event | category | flops | bytes accessed | tf_op | source)
XLA Modules:
  0.0 57.4 jit_solution(15211260372880995910)
XLA Ops:
  0.5 2.5 %collective-permute-start.3 = (f32[1,8,256]{2,1,0:T(8,128)}, f32[1,8,256]{2,1,0:T(8,128)S(1)}, u32[]{:S(2)}, u32[]{:S(2)}) collective-permute-start(f32[1,8,256]{2,1,0:T(8,128)} %bitcast.105), channel_id=1, source_target_pairs={{0,2},{1,3},{2,0},{3,1},{4,6},{5,7},{6,4},{7,5},{8,10},{9,11},{10,... | collective-permute-start | bytes 24584 | tf_op jit(solution)/shard_map/ppermute | solution.py:56
  3.1 0.8 %fusion.88 = (f32[8,896]{1,0:T(8,128)S(1)}, f32[8,896]{1,0:T(8,128)S(1)}) fusion(f32[16,896]{1,0:T(8,128)} %param.5), kind=kLoop, calls=%fused_computation.179 | loop fusion | bytes 114688 | tf_op jit(solution)/shard_map/slice | solution.py:27
  3.9 2.0 %collective-permute-start = (f32[8,8,112]{2,0,1:T(8,128)S(1)}, f32[8,8,112]{2,0,1:T(8,128)S(1)}, u32[]{:S(2)}, u32[]{:S(2)}) collective-permute-start(f32[8,8,112]{2,0,1:T(8,128)S(1)} %copy.70), channel_id=1, source_target_pairs={{0,1},{1,2},{2,3},{3,4},{4,5},{5,6},{6,7},{7,8},{8,9},{9,10},{10,1... | collective-permute-start | bytes 86024 | tf_op jit(solution)/shard_map/ppermute | solution.py:28
  6.0 1.3 %collective-permute-start.1 = (f32[8,8,112]{2,0,1:T(8,128)S(1)}, f32[8,8,112]{2,0,1:T(8,128)S(1)}, u32[]{:S(2)}, u32[]{:S(2)}) collective-permute-start(f32[8,8,112]{2,0,1:T(8,128)S(1)} %copy.71), channel_id=1, source_target_pairs={{1,0},{2,1},{3,2},{4,3},{5,4},{6,5},{7,6},{8,7},{9,8},{10,9},{11,1... | collective-permute-start | bytes 86024 | tf_op jit(solution)/shard_map/ppermute | solution.py:29
  7.4 0.7 %broadcast_compare_fusion.10 = (pred[8]{0:T(512)(128)(4,1)S(1)}, pred[8]{0:T(512)(128)(4,1)S(1)}, pred[8]{0:T(512)(128)(4,1)S(1)}, pred[8]{0:T(512)(128)(4,1)S(1...) fusion(s32[8]{0:T(128)} %param.8), kind=kLoop, calls=%fused_computation.161 | loop fusion | flops 64 | bytes 96 | tf_op jit(solution)/shard_map/eq | solution.py:74
  8.0 0.7 %broadcast_compare_fusion.1 = (pred[8]{0:T(512)(128)(4,1)S(1)}, s32[8]{0:T(128)S(1)}, pred[8]{0:T(512)(128)(4,1)S(1)}, s32[8]{0:T(128)S(1)}) fusion(s32[8]{0:T(128)} %param.7), kind=kLoop, calls=%fused_computation.152 | loop fusion | flops 376 | bytes 112 | tf_op jit(solution)/shard_map/eq | solution.py:83
  8.7 0.7 %convert_element_type.4 = f32[8]{0:T(128)S(1)} convert(s32[8]{0:T(128)} %param.9) | non-fusion elementwise | flops 8 | bytes 64 | tf_op jit(solution)/shard_map/convert_element_type | solution.py:163
  9.8 0.9 %reshape.128 = f32[16,8,112]{2,1,0:T(8,128)S(1)} reshape(f32[16,896]{1,0:T(8,128)} %param.5) | data formatting | bytes 114688 | tf_op jit(solution)/shard_map/reshape | solution.py:128
  11.2 0.7 %fusion.48 = (f32[1,8,256]{2,1,0:T(8,128)S(1)}, f32[1,8,256]{2,1,0:T(8,128)S(1)}, f32[1,8,256]{2,1,0:T(8,128)S(1)}) fusion(f32[1,8,256]{2,1,0:T(8,128)S(1)} %collective-permute-done.4, f32[1,8,256]{2,1,0:T(8,128)S(1)} %collective-permute-done.3, f32[1,8,256]{2,1,0:T(8,128)S(1)} %collective-permute-done.2, f32[8,256]{1,0:T(8,128)} %param.6, pred[]{:T(512)S(6)} %eq.179, ...), kind=kLoop, calls=%fused_computation.94 | loop fusion | flops 43008 | bytes 57356 | tf_op jit(solution)/shard_map/add | solution.py:62
  12.0 5.0 %collective-permute-start.5 = (f32[4,8,256]{2,1,0:T(8,128)S(1)}, f32[4,8,256]{2,1,0:T(8,128)S(1)}, u32[]{:S(2)}, u32[]{:S(2)}) collective-permute-start(f32[4,8,256]{2,1,0:T(8,128)S(1)} %pad_maximum_fusion.2), channel_id=1, source_target_pairs={{0,4},{1,5},{2,6},{3,7},{4,0},{5,1},{6,2},{7,3},{8,12},{9,13},{10,... | collective-permute-start | bytes 98312 | tf_op jit(solution)/shard_map/ppermute | solution.py:56
  17.0 2.6 %collective-permute-start.6 = (f32[4,8,256]{2,1,0:T(8,128)S(1)}, f32[4,8,256]{2,1,0:T(8,128)S(1)}, u32[]{:S(2)}, u32[]{:S(2)}) collective-permute-start(f32[4,8,256]{2,1,0:T(8,128)S(1)} %pad_maximum_fusion.2), channel_id=1, source_target_pairs={{0,8},{1,9},{2,10},{3,11},{4,12},{5,13},{6,14},{7,15},{8,0},{9,1},... | collective-permute-start | bytes 98312 | tf_op jit(solution)/shard_map/ppermute | solution.py:56
  20.4 0.9 %slice_bitcast_fusion.p_ref = f32[24,31,128]{2,1,0:T(8,128)} fusion(f32[32,8,112]{2,0,1:T(8,128)S(1)} %constant_dynamic-update-slice_fusion), kind=kLoop, calls=%fused_computation.41 | loop fusion | bytes 495616 | tf_op jit(solution)/shard_map/transpose | solution.py:139
  21.3 6.6 %shard_map.55 = f32[7,8,31,512]{3,2,1,0:T(8,128)} custom-call(f32[24,31,128]{2,1,0:T(8,128)} %slice_bitcast_fusion.p_ref), custom_call_target="tpu_custom_call" | custom-call | bytes 3555328 | tf_op jit(solution)/shard_map/pallas_call | solution.py:115
  28.4 1.1 %copy.109 = f32[16,56,128]{2,0,1:T(8,128)} copy(f32[16,56,128]{1,2,0:T(8,128)S(1)} %bitcast.95) | data formatting | bytes 917504 | tf_op jit(solution)/shard_map/sqrt | solution.py:162
  31.6 0.9 %select_add_fusion = f32[8,16,16,16]{2,3,1,0:T(8,128)S(1)} fusion(f32[16,16,16]{1,2,0:T(8,128)S(1)} %copy.87, f32[16,16,16]{1,2,0:T(8,128)S(1)} %copy.85, f32[16,16,16]{1,2,0:T(8,128)S(1)} %copy.83, f32[16,16,16]{1,2,0:T(8,128)S(1)} %copy.81, f32[16,16,16]{1,2,0:T(8,128)S(1)} %copy.79, f32[16,16,16]{1,2,0:T(8,128)S(1)} %copy.77, f32[16,16,16]{1,2,0:T(8,128)S(1)} %copy.75, ...), kind=kLoop, calls=%fused_computation.29 | loop fusion | flops 491520 | bytes 262208 | tf_op jit(solution)/shard_map/add | solution.py:74
  32.7 0.5 rev.13
  34.1 0.7 %copy.89 = f32[8,16,16,16]{1,3,2,0:T(8,128)S(1)} copy(f32[8,16,16,16]{2,3,1,0:T(8,128)S(1)} %broadcast_select_fusion.1) | data formatting | bytes 262144 | tf_op jit(solution)/shard_map/jit(_where)/select_n | solution.py:78
  35.2 1.3 %bitcast_add_fusion.3 = f32[8,16,16,16]{1,3,2,0:T(8,128)} fusion(f32[8,16,16,16]{2,3,1,0:T(8,128)S(1)} %broadcast_select_fusion.1, f32[8,16,16,16]{1,2,3,0:T(8,128)S(1)} %copy.91, f32[8,16,16,16]{1,3,2,0:T(8,128)S(1)} %copy.89, pred[8]{0:T(512)(128)(4,1)S(1)} %get-tuple-element.51, pred[8]{0:T(512)(128)(4,1)S(1)} %get-tuple-element.50, ...), kind=kLoop, calls=%fused_computation.25 | loop fusion | flops 163840 | bytes 524312 | tf_op jit(solution)/shard_map/add | solution.py:83
  36.5 1.5 %copy.94 = f32[8,16,16,16]{3,1,2,0:T(8,128)S(1)} copy(f32[8,16,16,16]{1,3,2,0:T(8,128)} %bitcast_add_fusion.3) | data formatting | bytes 262144 | tf_op jit(solution)/shard_map/add | solution.py:83
  38.3 0.6 %fusion.86 = (f32[8]{0:T(128)S(1)}, f32[8,16,16,16]{3,2,1,0:T(8,128)S(1)}) fusion(f32[8,16,16,16]{1,2,3,0:T(8,128)S(1)} %copy.91, pred[8]{0:T(512)(128)(4,1)S(1)} %get-tuple-element.15, f32[8,16,16,16]{3,1,2,0:T(8,128)S(1)} %bitcast_add_fusion.1), kind=kLoop, calls=%fused_computation.177 | loop fusion | flops 98296 | bytes 393256 | tf_op jit(solution)/shard_map/reduce_sum | solution.py:85
  40.4 2.9 %fusion.1 = f32[128,32,256]{2,0,1:T(8,128)S(1)} fusion(f32[128,256,1]{0,1,2:T(8,128)S(1)} %reshape.160, s32[256]{0:T(256)S(1)} %get-tuple-element.56, s32[256]{0:T(256)S(1)} %get-tuple-element.59, s32[256]{0:T(256)S(1)} %get-tuple-element.57, s32[256]{0:T(256)S(1)} %get-tuple-element.58, pred[256]{0:T(512)(128)(4,1)S(1)} %get-tuple-element.54, ...), kind=kOutput, calls=%fused_computation.3 | convolution fusion | flops 3238002688 | bytes 4329984 | tf_op jit(solution)/shard_map/rk,wkn->rwn/dot_general | solution.py:100
  43.3 2.4 %copy.100 = f32[128,32,256]{2,1,0:T(8,128)S(1)} copy(f32[128,32,256]{2,0,1:T(8,128)S(1)} %fusion.1) | data formatting | bytes 8388608 | tf_op jit(solution)/shard_map/rk,wkn->rwn/dot_general | solution.py:100
  45.7 8.1 %fusion.15 = f32[17,8,7,256]{3,1,2,0:T(8,128)S(1)} fusion(f32[8,1,512,256]{3,2,1,0:T(8,128)S(1)} %bitcast.93, f32[8,7,31,512]{3,2,1,0:T(8,128)S(1)} %bitcast.92), kind=kOutput, calls=%fused_computation.16 | convolution fusion | flops 5989466112 | bytes 8724480 | tf_op jit(solution)/shard_map/conv_general_dilated | solution.py:141
  56.7 0.7 %pad_maximum_fusion = f32[4,16,896]{2,1,0:T(8,128)} fusion(f32[1,16,896]{2,1,0:T(8,128)S(1)} %stack_reshape.15, f32[1,16,896]{2,1,0:T(8,128)S(1)} %stack_reshape.14, f32[1,16,896]{2,1,0:T(8,128)S(1)} %stack_reshape.13, f32[1,16,896]{2,1,0:T(8,128)S(1)} %stack_reshape.12), kind=kLoop, calls=%fused_computation.42 | loop fusion | flops 172032 | bytes 458752 | tf_op jit(solution)/shard_map/stack | solution.py:177
  (93 shorter events, 10.8 us)
Async XLA Ops:
  0.0 11.2 %collective-permute-start.2 = (f32[1,8,256]{2,1,0:T(8,128)}, f32[1,8,256]{2,1,0:T(8,128)S(1)}, u32[]{:S(2)}, u32[]{:S(2)}) collective-permute-start(f32[1,8,256]{2,1,0:T(8,128)} %bitcast.104), channel_id=1, source_target_pairs={{0,1},{1,0},{2,3},{3,2},{4,5},{5,4},{6,7},{7,6},{8,9},{9,8},{10,11... | collective-permute-start | bytes 24584 | tf_op jit(solution)/shard_map/ppermute | solution.py:56
  0.5 10.7 %collective-permute-start.3 = (f32[1,8,256]{2,1,0:T(8,128)}, f32[1,8,256]{2,1,0:T(8,128)S(1)}, u32[]{:S(2)}, u32[]{:S(2)}) collective-permute-start(f32[1,8,256]{2,1,0:T(8,128)} %bitcast.105), channel_id=1, source_target_pairs={{0,2},{1,3},{2,0},{3,1},{4,6},{5,7},{6,4},{7,5},{8,10},{9,11},{10,... | collective-permute-start | bytes 24584 | tf_op jit(solution)/shard_map/ppermute | solution.py:56
  2.9 8.3 %collective-permute-start.4 = (f32[1,8,256]{2,1,0:T(8,128)}, f32[1,8,256]{2,1,0:T(8,128)S(1)}, u32[]{:S(2)}, u32[]{:S(2)}) collective-permute-start(f32[1,8,256]{2,1,0:T(8,128)} %bitcast.106), channel_id=1, source_target_pairs={{0,3},{1,2},{2,1},{3,0},{4,7},{5,6},{6,5},{7,4},{8,11},{9,10},{10,... | collective-permute-start | bytes 24584 | tf_op jit(solution)/shard_map/ppermute | solution.py:56
  3.9 15.7 %collective-permute-start = (f32[8,8,112]{2,0,1:T(8,128)S(1)}, f32[8,8,112]{2,0,1:T(8,128)S(1)}, u32[]{:S(2)}, u32[]{:S(2)}) collective-permute-start(f32[8,8,112]{2,0,1:T(8,128)S(1)} %copy.70), channel_id=1, source_target_pairs={{0,1},{1,2},{2,3},{3,4},{4,5},{5,6},{6,7},{7,8},{8,9},{9,10},{10,1... | collective-permute-start | bytes 86024 | tf_op jit(solution)/shard_map/ppermute | solution.py:28
  6.0 13.6 %collective-permute-start.1 = (f32[8,8,112]{2,0,1:T(8,128)S(1)}, f32[8,8,112]{2,0,1:T(8,128)S(1)}, u32[]{:S(2)}, u32[]{:S(2)}) collective-permute-start(f32[8,8,112]{2,0,1:T(8,128)S(1)} %copy.71), channel_id=1, source_target_pairs={{1,0},{2,1},{3,2},{4,3},{5,4},{6,5},{7,6},{8,7},{9,8},{10,9},{11,1... | collective-permute-start | bytes 86024 | tf_op jit(solution)/shard_map/ppermute | solution.py:29
  12.0 17.6 %collective-permute-start.5 = (f32[4,8,256]{2,1,0:T(8,128)S(1)}, f32[4,8,256]{2,1,0:T(8,128)S(1)}, u32[]{:S(2)}, u32[]{:S(2)}) collective-permute-start(f32[4,8,256]{2,1,0:T(8,128)S(1)} %pad_maximum_fusion.2), channel_id=1, source_target_pairs={{0,4},{1,5},{2,6},{3,7},{4,0},{5,1},{6,2},{7,3},{8,12},{9,13},{10,... | collective-permute-start | bytes 98312 | tf_op jit(solution)/shard_map/ppermute | solution.py:56
  17.0 12.5 %collective-permute-start.6 = (f32[4,8,256]{2,1,0:T(8,128)S(1)}, f32[4,8,256]{2,1,0:T(8,128)S(1)}, u32[]{:S(2)}, u32[]{:S(2)}) collective-permute-start(f32[4,8,256]{2,1,0:T(8,128)S(1)} %pad_maximum_fusion.2), channel_id=1, source_target_pairs={{0,8},{1,9},{2,10},{3,11},{4,12},{5,13},{6,14},{7,15},{8,0},{9,1},... | collective-permute-start | bytes 98312 | tf_op jit(solution)/shard_map/ppermute | solution.py:56
  19.6 10.0 %collective-permute-start.7 = (f32[4,8,256]{2,1,0:T(8,128)S(1)}, f32[4,8,256]{2,1,0:T(8,128)S(1)}, u32[]{:S(2)}, u32[]{:S(2)}) collective-permute-start(f32[4,8,256]{2,1,0:T(8,128)S(1)} %pad_maximum_fusion.2), channel_id=1, source_target_pairs={{0,12},{1,13},{2,14},{3,15},{4,8},{5,9},{6,10},{7,11},{8,4},{9,5},... | collective-permute-start | bytes 98312 | tf_op jit(solution)/shard_map/ppermute | solution.py:56
  43.3 2.4 %copy-start = (f32[7,8,31,512]{3,2,1,0:T(8,128)S(1)}, f32[7,8,31,512]{3,2,1,0:T(8,128)}, u32[]{:S(2)}) copy-start(f32[7,8,31,512]{3,2,1,0:T(8,128)} %shard_map.55) | copy-start | bytes 10665988
  45.7 8.2 %copy-start.1 = (f32[16,56,128]{2,0,1:T(8,128)S(1)}, f32[16,56,128]{2,0,1:T(8,128)}, u32[]{:S(2)}) copy-start(f32[16,56,128]{2,0,1:T(8,128)} %copy.109) | copy-start | bytes 1376260

commit v12 on v11

--- a/solution.py
+++ b/solution.py
@@ -37,7 +37,7 @@
 
 
 def contract(letters, data, table):
-    return jnp.einsum(letters, data, table, precision=lax.Precision.HIGHEST)
+    return jnp.einsum(letters, data, table, precision=lax.Precision.HIGH)
 
 
 def expand(flag):

time: 57.9 us -> 57.8 us (level)
  no operation moved by 1% of the time
where the time goes in v12:
time: 57.8 us; the launch traced here: 57.3 us
  local copies, waits for them, and re-layouts  16.1 us (28%)
  starting transfers between devices  14 us (24%)
  matrix products  11.6 us (20%)
  other arithmetic  8.4 us (15%)
  Pallas kernels  6.61 us (11%)
  between operations  0.63 us (1%)
    ppermute x6, starting transfers between devices, gather_planes(): lax.ppermute(held, axis, [(i, i ^ s * step) for i in range(size)])  10.7 us
    conv_general_dilated x1, matrix products, local(): lax.conv_general_dilated(cols, rhs, (1, 1), 'VALID', rhs_dilation=(2, 1),...  8.07 us
    pallas_call x1, Pallas kernels, im2col(): pl.pallas_call(im2col_kernel, out_shape=jax.ShapeDtypeStruct((blocks, BY,...  6.61 us
    dot_general x1, matrix products, toeplitz_rhs(): rhs = jnp.einsum('rk,wkn->rwn', kt, shift, precision=lax.Precision.HIGHEST)  2.85 us
    dot_general x1, local copies, waits for them, and re-layouts, toeplitz_rhs(): rhs = jnp.einsum('rk,wkn->rwn', kt, shift, precision=lax.Precision.HIGHEST)  2.43 us
    ppermute x1, starting transfers between devices, extended(): before = lax.ppermute(last, axis, up)  1.99 us
    add x2, other arithmetic, rotated_kernels(): rotated + jnp.where(expand(order_row == row), jnp.transpose(picked, perm)...  1.55 us
    add x1, local copies, waits for them, and re-layouts, rotated_kernels(): rotated + jnp.where(expand(order_row == row), jnp.transpose(picked, perm)...  1.55 us
  transfers between devices with their start and end apart: 8, of which 0 were waited for; matrix products, arithmetic and copies ran while one was open for 15% of the time, Pallas kernels for 12%

profile of v12, /device:TPU:0, one launch (start us, length us, event | category | flops | bytes accessed | tf_op | source)
XLA Modules:
  0.0 57.3 jit_solution(17738562169739157874)
XLA Ops:
  0.5 2.5 %collective-permute-start.3 = (f32[1,8,256]{2,1,0:T(8,128)}, f32[1,8,256]{2,1,0:T(8,128)S(1)}, u32[]{:S(2)}, u32[]{:S(2)}) collective-permute-start(f32[1,8,256]{2,1,0:T(8,128)} %bitcast.105), channel_id=1, source_target_pairs={{0,2},{1,3},{2,0},{3,1},{4,6},{5,7},{6,4},{7,5},{8,10},{9,11},{10,... | collective-permute-start | bytes 24584 | tf_op jit(solution)/shard_map/ppermute | solution.py:56
  3.1 0.8 %fusion.88 = (f32[8,896]{1,0:T(8,128)S(1)}, f32[8,896]{1,0:T(8,128)S(1)}) fusion(f32[16,896]{1,0:T(8,128)} %param.5), kind=kLoop, calls=%fused_computation.179 | loop fusion | bytes 114688 | tf_op jit(solution)/shard_map/slice | solution.py:27
  3.9 2.0 %collective-permute-start = (f32[8,8,112]{2,0,1:T(8,128)S(1)}, f32[8,8,112]{2,0,1:T(8,128)S(1)}, u32[]{:S(2)}, u32[]{:S(2)}) collective-permute-start(f32[8,8,112]{2,0,1:T(8,128)S(1)} %copy.70), channel_id=1, source_target_pairs={{0,1},{1,2},{2,3},{3,4},{4,5},{5,6},{6,7},{7,8},{8,9},{9,10},{10,1... | collective-permute-start | bytes 86024 | tf_op jit(solution)/shard_map/ppermute | solution.py:28
  6.0 1.3 %collective-permute-start.1 = (f32[8,8,112]{2,0,1:T(8,128)S(1)}, f32[8,8,112]{2,0,1:T(8,128)S(1)}, u32[]{:S(2)}, u32[]{:S(2)}) collective-permute-start(f32[8,8,112]{2,0,1:T(8,128)S(1)} %copy.71), channel_id=1, source_target_pairs={{1,0},{2,1},{3,2},{4,3},{5,4},{6,5},{7,6},{8,7},{9,8},{10,9},{11,1... | collective-permute-start | bytes 86024 | tf_op jit(solution)/shard_map/ppermute | solution.py:29
  7.4 0.7 %broadcast_compare_fusion.10 = (pred[8]{0:T(512)(128)(4,1)S(1)}, pred[8]{0:T(512)(128)(4,1)S(1)}, pred[8]{0:T(512)(128)(4,1)S(1)}, pred[8]{0:T(512)(128)(4,1)S(1...) fusion(s32[8]{0:T(128)} %param.8), kind=kLoop, calls=%fused_computation.161 | loop fusion | flops 64 | bytes 96 | tf_op jit(solution)/shard_map/eq | solution.py:74
  8.0 0.7 %broadcast_compare_fusion.1 = (pred[8]{0:T(512)(128)(4,1)S(1)}, s32[8]{0:T(128)S(1)}, pred[8]{0:T(512)(128)(4,1)S(1)}, s32[8]{0:T(128)S(1)}) fusion(s32[8]{0:T(128)} %param.7), kind=kLoop, calls=%fused_computation.152 | loop fusion | flops 376 | bytes 112 | tf_op jit(solution)/shard_map/eq | solution.py:83
  8.7 0.7 %convert_element_type.4 = f32[8]{0:T(128)S(1)} convert(s32[8]{0:T(128)} %param.9) | non-fusion elementwise | flops 8 | bytes 64 | tf_op jit(solution)/shard_map/convert_element_type | solution.py:163
  9.8 0.9 %reshape.128 = f32[16,8,112]{2,1,0:T(8,128)S(1)} reshape(f32[16,896]{1,0:T(8,128)} %param.5) | data formatting | bytes 114688 | tf_op jit(solution)/shard_map/reshape | solution.py:128
  11.2 0.7 %fusion.48 = (f32[1,8,256]{2,1,0:T(8,128)S(1)}, f32[1,8,256]{2,1,0:T(8,128)S(1)}, f32[1,8,256]{2,1,0:T(8,128)S(1)}) fusion(f32[1,8,256]{2,1,0:T(8,128)S(1)} %collective-permute-done.4, f32[1,8,256]{2,1,0:T(8,128)S(1)} %collective-permute-done.3, f32[1,8,256]{2,1,0:T(8,128)S(1)} %collective-permute-done.2, f32[8,256]{1,0:T(8,128)} %param.6, pred[]{:T(512)S(6)} %eq.179, ...), kind=kLoop, calls=%fused_computation.94 | loop fusion | flops 43008 | bytes 57356 | tf_op jit(solution)/shard_map/add | solution.py:62
  12.0 5.0 %collective-permute-start.5 = (f32[4,8,256]{2,1,0:T(8,128)S(1)}, f32[4,8,256]{2,1,0:T(8,128)S(1)}, u32[]{:S(2)}, u32[]{:S(2)}) collective-permute-start(f32[4,8,256]{2,1,0:T(8,128)S(1)} %pad_maximum_fusion.2), channel_id=1, source_target_pairs={{0,4},{1,5},{2,6},{3,7},{4,0},{5,1},{6,2},{7,3},{8,12},{9,13},{10,... | collective-permute-start | bytes 98312 | tf_op jit(solution)/shard_map/ppermute | solution.py:56
  17.0 2.6 %collective-permute-start.6 = (f32[4,8,256]{2,1,0:T(8,128)S(1)}, f32[4,8,256]{2,1,0:T(8,128)S(1)}, u32[]{:S(2)}, u32[]{:S(2)}) collective-permute-start(f32[4,8,256]{2,1,0:T(8,128)S(1)} %pad_maximum_fusion.2), channel_id=1, source_target_pairs={{0,8},{1,9},{2,10},{3,11},{4,12},{5,13},{6,14},{7,15},{8,0},{9,1},... | collective-permute-start | bytes 98312 | tf_op jit(solution)/shard_map/ppermute | solution.py:56
  20.3 0.9 %slice_bitcast_fusion.p_ref = f32[24,31,128]{2,1,0:T(8,128)} fusion(f32[32,8,112]{2,0,1:T(8,128)S(1)} %constant_dynamic-update-slice_fusion), kind=kLoop, calls=%fused_computation.41 | loop fusion | bytes 495616 | tf_op jit(solution)/shard_map/transpose | solution.py:139
  21.2 6.6 %shard_map.55 = f32[7,8,31,512]{3,2,1,0:T(8,128)} custom-call(f32[24,31,128]{2,1,0:T(8,128)} %slice_bitcast_fusion.p_ref), custom_call_target="tpu_custom_call" | custom-call | bytes 3555328 | tf_op jit(solution)/shard_map/pallas_call | solution.py:115
  28.3 1.1 %copy.109 = f32[16,56,128]{2,0,1:T(8,128)} copy(f32[16,56,128]{1,2,0:T(8,128)S(1)} %bitcast.95) | data formatting | bytes 917504 | tf_op jit(solution)/shard_map/sqrt | solution.py:162
  31.5 0.9 %select_add_fusion = f32[8,16,16,16]{2,3,1,0:T(8,128)S(1)} fusion(f32[16,16,16]{1,2,0:T(8,128)S(1)} %copy.87, f32[16,16,16]{1,2,0:T(8,128)S(1)} %copy.85, f32[16,16,16]{1,2,0:T(8,128)S(1)} %copy.83, f32[16,16,16]{1,2,0:T(8,128)S(1)} %copy.81, f32[16,16,16]{1,2,0:T(8,128)S(1)} %copy.79, f32[16,16,16]{1,2,0:T(8,128)S(1)} %copy.77, f32[16,16,16]{1,2,0:T(8,128)S(1)} %copy.75, ...), kind=kLoop, calls=%fused_computation.29 | loop fusion | flops 491520 | bytes 262208 | tf_op jit(solution)/shard_map/add | solution.py:74
  32.6 0.5 rev.13
  34.0 0.7 %copy.89 = f32[8,16,16,16]{1,3,2,0:T(8,128)S(1)} copy(f32[8,16,16,16]{2,3,1,0:T(8,128)S(1)} %broadcast_select_fusion.1) | data formatting | bytes 262144 | tf_op jit(solution)/shard_map/jit(_where)/select_n | solution.py:78
  35.1 1.3 %bitcast_add_fusion.3 = f32[8,16,16,16]{1,3,2,0:T(8,128)} fusion(f32[8,16,16,16]{2,3,1,0:T(8,128)S(1)} %broadcast_select_fusion.1, f32[8,16,16,16]{1,2,3,0:T(8,128)S(1)} %copy.91, f32[8,16,16,16]{1,3,2,0:T(8,128)S(1)} %copy.89, pred[8]{0:T(512)(128)(4,1)S(1)} %get-tuple-element.51, pred[8]{0:T(512)(128)(4,1)S(1)} %get-tuple-element.50, ...), kind=kLoop, calls=%fused_computation.25 | loop fusion | flops 163840 | bytes 524312 | tf_op jit(solution)/shard_map/add | solution.py:83
  36.4 1.5 %copy.94 = f32[8,16,16,16]{3,1,2,0:T(8,128)S(1)} copy(f32[8,16,16,16]{1,3,2,0:T(8,128)} %bitcast_add_fusion.3) | data formatting | bytes 262144 | tf_op jit(solution)/shard_map/add | solution.py:83
  38.2 0.6 %fusion.86 = (f32[8]{0:T(128)S(1)}, f32[8,16,16,16]{3,2,1,0:T(8,128)S(1)}) fusion(f32[8,16,16,16]{1,2,3,0:T(8,128)S(1)} %copy.91, pred[8]{0:T(512)(128)(4,1)S(1)} %get-tuple-element.15, f32[8,16,16,16]{3,1,2,0:T(8,128)S(1)} %bitcast_add_fusion.1), kind=kLoop, calls=%fused_computation.177 | loop fusion | flops 98296 | bytes 393256 | tf_op jit(solution)/shard_map/reduce_sum | solution.py:85
  40.3 2.8 %fusion.1 = f32[128,32,256]{2,0,1:T(8,128)S(1)} fusion(f32[128,256,1]{0,1,2:T(8,128)S(1)} %reshape.160, s32[256]{0:T(256)S(1)} %get-tuple-element.56, s32[256]{0:T(256)S(1)} %get-tuple-element.59, s32[256]{0:T(256)S(1)} %get-tuple-element.57, s32[256]{0:T(256)S(1)} %get-tuple-element.58, pred[256]{0:T(512)(128)(4,1)S(1)} %get-tuple-element.54, ...), kind=kOutput, calls=%fused_computation.3 | convolution fusion | flops 3238002688 | bytes 4329984 | tf_op jit(solution)/shard_map/rk,wkn->rwn/dot_general | solution.py:100
  43.2 2.4 %copy.100 = f32[128,32,256]{2,1,0:T(8,128)S(1)} copy(f32[128,32,256]{2,0,1:T(8,128)S(1)} %fusion.1) | data formatting | bytes 8388608 | tf_op jit(solution)/shard_map/rk,wkn->rwn/dot_general | solution.py:100
  45.6 8.1 %fusion.15 = f32[17,8,7,256]{3,1,2,0:T(8,128)S(1)} fusion(f32[8,1,512,256]{3,2,1,0:T(8,128)S(1)} %bitcast.93, f32[8,7,31,512]{3,2,1,0:T(8,128)S(1)} %bitcast.92), kind=kOutput, calls=%fused_computation.16 | convolution fusion | flops 5989466112 | bytes 8724480 | tf_op jit(solution)/shard_map/conv_general_dilated | solution.py:141
  56.6 0.7 %pad_maximum_fusion = f32[4,16,896]{2,1,0:T(8,128)} fusion(f32[1,16,896]{2,1,0:T(8,128)S(1)} %stack_reshape.15, f32[1,16,896]{2,1,0:T(8,128)S(1)} %stack_reshape.14, f32[1,16,896]{2,1,0:T(8,128)S(1)} %stack_reshape.13, f32[1,16,896]{2,1,0:T(8,128)S(1)} %stack_reshape.12), kind=kLoop, calls=%fused_computation.42 | loop fusion | flops 172032 | bytes 458752 | tf_op jit(solution)/shard_map/stack | solution.py:177
  (93 shorter events, 10.7 us)
Async XLA Ops:
  0.0 11.2 %collective-permute-start.2 = (f32[1,8,256]{2,1,0:T(8,128)}, f32[1,8,256]{2,1,0:T(8,128)S(1)}, u32[]{:S(2)}, u32[]{:S(2)}) collective-permute-start(f32[1,8,256]{2,1,0:T(8,128)} %bitcast.104), channel_id=1, source_target_pairs={{0,1},{1,0},{2,3},{3,2},{4,5},{5,4},{6,7},{7,6},{8,9},{9,8},{10,11... | collective-permute-start | bytes 24584 | tf_op jit(solution)/shard_map/ppermute | solution.py:56
  0.5 10.7 %collective-permute-start.3 = (f32[1,8,256]{2,1,0:T(8,128)}, f32[1,8,256]{2,1,0:T(8,128)S(1)}, u32[]{:S(2)}, u32[]{:S(2)}) collective-permute-start(f32[1,8,256]{2,1,0:T(8,128)} %bitcast.105), channel_id=1, source_target_pairs={{0,2},{1,3},{2,0},{3,1},{4,6},{5,7},{6,4},{7,5},{8,10},{9,11},{10,... | collective-permute-start | bytes 24584 | tf_op jit(solution)/shard_map/ppermute | solution.py:56
  2.9 8.3 %collective-permute-start.4 = (f32[1,8,256]{2,1,0:T(8,128)}, f32[1,8,256]{2,1,0:T(8,128)S(1)}, u32[]{:S(2)}, u32[]{:S(2)}) collective-permute-start(f32[1,8,256]{2,1,0:T(8,128)} %bitcast.106), channel_id=1, source_target_pairs={{0,3},{1,2},{2,1},{3,0},{4,7},{5,6},{6,5},{7,4},{8,11},{9,10},{10,... | collective-permute-start | bytes 24584 | tf_op jit(solution)/shard_map/ppermute | solution.py:56
  3.9 15.7 %collective-permute-start = (f32[8,8,112]{2,0,1:T(8,128)S(1)}, f32[8,8,112]{2,0,1:T(8,128)S(1)}, u32[]{:S(2)}, u32[]{:S(2)}) collective-permute-start(f32[8,8,112]{2,0,1:T(8,128)S(1)} %copy.70), channel_id=1, source_target_pairs={{0,1},{1,2},{2,3},{3,4},{4,5},{5,6},{6,7},{7,8},{8,9},{9,10},{10,1... | collective-permute-start | bytes 86024 | tf_op jit(solution)/shard_map/ppermute | solution.py:28
  6.0 13.6 %collective-permute-start.1 = (f32[8,8,112]{2,0,1:T(8,128)S(1)}, f32[8,8,112]{2,0,1:T(8,128)S(1)}, u32[]{:S(2)}, u32[]{:S(2)}) collective-permute-start(f32[8,8,112]{2,0,1:T(8,128)S(1)} %copy.71), channel_id=1, source_target_pairs={{1,0},{2,1},{3,2},{4,3},{5,4},{6,5},{7,6},{8,7},{9,8},{10,9},{11,1... | collective-permute-start | bytes 86024 | tf_op jit(solution)/shard_map/ppermute | solution.py:29
  12.0 17.5 %collective-permute-start.5 = (f32[4,8,256]{2,1,0:T(8,128)S(1)}, f32[4,8,256]{2,1,0:T(8,128)S(1)}, u32[]{:S(2)}, u32[]{:S(2)}) collective-permute-start(f32[4,8,256]{2,1,0:T(8,128)S(1)} %pad_maximum_fusion.2), channel_id=1, source_target_pairs={{0,4},{1,5},{2,6},{3,7},{4,0},{5,1},{6,2},{7,3},{8,12},{9,13},{10,... | collective-permute-start | bytes 98312 | tf_op jit(solution)/shard_map/ppermute | solution.py:56
  17.0 12.5 %collective-permute-start.6 = (f32[4,8,256]{2,1,0:T(8,128)S(1)}, f32[4,8,256]{2,1,0:T(8,128)S(1)}, u32[]{:S(2)}, u32[]{:S(2)}) collective-permute-start(f32[4,8,256]{2,1,0:T(8,128)S(1)} %pad_maximum_fusion.2), channel_id=1, source_target_pairs={{0,8},{1,9},{2,10},{3,11},{4,12},{5,13},{6,14},{7,15},{8,0},{9,1},... | collective-permute-start | bytes 98312 | tf_op jit(solution)/shard_map/ppermute | solution.py:56
  19.6 9.9 %collective-permute-start.7 = (f32[4,8,256]{2,1,0:T(8,128)S(1)}, f32[4,8,256]{2,1,0:T(8,128)S(1)}, u32[]{:S(2)}, u32[]{:S(2)}) collective-permute-start(f32[4,8,256]{2,1,0:T(8,128)S(1)} %pad_maximum_fusion.2), channel_id=1, source_target_pairs={{0,12},{1,13},{2,14},{3,15},{4,8},{5,9},{6,10},{7,11},{8,4},{9,5},... | collective-permute-start | bytes 98312 | tf_op jit(solution)/shard_map/ppermute | solution.py:56
  43.2 2.4 %copy-start = (f32[7,8,31,512]{3,2,1,0:T(8,128)S(1)}, f32[7,8,31,512]{3,2,1,0:T(8,128)}, u32[]{:S(2)}) copy-start(f32[7,8,31,512]{3,2,1,0:T(8,128)} %shard_map.55) | copy-start | bytes 10665988
  45.6 8.2 %copy-start.1 = (f32[16,56,128]{2,0,1:T(8,128)S(1)}, f32[16,56,128]{2,0,1:T(8,128)}, u32[]{:S(2)}) copy-start(f32[16,56,128]{2,0,1:T(8,128)} %copy.109) | copy-start | bytes 1376260

commit v13 on v11

--- a/solution.py
+++ b/solution.py
@@ -104,8 +104,8 @@
 def im2col_kernel(p_ref, o_ref):
     def body(y, carry):
         for zb in range(o_ref.shape[0]):
-            for b in range(TS):
-                o_ref[zb, y, :, b * (TS + ZB):(b + 1) * (TS + ZB)] = p_ref[y + b, :, zb * ZB: zb * ZB + TS + ZB]
+            pieces = [p_ref[y + b, :, zb * ZB: zb * ZB + TS + ZB] for b in range(TS)]
+            o_ref[zb, y, :, :] = jnp.concatenate(pieces, axis=-1)
         return carry
     lax.fori_loop(0, BY, body, 0)
 

time: 57.9 us -> 57.8 us (level)
  transfers between devices with their start and end apart: 8 -> 8, of which waited for: 0 -> 0; matrix products, arithmetic and copies ran while one was open for 15% -> 15% of each run, Pallas kernels for 12% -> 11%
where the time goes in v13:
time: 57.8 us; the launch traced here: 57.4 us
  local copies, waits for them, and re-layouts  16.1 us (28%)
  starting transfers between devices  14 us (24%)
  matrix products  11.7 us (20%)
  other arithmetic  8.4 us (15%)
  Pallas kernels  6.57 us (11%)
  between operations  0.63 us (1%)
    ppermute x6, starting transfers between devices, gather_planes(): lax.ppermute(held, axis, [(i, i ^ s * step) for i in range(size)])  10.7 us
    conv_general_dilated x1, matrix products, local(): lax.conv_general_dilated(cols, rhs, (1, 1), 'VALID', rhs_dilation=(2, 1),...  8.07 us
    pallas_call x1, Pallas kernels, im2col(): pl.pallas_call(im2col_kernel, out_shape=jax.ShapeDtypeStruct((blocks, BY,...  6.57 us
    dot_general x1, matrix products, toeplitz_rhs(): rhs = jnp.einsum('rk,wkn->rwn', kt, shift, precision=lax.Precision.HIGHEST)  2.85 us
    dot_general x1, local copies, waits for them, and re-layouts, toeplitz_rhs(): rhs = jnp.einsum('rk,wkn->rwn', kt, shift, precision=lax.Precision.HIGHEST)  2.43 us
    ppermute x1, starting transfers between devices, extended(): before = lax.ppermute(last, axis, up)  1.99 us
    add x2, other arithmetic, rotated_kernels(): rotated + jnp.where(expand(order_row == row), jnp.transpose(picked, perm)...  1.55 us
    add x1, local copies, waits for them, and re-layouts, rotated_kernels(): rotated + jnp.where(expand(order_row == row), jnp.transpose(picked, perm)...  1.55 us
  transfers between devices with their start and end apart: 8, of which 0 were waited for; matrix products, arithmetic and copies ran while one was open for 15% of the time, Pallas kernels for 11%

profile of v13, /device:TPU:0, one launch (start us, length us, event | category | flops | bytes accessed | tf_op | source)
XLA Modules:
  0.0 57.4 jit_solution(14194214669355707058)
XLA Ops:
  0.5 2.5 %collective-permute-start.3 = (f32[1,8,256]{2,1,0:T(8,128)}, f32[1,8,256]{2,1,0:T(8,128)S(1)}, u32[]{:S(2)}, u32[]{:S(2)}) collective-permute-start(f32[1,8,256]{2,1,0:T(8,128)} %bitcast.105), channel_id=1, source_target_pairs={{0,2},{1,3},{2,0},{3,1},{4,6},{5,7},{6,4},{7,5},{8,10},{9,11},{10,... | collective-permute-start | bytes 24584 | tf_op jit(solution)/shard_map/ppermute | solution.py:56
  3.1 0.8 %fusion.88 = (f32[8,896]{1,0:T(8,128)S(1)}, f32[8,896]{1,0:T(8,128)S(1)}) fusion(f32[16,896]{1,0:T(8,128)} %param.5), kind=kLoop, calls=%fused_computation.179 | loop fusion | bytes 114688 | tf_op jit(solution)/shard_map/slice | solution.py:27
  3.9 2.0 %collective-permute-start = (f32[8,8,112]{2,0,1:T(8,128)S(1)}, f32[8,8,112]{2,0,1:T(8,128)S(1)}, u32[]{:S(2)}, u32[]{:S(2)}) collective-permute-start(f32[8,8,112]{2,0,1:T(8,128)S(1)} %copy.70), channel_id=1, source_target_pairs={{0,1},{1,2},{2,3},{3,4},{4,5},{5,6},{6,7},{7,8},{8,9},{9,10},{10,1... | collective-permute-start | bytes 86024 | tf_op jit(solution)/shard_map/ppermute | solution.py:28
  6.0 1.3 %collective-permute-start.1 = (f32[8,8,112]{2,0,1:T(8,128)S(1)}, f32[8,8,112]{2,0,1:T(8,128)S(1)}, u32[]{:S(2)}, u32[]{:S(2)}) collective-permute-start(f32[8,8,112]{2,0,1:T(8,128)S(1)} %copy.71), channel_id=1, source_target_pairs={{1,0},{2,1},{3,2},{4,3},{5,4},{6,5},{7,6},{8,7},{9,8},{10,9},{11,1... | collective-permute-start | bytes 86024 | tf_op jit(solution)/shard_map/ppermute | solution.py:29
  7.4 0.7 %broadcast_compare_fusion.10 = (pred[8]{0:T(512)(128)(4,1)S(1)}, pred[8]{0:T(512)(128)(4,1)S(1)}, pred[8]{0:T(512)(128)(4,1)S(1)}, pred[8]{0:T(512)(128)(4,1)S(1...) fusion(s32[8]{0:T(128)} %param.8), kind=kLoop, calls=%fused_computation.161 | loop fusion | flops 64 | bytes 96 | tf_op jit(solution)/shard_map/eq | solution.py:74
  8.0 0.7 %broadcast_compare_fusion.1 = (pred[8]{0:T(512)(128)(4,1)S(1)}, s32[8]{0:T(128)S(1)}, pred[8]{0:T(512)(128)(4,1)S(1)}, s32[8]{0:T(128)S(1)}) fusion(s32[8]{0:T(128)} %param.7), kind=kLoop, calls=%fused_computation.152 | loop fusion | flops 376 | bytes 112 | tf_op jit(solution)/shard_map/eq | solution.py:83
  8.7 0.7 %convert_element_type.4 = f32[8]{0:T(128)S(1)} convert(s32[8]{0:T(128)} %param.9) | non-fusion elementwise | flops 8 | bytes 64 | tf_op jit(solution)/shard_map/convert_element_type | solution.py:163
  9.8 0.9 %reshape.128 = f32[16,8,112]{2,1,0:T(8,128)S(1)} reshape(f32[16,896]{1,0:T(8,128)} %param.5) | data formatting | bytes 114688 | tf_op jit(solution)/shard_map/reshape | solution.py:128
  11.2 0.7 %fusion.48 = (f32[1,8,256]{2,1,0:T(8,128)S(1)}, f32[1,8,256]{2,1,0:T(8,128)S(1)}, f32[1,8,256]{2,1,0:T(8,128)S(1)}) fusion(f32[1,8,256]{2,1,0:T(8,128)S(1)} %collective-permute-done.4, f32[1,8,256]{2,1,0:T(8,128)S(1)} %collective-permute-done.3, f32[1,8,256]{2,1,0:T(8,128)S(1)} %collective-permute-done.2, f32[8,256]{1,0:T(8,128)} %param.6, pred[]{:T(512)S(6)} %eq.179, ...), kind=kLoop, calls=%fused_computation.94 | loop fusion | flops 43008 | bytes 57356 | tf_op jit(solution)/shard_map/add | solution.py:62
  12.0 5.0 %collective-permute-start.5 = (f32[4,8,256]{2,1,0:T(8,128)S(1)}, f32[4,8,256]{2,1,0:T(8,128)S(1)}, u32[]{:S(2)}, u32[]{:S(2)}) collective-permute-start(f32[4,8,256]{2,1,0:T(8,128)S(1)} %pad_maximum_fusion.2), channel_id=1, source_target_pairs={{0,4},{1,5},{2,6},{3,7},{4,0},{5,1},{6,2},{7,3},{8,12},{9,13},{10,... | collective-permute-start | bytes 98312 | tf_op jit(solution)/shard_map/ppermute | solution.py:56
  17.0 2.6 %collective-permute-start.6 = (f32[4,8,256]{2,1,0:T(8,128)S(1)}, f32[4,8,256]{2,1,0:T(8,128)S(1)}, u32[]{:S(2)}, u32[]{:S(2)}) collective-permute-start(f32[4,8,256]{2,1,0:T(8,128)S(1)} %pad_maximum_fusion.2), channel_id=1, source_target_pairs={{0,8},{1,9},{2,10},{3,11},{4,12},{5,13},{6,14},{7,15},{8,0},{9,1},... | collective-permute-start | bytes 98312 | tf_op jit(solution)/shard_map/ppermute | solution.py:56
  20.4 0.9 %slice_bitcast_fusion.p_ref = f32[24,31,128]{2,1,0:T(8,128)} fusion(f32[32,8,112]{2,0,1:T(8,128)S(1)} %constant_dynamic-update-slice_fusion), kind=kLoop, calls=%fused_computation.41 | loop fusion | bytes 495616 | tf_op jit(solution)/shard_map/transpose | solution.py:139
  21.3 6.6 %shard_map.55 = f32[7,8,31,512]{3,2,1,0:T(8,128)} custom-call(f32[24,31,128]{2,1,0:T(8,128)} %slice_bitcast_fusion.p_ref), custom_call_target="tpu_custom_call" | custom-call | bytes 3555328 | tf_op jit(solution)/shard_map/pallas_call | solution.py:115
  28.4 1.1 %copy.109 = f32[16,56,128]{2,0,1:T(8,128)} copy(f32[16,56,128]{1,2,0:T(8,128)S(1)} %bitcast.95) | data formatting | bytes 917504 | tf_op jit(solution)/shard_map/sqrt | solution.py:162
  31.6 0.9 %select_add_fusion = f32[8,16,16,16]{2,3,1,0:T(8,128)S(1)} fusion(f32[16,16,16]{1,2,0:T(8,128)S(1)} %copy.87, f32[16,16,16]{1,2,0:T(8,128)S(1)} %copy.85, f32[16,16,16]{1,2,0:T(8,128)S(1)} %copy.83, f32[16,16,16]{1,2,0:T(8,128)S(1)} %copy.81, f32[16,16,16]{1,2,0:T(8,128)S(1)} %copy.79, f32[16,16,16]{1,2,0:T(8,128)S(1)} %copy.77, f32[16,16,16]{1,2,0:T(8,128)S(1)} %copy.75, ...), kind=kLoop, calls=%fused_computation.29 | loop fusion | flops 491520 | bytes 262208 | tf_op jit(solution)/shard_map/add | solution.py:74
  32.7 0.5 rev.13
  34.0 0.7 %copy.89 = f32[8,16,16,16]{1,3,2,0:T(8,128)S(1)} copy(f32[8,16,16,16]{2,3,1,0:T(8,128)S(1)} %broadcast_select_fusion.1) | data formatting | bytes 262144 | tf_op jit(solution)/shard_map/jit(_where)/select_n | solution.py:78
  35.2 1.3 %bitcast_add_fusion.3 = f32[8,16,16,16]{1,3,2,0:T(8,128)} fusion(f32[8,16,16,16]{2,3,1,0:T(8,128)S(1)} %broadcast_select_fusion.1, f32[8,16,16,16]{1,2,3,0:T(8,128)S(1)} %copy.91, f32[8,16,16,16]{1,3,2,0:T(8,128)S(1)} %copy.89, pred[8]{0:T(512)(128)(4,1)S(1)} %get-tuple-element.51, pred[8]{0:T(512)(128)(4,1)S(1)} %get-tuple-element.50, ...), kind=kLoop, calls=%fused_computation.25 | loop fusion | flops 163840 | bytes 524312 | tf_op jit(solution)/shard_map/add | solution.py:83
  36.4 1.5 %copy.94 = f32[8,16,16,16]{3,1,2,0:T(8,128)S(1)} copy(f32[8,16,16,16]{1,3,2,0:T(8,128)} %bitcast_add_fusion.3) | data formatting | bytes 262144 | tf_op jit(solution)/shard_map/add | solution.py:83
  38.3 0.6 %fusion.86 = (f32[8]{0:T(128)S(1)}, f32[8,16,16,16]{3,2,1,0:T(8,128)S(1)}) fusion(f32[8,16,16,16]{1,2,3,0:T(8,128)S(1)} %copy.91, pred[8]{0:T(512)(128)(4,1)S(1)} %get-tuple-element.15, f32[8,16,16,16]{3,1,2,0:T(8,128)S(1)} %bitcast_add_fusion.1), kind=kLoop, calls=%fused_computation.177 | loop fusion | flops 98296 | bytes 393256 | tf_op jit(solution)/shard_map/reduce_sum | solution.py:85
  40.4 2.9 %fusion.1 = f32[128,32,256]{2,0,1:T(8,128)S(1)} fusion(f32[128,256,1]{0,1,2:T(8,128)S(1)} %reshape.160, s32[256]{0:T(256)S(1)} %get-tuple-element.56, s32[256]{0:T(256)S(1)} %get-tuple-element.59, s32[256]{0:T(256)S(1)} %get-tuple-element.57, s32[256]{0:T(256)S(1)} %get-tuple-element.58, pred[256]{0:T(512)(128)(4,1)S(1)} %get-tuple-element.54, ...), kind=kOutput, calls=%fused_computation.3 | convolution fusion | flops 3238002688 | bytes 4329984 | tf_op jit(solution)/shard_map/rk,wkn->rwn/dot_general | solution.py:100
  43.2 2.4 %copy.100 = f32[128,32,256]{2,1,0:T(8,128)S(1)} copy(f32[128,32,256]{2,0,1:T(8,128)S(1)} %fusion.1) | data formatting | bytes 8388608 | tf_op jit(solution)/shard_map/rk,wkn->rwn/dot_general | solution.py:100
  45.7 8.1 %fusion.15 = f32[17,8,7,256]{3,1,2,0:T(8,128)S(1)} fusion(f32[8,1,512,256]{3,2,1,0:T(8,128)S(1)} %bitcast.93, f32[8,7,31,512]{3,2,1,0:T(8,128)S(1)} %bitcast.92), kind=kOutput, calls=%fused_computation.16 | convolution fusion | flops 5989466112 | bytes 8724480 | tf_op jit(solution)/shard_map/conv_general_dilated | solution.py:141
  56.7 0.7 %pad_maximum_fusion = f32[4,16,896]{2,1,0:T(8,128)} fusion(f32[1,16,896]{2,1,0:T(8,128)S(1)} %stack_reshape.15, f32[1,16,896]{2,1,0:T(8,128)S(1)} %stack_reshape.14, f32[1,16,896]{2,1,0:T(8,128)S(1)} %stack_reshape.13, f32[1,16,896]{2,1,0:T(8,128)S(1)} %stack_reshape.12), kind=kLoop, calls=%fused_computation.42 | loop fusion | flops 172032 | bytes 458752 | tf_op jit(solution)/shard_map/stack | solution.py:177
  (93 shorter events, 10.8 us)
Async XLA Ops:
  0.0 11.2 %collective-permute-start.2 = (f32[1,8,256]{2,1,0:T(8,128)}, f32[1,8,256]{2,1,0:T(8,128)S(1)}, u32[]{:S(2)}, u32[]{:S(2)}) collective-permute-start(f32[1,8,256]{2,1,0:T(8,128)} %bitcast.104), channel_id=1, source_target_pairs={{0,1},{1,0},{2,3},{3,2},{4,5},{5,4},{6,7},{7,6},{8,9},{9,8},{10,11... | collective-permute-start | bytes 24584 | tf_op jit(solution)/shard_map/ppermute | solution.py:56
  0.5 10.7 %collective-permute-start.3 = (f32[1,8,256]{2,1,0:T(8,128)}, f32[1,8,256]{2,1,0:T(8,128)S(1)}, u32[]{:S(2)}, u32[]{:S(2)}) collective-permute-start(f32[1,8,256]{2,1,0:T(8,128)} %bitcast.105), channel_id=1, source_target_pairs={{0,2},{1,3},{2,0},{3,1},{4,6},{5,7},{6,4},{7,5},{8,10},{9,11},{10,... | collective-permute-start | bytes 24584 | tf_op jit(solution)/shard_map/ppermute | solution.py:56
  2.9 8.3 %collective-permute-start.4 = (f32[1,8,256]{2,1,0:T(8,128)}, f32[1,8,256]{2,1,0:T(8,128)S(1)}, u32[]{:S(2)}, u32[]{:S(2)}) collective-permute-start(f32[1,8,256]{2,1,0:T(8,128)} %bitcast.106), channel_id=1, source_target_pairs={{0,3},{1,2},{2,1},{3,0},{4,7},{5,6},{6,5},{7,4},{8,11},{9,10},{10,... | collective-permute-start | bytes 24584 | tf_op jit(solution)/shard_map/ppermute | solution.py:56
  3.9 15.7 %collective-permute-start = (f32[8,8,112]{2,0,1:T(8,128)S(1)}, f32[8,8,112]{2,0,1:T(8,128)S(1)}, u32[]{:S(2)}, u32[]{:S(2)}) collective-permute-start(f32[8,8,112]{2,0,1:T(8,128)S(1)} %copy.70), channel_id=1, source_target_pairs={{0,1},{1,2},{2,3},{3,4},{4,5},{5,6},{6,7},{7,8},{8,9},{9,10},{10,1... | collective-permute-start | bytes 86024 | tf_op jit(solution)/shard_map/ppermute | solution.py:28
  6.0 13.6 %collective-permute-start.1 = (f32[8,8,112]{2,0,1:T(8,128)S(1)}, f32[8,8,112]{2,0,1:T(8,128)S(1)}, u32[]{:S(2)}, u32[]{:S(2)}) collective-permute-start(f32[8,8,112]{2,0,1:T(8,128)S(1)} %copy.71), channel_id=1, source_target_pairs={{1,0},{2,1},{3,2},{4,3},{5,4},{6,5},{7,6},{8,7},{9,8},{10,9},{11,1... | collective-permute-start | bytes 86024 | tf_op jit(solution)/shard_map/ppermute | solution.py:29
  12.0 17.5 %collective-permute-start.5 = (f32[4,8,256]{2,1,0:T(8,128)S(1)}, f32[4,8,256]{2,1,0:T(8,128)S(1)}, u32[]{:S(2)}, u32[]{:S(2)}) collective-permute-start(f32[4,8,256]{2,1,0:T(8,128)S(1)} %pad_maximum_fusion.2), channel_id=1, source_target_pairs={{0,4},{1,5},{2,6},{3,7},{4,0},{5,1},{6,2},{7,3},{8,12},{9,13},{10,... | collective-permute-start | bytes 98312 | tf_op jit(solution)/shard_map/ppermute | solution.py:56
  17.0 12.5 %collective-permute-start.6 = (f32[4,8,256]{2,1,0:T(8,128)S(1)}, f32[4,8,256]{2,1,0:T(8,128)S(1)}, u32[]{:S(2)}, u32[]{:S(2)}) collective-permute-start(f32[4,8,256]{2,1,0:T(8,128)S(1)} %pad_maximum_fusion.2), channel_id=1, source_target_pairs={{0,8},{1,9},{2,10},{3,11},{4,12},{5,13},{6,14},{7,15},{8,0},{9,1},... | collective-permute-start | bytes 98312 | tf_op jit(solution)/shard_map/ppermute | solution.py:56
  19.6 9.9 %collective-permute-start.7 = (f32[4,8,256]{2,1,0:T(8,128)S(1)}, f32[4,8,256]{2,1,0:T(8,128)S(1)}, u32[]{:S(2)}, u32[]{:S(2)}) collective-permute-start(f32[4,8,256]{2,1,0:T(8,128)S(1)} %pad_maximum_fusion.2), channel_id=1, source_target_pairs={{0,12},{1,13},{2,14},{3,15},{4,8},{5,9},{6,10},{7,11},{8,4},{9,5},... | collective-permute-start | bytes 98312 | tf_op jit(solution)/shard_map/ppermute | solution.py:56
  43.2 2.4 %copy-start = (f32[7,8,31,512]{3,2,1,0:T(8,128)S(1)}, f32[7,8,31,512]{3,2,1,0:T(8,128)}, u32[]{:S(2)}) copy-start(f32[7,8,31,512]{3,2,1,0:T(8,128)} %shard_map.55) | copy-start | bytes 10665988
  45.7 8.2 %copy-start.1 = (f32[16,56,128]{2,0,1:T(8,128)S(1)}, f32[16,56,128]{2,0,1:T(8,128)}, u32[]{:S(2)}) copy-start(f32[16,56,128]{2,0,1:T(8,128)} %copy.109) | copy-start | bytes 1376260
